TPU v7x, 32 devices: a whole 2x2x4 slice. The times are simulated.
32 devices in a mesh: dp: 4 (over z), expert: 4 (over y, x), tensor: 2 (over core).
Axes of the slice: x: 2, y: 2, z: 4, core: 2. Of those that a mesh axis runs over, the one named last changes fastest.
Arguments:
- tokens: bfloat16 [2048, 2048], P(('dp', 'expert')), may hold values from -6 to 6
- grad_out: bfloat16 [2048, 2048], P(('dp', 'expert')), may hold values from -6 to 6
- route_ids: int32 [2048, 8], P(('dp', 'expert')), may hold values from 0 to 15, all different within a row; in each aligned block of 128 rows (0 to 127, 128 to 255, ...) at most 72 rows name the same one
- gate_values: bfloat16 [2048, 8], P(('dp', 'expert')), may hold values from 0.049804688 to 0.5
- gate_proj: bfloat16 [16, 2048, 768], P(('dp', 'expert'), None, 'tensor'), may hold values from -0.125 to 0.125
- up_proj: bfloat16 [16, 2048, 768], P(('dp', 'expert'), None, 'tensor'), may hold values from -0.125 to 0.125
- down_proj: bfloat16 [16, 768, 2048], P(('dp', 'expert'), 'tensor'), may hold values from -0.21875 to 0.21875
Outputs:
- token_grad: bfloat16 [2048, 2048], P(('dp', 'expert'), 'tensor')
- gate_grad: bfloat16 [2048, 8], P(('dp', 'expert'))
- gate_proj_grad: bfloat16 [16, 2048, 768], P(('dp', 'expert'), None, 'tensor')
- up_proj_grad: bfloat16 [16, 2048, 768], P(('dp', 'expert'), None, 'tensor')
- down_proj_grad: bfloat16 [16, 768, 2048], P(('dp', 'expert'), 'tensor')
Inputs may be any that keep to these rules, and one draw needn't show every extreme that they name: `route_ids`: each token names 8 different experts. Among the rows of one device (128 tokens), no expert is named more than 72 times, a bound that some block reaches.
All inputs are finite; a program needn't handle non-finite values.
Results may differ from a plain program's by a relative error of at most 0.008.
Values may be sent and summed in bfloat16 or wider, within the bound.
No kernel may reach another device: no remote copies, remote signals or barrier semaphores. Data moves between devices by JAX's collectives and lax.ppermute only.
A program may use at most 128 MiB of HBM per device.

v0:
```python
import jax
import jax.numpy as jnp
from jax import lax
from jax.sharding import PartitionSpec as P


def on_device(tokens, grad_out, route_ids, gate_values, gate_proj, up_proj, down_proj):
    tok_rows, features = tokens.shape
    top_count = route_ids.shape[1]
    n_dp = lax.axis_size("dp")
    n_ex = lax.axis_size("expert")
    groups = n_dp * n_ex
    capacity = max(2, tok_rows * top_count * 9 // (8 * groups))
    plane = lax.axis_index("dp")
    core = lax.axis_index("tensor")
    routes = tok_rows * top_count
    block_slots = n_ex * capacity
    lanes = 128

    carried = jnp.where(core == 0, tokens, grad_out)
    aux = jnp.concatenate([route_ids.astype(tokens.dtype), gate_values.astype(tokens.dtype)], axis=1)
    aux = jnp.pad(aux, ((0, 0), (0, lanes - aux.shape[1])))
    ext = jnp.concatenate([carried, aux], axis=1)
    blocks = [ext] + [
        lax.ppermute(ext, "dp", [(i, (i + s) % n_dp) for i in range(n_dp)])
        for s in range(1, n_dp)
    ]

    r_iota = jnp.arange(routes, dtype=jnp.int32)
    earlier = (r_iota[None, :] < r_iota[:, None]).astype(jnp.bfloat16)
    e_iota = jnp.arange(n_ex, dtype=jnp.int32)
    q_iota = jnp.arange(block_slots, dtype=jnp.int32)

    weight_g = gate_proj[0]
    weight_u = up_proj[0]
    weight_d = down_proj[0]
    rows_x, rows_dy, rows_pre, rows_up, rows_w = [], [], [], [], []
    col_parts = []
    anchors = []
    pair = 2 if n_dp % 2 == 0 else 1
    groups_of = [list(range(g, g + pair)) for g in range(0, n_dp, pair)]
    for gi, members in enumerate(groups_of):
        sends, selects, matches = [], [], []
        for s in members:
            blk = blocks[s]
            carried_b = blk[:, :features]
            ids_b = blk[:, features:features + top_count].astype(jnp.int32)
            gates_b = blk[:, features + top_count:features + 2 * top_count].astype(jnp.float32)

            local_ex = ids_b.reshape(routes) - plane * n_ex
            in_plane = (local_ex >= 0) & (local_ex < n_ex)
            one_hot = local_ex[:, None] == e_iota[None, :]
            running = jnp.dot(earlier, one_hot.astype(jnp.bfloat16), preferred_element_type=jnp.float32)
            position = jnp.sum(running * one_hot.astype(jnp.float32), axis=1).astype(jnp.int32)
            key = jnp.where(in_plane, local_ex * capacity + position, -1).reshape(tok_rows, top_count)
            match = key[None, :, :] == q_iota[:, None, None]
            select = jnp.sum(match.astype(jnp.bfloat16), axis=2)
            send_rows = jnp.dot(select, carried_b, preferred_element_type=jnp.float32).astype(tokens.dtype)
            send_gate = jnp.sum(jnp.where(match, gates_b[None, :, :], 0.0), axis=(1, 2))
            gate_cols = jnp.pad(send_gate.astype(tokens.dtype)[:, None], ((0, 0), (0, lanes - 1)))
            sends.append(jnp.concatenate([send_rows, gate_cols], axis=1))
            selects.append(select)
            matches.append(match)
        send = jnp.stack(sends)
        n_mem = len(members)

        if gi >= 2:
            send = lax.optimization_barrier((send, anchors[gi - 2]))[0]
        recv = lax.all_to_all(
            send.reshape(n_mem, n_ex, capacity, features + lanes), "expert", split_axis=1, concat_axis=1, tiled=True
        ).reshape(n_mem * block_slots, features + lanes)
        both = lax.all_gather(recv, "tensor")
        routed_x = both[0, :, :features]
        routed_dy = both[1, :, :features]
        routed_gate = both[0, :, features]

        gate_pre = jnp.dot(routed_x, weight_g, preferred_element_type=jnp.float32)
        up_pre = jnp.dot(routed_x, weight_u, preferred_element_type=jnp.float32)
        sig_gate = jax.nn.sigmoid(gate_pre)
        silu_gate = gate_pre * sig_gate
        activation = (silu_gate * up_pre).astype(jnp.bfloat16)
        hidden_grad = lax.dot_general(
            routed_dy, weight_d, (((1,), (1,)), ((), ())), preferred_element_type=jnp.float32
        )
        gate_terms = jnp.sum(hidden_grad * activation.astype(jnp.float32), axis=1)
        row_gate = routed_gate.astype(jnp.float32)[:, None]
        scaled = row_gate * hidden_grad
        up_grad = (scaled * silu_gate).astype(jnp.bfloat16)
        pre_grad = (scaled * up_pre * sig_gate * (1.0 + gate_pre * (1.0 - sig_gate))).astype(
            jnp.bfloat16
        )
        anchors.append(pre_grad)
        weighted = (row_gate * activation.astype(jnp.float32)).astype(jnp.bfloat16)
        rows_x.append(routed_x)
        rows_dy.append(routed_dy)
        rows_pre.append(pre_grad)
        rows_up.append(up_grad)
        rows_w.append(weighted)
        gate_col = jnp.pad(gate_terms[:, None], ((0, 0), (0, lanes - 1)))
        pieces = []
        half = features // 2
        for h in range(2):
            rows = slice(h * half, (h + 1) * half)
            pieces.append(
                lax.dot_general(
                    pre_grad, weight_g[rows], (((1,), (1,)), ((), ())), preferred_element_type=jnp.float32
                ) + lax.dot_general(
                    up_grad, weight_u[rows], (((1,), (1,)), ((), ())), preferred_element_type=jnp.float32
                )
            )
            pieces.append(gate_col)
        ret = lax.psum_scatter(
            jnp.concatenate(pieces, axis=1), "tensor", scatter_dimension=1, tiled=True
        ).astype(jnp.bfloat16)
        back = lax.all_to_all(
            ret.reshape(n_mem, n_ex, capacity, half + lanes), "expert", split_axis=1, concat_axis=1, tiled=True
        ).reshape(n_mem, block_slots, half + lanes)

        for m, s in enumerate(members):
            col_grad = lax.dot_general(
                selects[m], back[m, :, :half], (((0,), (0,)), ((), ())), preferred_element_type=jnp.float32
            )
            col_gate = jnp.sum(
                jnp.where(matches[m], back[m, :, half].astype(jnp.float32)[:, None, None], 0.0), axis=0
            )
            part = jnp.concatenate(
                [col_grad, jnp.pad(col_gate, ((0, 0), (0, lanes - top_count)))], axis=1
            ).astype(jnp.bfloat16)
            if s:
                part = lax.ppermute(part, "dp", [(i, (i - s) % n_dp) for i in range(n_dp)])
            col_parts.append(part.astype(jnp.float32))

    total = sum(col_parts[1:], col_parts[0])
    half = total.shape[1] - lanes
    token_grad = total[:, :half].astype(jnp.bfloat16)
    gate_grad = total[:, half:half + top_count].astype(jnp.bfloat16)
    all_x = jnp.concatenate(rows_x, axis=0)
    all_dy = jnp.concatenate(rows_dy, axis=0)
    grad_g = lax.dot_general(
        all_x, jnp.concatenate(rows_pre, axis=0), (((0,), (0,)), ((), ())),
        preferred_element_type=jnp.float32,
    ).astype(jnp.bfloat16)
    grad_u = lax.dot_general(
        all_x, jnp.concatenate(rows_up, axis=0), (((0,), (0,)), ((), ())),
        preferred_element_type=jnp.float32,
    ).astype(jnp.bfloat16)
    grad_d = lax.dot_general(
        jnp.concatenate(rows_w, axis=0), all_dy, (((0,), (0,)), ((), ())),
        preferred_element_type=jnp.float32,
    ).astype(jnp.bfloat16)
    return (token_grad, gate_grad, grad_g[None], grad_u[None], grad_d[None])


def solution(mesh):
    in_specs = (
        P(("dp", "expert"), None),
        P(("dp", "expert"), None),
        P(("dp", "expert"), None),
        P(("dp", "expert"), None),
        P(("dp", "expert"), None, "tensor"),
        P(("dp", "expert"), None, "tensor"),
        P(("dp", "expert"), "tensor", None),
    )
    out_specs = (
        P(("dp", "expert"), "tensor"),
        P(("dp", "expert"), None),
        P(("dp", "expert"), None, "tensor"),
        P(("dp", "expert"), None, "tensor"),
        P(("dp", "expert"), "tensor", None),
    )
    return jax.shard_map(
        on_device, mesh=mesh, in_specs=in_specs, out_specs=out_specs, check_vma=False
    )
```

profile of v0, /device:TPU:0, one launch (start us, length us, event | category | flops | bytes accessed | tf_op | source)
XLA Modules:
  0.0 259.0 jit_solution(7054400704870810078)
XLA Ops:
  7.2 1.4 copy.101
  8.6 1.3 copy.102
  11.4 0.8 pad_maximum_fusion.15
  12.2 5.0 %collective-permute-start.3 = (bf16[128,2176]{0,1:T(8,128)(2,1)}, bf16[128,2176]{0,1:T(8,128)(2,1)S(1)}, u32[]{:S(2)}, u32[]{:S(2)}) collective-permute-start(bf16[128,2176]{0,1:T(8,128)(2,1)} %pad_maximum_fusion.15), channel_id=1, source_target_pairs={{0,24},{8,0},{16,8},{24,16},{1,25},{9,1},{17,9},{25,17},{2,26},{10... | collective-permute-start | bytes 1671176 | tf_op jit(solution)/shard_map/ppermute | solution.py:25
  17.3 13.3 %collective-permute-done.3 = bf16[128,2176]{0,1:T(8,128)(2,1)S(1)} collective-permute-done((bf16[128,2176]{0,1:T(8,128)(2,1)}, bf16[128,2176]{0,1:T(8,128)(2,1)S(1)}, u32[]{:S(2)}, u32[]{:S(2)}) %collective-permute-start.3) | collective-permute-done | bytes 557088 | tf_op jit(solution)/shard_map/ppermute | solution.py:25
  31.5 1.1 select_reduce_fusion.2
  33.1 20.1 %collective-permute-done.2 = bf16[128,2176]{0,1:T(8,128)(2,1)} collective-permute-done((bf16[128,2176]{0,1:T(8,128)(2,1)}, bf16[128,2176]{0,1:T(8,128)(2,1)}, u32[]{:S(2)}, u32[]{:S(2)}) %collective-permute-start.2) | collective-permute-done | bytes 557088 | tf_op jit(solution)/shard_map/ppermute | solution.py:25
  56.6 1.1 select_reduce_fusion.3
  57.8 1.5 convolution_convert_fusion.1
  60.0 1.7 pad_maximum_fusion.14
  61.7 4.5 %all-to-all-start.2 = ((bf16[2,4,72,2176]{3,2,0,1:T(8,128)(2,1)}), bf16[2,4,72,2176]{3,2,0,1:T(8,128)(2,1)}, u32[]{:S(2)}, u32[]{:S(2)}) async-start(bf16[2,4,72,2176]{3,2,0,1:T(8,128)(2,1)} %pad_maximum_fusion.14), calls=%async_computation.3 | async-start | bytes 5013504 | tf_op jit(solution)/shard_map/all_to_all | solution.py:69
  66.3 0.9 collective-permute-start
  68.0 27.0 %all-to-all-done.2 = bf16[2,4,72,2176]{3,2,0,1:T(8,128)(2,1)} async-done(((bf16[2,4,72,2176]{3,2,0,1:T(8,128)(2,1)}), bf16[2,4,72,2176]{3,2,0,1:T(8,128)(2,1)}, u32[]{:S(2)}, u32[]{:S(2)}) %all-to-all-start.2) | async-done | bytes 2506784 | tf_op jit(solution)/shard_map/all_to_all | solution.py:69
  95.0 3.3 %copy.123 = bf16[2,4,72,2176]{3,2,1,0:T(8,128)(2,1)} copy(bf16[2,4,72,2176]{3,2,0,1:T(8,128)(2,1)} %all-to-all-done.2) | data formatting | bytes 5013504 | tf_op jit(solution)/shard_map/all_to_all | solution.py:69
  99.0 1.1 select_reduce_fusion.7
  104.1 1.1 select_reduce_fusion.6
  105.7 1.6 convolution_convert_fusion.2
  107.7 32.0 %all_to_all.20 = bf16[2,4,72,2176]{3,2,0,1:T(8,128)(2,1)S(1)} all-to-all(bf16[2,4,72,2176]{3,2,0,1:T(8,128)(2,1)S(1)} %pad_maximum_fusion.13), channel_id=1, replica_groups=mesh['dp'=4,'expert'=4,'tensor'=2] {'expert'}, dimensions={1} | all-to-all | bytes 5013504 | tf_op jit(solution)/shard_map/all_to_all | solution.py:69
  139.6 1.6 copy.109
  141.5 1.2 convert_reduce_fusion
  142.8 3.2 %fusion.24 = f32[576,384]{1,0:T(8,128)S(1)} fusion(bf16[1,2048,384]{2,1,0:T(8,128)(2,1)S(1)} %copy-done.2, bf16[2,576,2176]{2,1,0:T(8,128)(2,1)} %all-gather.5.cloned.1.call-done), kind=kOutput, calls=%fused_computation.39 | convolution fusion | flops 905969664 | bytes 4816896 | tf_op jit(solution)/shard_map/dot_general | solution.py:77
  146.4 1.4 fusion.28
  147.7 2.6 multiply_convert_fusion.1
  150.7 0.8 fusion.69
  151.5 0.8 fusion.75
  152.3 0.8 convolution_add_fusion
  153.1 0.8 convolution_add_fusion.1
  154.0 2.8 %pad_maximum_fusion.1 = f32[576,2304]{1,0:T(8,128)} fusion(f32[576,128]{1,0:T(8,128)S(1)} %pad.49, f32[576,1024]{1,0:T(8,128)S(1)} %convolution_add_fusion, f32[576,1024]{1,0:T(8,128)S(1)} %convolution_add_fusion.1), kind=kLoop, calls=%fused_computation.1 | loop fusion | flops 3981312 | bytes 10321920 | tf_op jit(solution)/shard_map/concatenate | solution.py:113
  156.8 1.1 convert_reduce_fusion.1
  157.9 3.2 %fusion.26 = f32[576,384]{1,0:T(8,128)S(1)} fusion(bf16[1,2048,384]{2,1,0:T(8,128)(2,1)S(1)} %copy-done.2, bf16[2,576,2176]{2,1,0:T(8,128)(2,1)} %all-gather.3.cloned.1.call-done), kind=kOutput, calls=%fused_computation.41 | convolution fusion | flops 905969664 | bytes 4816896 | tf_op jit(solution)/shard_map/dot_general | solution.py:77
  161.5 1.4 fusion.30
  162.9 2.5 multiply_convert_fusion.4
  165.8 0.8 fusion.71
  166.6 0.8 fusion.77
  167.4 0.8 convolution_add_fusion.2
  168.2 0.8 convolution_add_fusion.3
  169.1 2.8 %pad_maximum_fusion = f32[576,2304]{1,0:T(8,128)} fusion(f32[576,128]{1,0:T(8,128)S(1)} %pad.44, f32[576,1024]{1,0:T(8,128)S(1)} %convolution_add_fusion.2, f32[576,1024]{1,0:T(8,128)S(1)} %convolution_add_fusion.3), kind=kLoop, calls=%fused_computation | loop fusion | flops 3981312 | bytes 10321920 | tf_op jit(solution)/shard_map/concatenate | solution.py:113
  171.9 5.5 %slice_bitcast_fusion.3 = (bf16[576,2048]{1,0:T(8,128)(2,1)}, bf16[576,2048]{1,0:T(8,128)(2,1)}) fusion(bf16[2,576,2176]{2,1,0:T(8,128)(2,1)} %all-gather.3.cloned.1.call-done), kind=kLoop, calls=%fused_computation.34 | loop fusion | bytes 9437184 | tf_op jit(solution)/shard_map/squeeze | solution.py:74
  177.4 1.9 convert_element_type.344
  179.3 1.2 copy.125
  180.5 3.6 %all-to-all-start.3 = ((bf16[2,4,72,1152]{3,2,0,1:T(8,128)(2,1)}), bf16[2,4,72,1152]{3,2,0,1:T(8,128)(2,1)S(1)}, u32[]{:S(2)}, u32[]{:S(2)}) async-start(bf16[2,4,72,1152]{3,2,0,1:T(8,128)(2,1)} %copy.125), calls=%async_computation.5 | async-start | bytes 2654208 | tf_op jit(solution)/shard_map/all_to_all | solution.py:115
  184.1 5.8 %slice_bitcast_fusion.1 = (bf16[576,2048]{1,0:T(8,128)(2,1)}, bf16[576,2048]{1,0:T(8,128)(2,1)S(1)}) fusion(bf16[2,576,2176]{2,1,0:T(8,128)(2,1)} %all-gather.5.cloned.1.call-done), kind=kLoop, calls=%fused_computation.32 | loop fusion | bytes 9437184 | tf_op jit(solution)/shard_map/squeeze | solution.py:74
  189.8 1.4 copy-done.10
  191.3 3.9 %fusion.18 = bf16[1,2048,384]{2,1,0:T(8,128)(2,1)} fusion(bf16[576,2048]{1,0:T(8,128)(2,1)S(1)} %get-tuple-element.48, bf16[576,2048]{1,0:T(8,128)(2,1)S(1)} %copy-done.8, bf16[576,384]{1,0:T(8,128)(2,1)S(1)} %copy-done.12, bf16[576,384]{1,0:T(8,128)(2,1)S(1)} %copy-done.14), kind=kOutput, calls=%fused_computation.22 | convolution fusion | flops 1823932416 | bytes 7176192 | tf_op jit(solution)/shard_map/dot_general | solution.py:143
  195.2 1.9 convert_element_type.315
  197.1 1.2 copy.111
  198.3 2.7 %all-to-all-done.3 = bf16[2,4,72,1152]{3,2,0,1:T(8,128)(2,1)S(1)} async-done(((bf16[2,4,72,1152]{3,2,0,1:T(8,128)(2,1)}), bf16[2,4,72,1152]{3,2,0,1:T(8,128)(2,1)S(1)}, u32[]{:S(2)}, u32[]{:S(2)}) %all-to-all-start.3) | async-done | bytes 1327136 | tf_op jit(solution)/shard_map/all_to_all | solution.py:115
  200.9 4.5 %all-to-all-start.1 = ((bf16[2,4,72,1152]{3,2,0,1:T(8,128)(2,1)}), bf16[2,4,72,1152]{3,2,0,1:T(8,128)(2,1)}, u32[]{:S(2)}, u32[]{:S(2)}) async-start(bf16[2,4,72,1152]{3,2,0,1:T(8,128)(2,1)} %copy.111), calls=%async_computation.2 | async-start | bytes 2654208 | tf_op jit(solution)/shard_map/all_to_all | solution.py:115
  205.5 6.5 %fusion.19 = bf16[1,2048,384]{2,1,0:T(8,128)(2,1)} fusion(bf16[576,2048]{1,0:T(8,128)(2,1)} %copy-done.10, bf16[576,2048]{1,0:T(8,128)(2,1)} %get-tuple-element.46, bf16[576,384]{1,0:T(8,128)(2,1)S(1)} %copy-done.16, bf16[576,384]{1,0:T(8,128)(2,1)S(1)} %copy-done.18), kind=kOutput, calls=%fused_computation.23 | convolution fusion | flops 1823932416 | bytes 7176192 | tf_op jit(solution)/shard_map/dot_general | solution.py:139
  212.0 3.4 %fusion.15 = bf16[1,384,2048]{2,1,0:T(8,128)(2,1)} fusion(bf16[576,2048]{1,0:T(8,128)(2,1)S(1)} %copy-done.9, bf16[576,2048]{1,0:T(8,128)(2,1)S(1)} %copy-done.7, bf16[576,384]{1,0:T(8,128)(2,1)S(1)} %copy-done.22, bf16[576,384]{1,0:T(8,128)(2,1)S(1)} %copy-done.23), kind=kOutput, calls=%fused_computation.21 | convolution fusion | flops 1823932416 | bytes 7176192 | tf_op jit(solution)/shard_map/dot_general | solution.py:147
  215.7 1.0 convolution_convert_fusion.4
  217.0 4.4 %all-to-all-done.1 = bf16[2,4,72,1152]{3,2,0,1:T(8,128)(2,1)} async-done(((bf16[2,4,72,1152]{3,2,0,1:T(8,128)(2,1)}), bf16[2,4,72,1152]{3,2,0,1:T(8,128)(2,1)}, u32[]{:S(2)}, u32[]{:S(2)}) %all-to-all-start.1) | async-done | bytes 1327136 | tf_op jit(solution)/shard_map/all_to_all | solution.py:115
  221.5 1.4 copy.112
  223.4 1.1 select_reduce_fusion
  225.3 1.8 fusion.101
  227.1 2.1 collective-permute-start.5
  229.1 0.7 fusion.100
  229.9 2.0 collective-permute-start.4
  232.4 0.8 fusion.99
  233.1 1.8 collective-permute-start.1
  235.8 3.4 %collective-permute-done.5 = bf16[128,1152]{1,0:T(8,128)(2,1)} collective-permute-done((bf16[128,1152]{1,0:T(8,128)(2,1)}, bf16[128,1152]{1,0:T(8,128)(2,1)}, u32[]{:S(2)}, u32[]{:S(2)}) %collective-permute-start.5) | collective-permute-done | bytes 294944 | tf_op jit(solution)/shard_map/ppermute | solution.py:130
  239.2 10.6 %collective-permute-done.4 = bf16[128,1152]{1,0:T(8,128)(2,1)} collective-permute-done((bf16[128,1152]{1,0:T(8,128)(2,1)}, bf16[128,1152]{1,0:T(8,128)(2,1)}, u32[]{:S(2)}, u32[]{:S(2)}) %collective-permute-start.4) | collective-permute-done | bytes 294944 | tf_op jit(solution)/shard_map/ppermute | solution.py:130
  249.8 1.2 add_convert_fusion
  251.1 0.7 slice.165
  (135 shorter events, 19.0 us)
Async XLA Ops:
  7.2 140.6 %copy-start = (bf16[1,384,2048]{2,1,0:T(8,128)(2,1)S(1)}, bf16[1,384,2048]{2,1,0:T(8,128)(2,1)}, u32[]{:S(2)}) copy-start(bf16[1,384,2048]{2,1,0:T(8,128)(2,1)} %param.13) | copy-start | bytes 4718596
  12.2 18.4 %collective-permute-start.3 = (bf16[128,2176]{0,1:T(8,128)(2,1)}, bf16[128,2176]{0,1:T(8,128)(2,1)S(1)}, u32[]{:S(2)}, u32[]{:S(2)}) collective-permute-start(bf16[128,2176]{0,1:T(8,128)(2,1)} %pad_maximum_fusion.15), channel_id=1, source_target_pairs={{0,24},{8,0},{16,8},{24,16},{1,25},{9,1},{17,9},{25,17},{2,26},{10... | collective-permute-start | bytes 1671176 | tf_op jit(solution)/shard_map/ppermute | solution.py:25
  17.3 36.0 %collective-permute-start.2 = (bf16[128,2176]{0,1:T(8,128)(2,1)}, bf16[128,2176]{0,1:T(8,128)(2,1)}, u32[]{:S(2)}, u32[]{:S(2)}) collective-permute-start(bf16[128,2176]{0,1:T(8,128)(2,1)} %pad_maximum_fusion.15), channel_id=1, source_target_pairs={{0,16},{8,24},{16,0},{24,8},{1,17},{9,25},{17,1},{25,9},{2,18},{10... | collective-permute-start | bytes 1671176 | tf_op jit(solution)/shard_map/ppermute | solution.py:25
  61.7 33.3 %all-to-all-start.2 = ((bf16[2,4,72,2176]{3,2,0,1:T(8,128)(2,1)}), bf16[2,4,72,2176]{3,2,0,1:T(8,128)(2,1)}, u32[]{:S(2)}, u32[]{:S(2)}) async-start(bf16[2,4,72,2176]{3,2,0,1:T(8,128)(2,1)} %pad_maximum_fusion.14), calls=%async_computation.3 | async-start | bytes 5013504 | tf_op jit(solution)/shard_map/all_to_all | solution.py:69
  66.2 75.3 %all-gather.5.cloned.1.call-start = ((), (), s32[]{:S(2)}) async-start(), calls=%async_computation.8 | async-start | bytes 7520256 | tf_op jit(solution)/shard_map/all_gather | solution.py:72
  66.3 34.9 %collective-permute-start = (bf16[128,2176]{0,1:T(8,128)(2,1)}, bf16[128,2176]{0,1:T(8,128)(2,1)}, u32[]{:S(2)}, u32[]{:S(2)}) collective-permute-start(bf16[128,2176]{0,1:T(8,128)(2,1)} %pad_maximum_fusion.15), channel_id=1, source_target_pairs={{0,8},{8,16},{16,24},{24,0},{1,9},{9,17},{17,25},{25,1},{2,10},{10... | collective-permute-start | bytes 1671176 | tf_op jit(solution)/shard_map/ppermute | solution.py:25
  98.3 0.7 copy-start.21
  98.3 58.5 %all-gather.3.cloned.1.call-start = ((), (), s32[]{:S(2)}) async-start(), calls=%async_computation.6 | async-start | bytes 7520256 | tf_op jit(solution)/shard_map/all_gather | solution.py:72
  105.7 2.0 copy-start.19
  141.2 1.5 copy-start.2
  141.3 36.1 %reduce-scatter.5.cloned.1.call-start = ((), (), s32[]{:S(2)}) async-start(), calls=%async_computation.9 | async-start | bytes 7962624 | tf_op jit(solution)/shard_map/reduce_scatter | solution.py:112
  142.7 3.2 %copy-start.3 = (bf16[1,2048,384]{2,1,0:T(8,128)(2,1)S(1)}, bf16[1,2048,384]{2,1,0:T(8,128)(2,1)}, u32[]{:S(2)}) copy-start(bf16[1,2048,384]{2,1,0:T(8,128)(2,1)} %param.12) | copy-start | bytes 4718596
  142.7 3.6 %copy-start.5 = (bf16[2,576,2176]{2,1,0:T(8,128)(2,1)S(1)}, bf16[2,576,2176]{2,1,0:T(8,128)(2,1)}, u32[]{:S(2)}) copy-start(bf16[2,576,2176]{2,1,0:T(8,128)(2,1)} %all-gather.5.cloned.1.call-done) | copy-start | bytes 15040516
  150.3 1.2 copy-start.15
  150.3 2.8 %copy-start.11 = (bf16[576,384]{1,0:T(8,128)(2,1)}, bf16[576,384]{1,0:T(8,128)(2,1)S(1)}, u32[]{:S(2)}) copy-start(bf16[576,384]{1,0:T(8,128)(2,1)S(1)} %get-tuple-element.53) | copy-start | bytes 1327108
  156.8 38.4 %reduce-scatter.3.cloned.1.call-start = ((), (), s32[]{:S(2)}) async-start(), calls=%async_computation.7 | async-start | bytes 7962624 | tf_op jit(solution)/shard_map/reduce_scatter | solution.py:112
  157.9 3.2 %copy-start.4 = (bf16[1,2048,384]{2,1,0:T(8,128)(2,1)S(1)}, bf16[1,2048,384]{2,1,0:T(8,128)(2,1)}, u32[]{:S(2)}) copy-start(bf16[1,2048,384]{2,1,0:T(8,128)(2,1)} %param.12) | copy-start | bytes 4718596
  157.9 3.6 %copy-start.6 = (bf16[2,576,2176]{2,1,0:T(8,128)(2,1)S(1)}, bf16[2,576,2176]{2,1,0:T(8,128)(2,1)}, u32[]{:S(2)}) copy-start(bf16[2,576,2176]{2,1,0:T(8,128)(2,1)} %all-gather.3.cloned.1.call-done) | copy-start | bytes 15040516
  165.4 1.2 copy-start.17
  165.4 2.8 %copy-start.13 = (bf16[576,384]{1,0:T(8,128)(2,1)}, bf16[576,384]{1,0:T(8,128)(2,1)S(1)}, u32[]{:S(2)}) copy-start(bf16[576,384]{1,0:T(8,128)(2,1)S(1)} %get-tuple-element.49) | copy-start | bytes 1327108
  180.5 20.5 %all-to-all-start.3 = ((bf16[2,4,72,1152]{3,2,0,1:T(8,128)(2,1)}), bf16[2,4,72,1152]{3,2,0,1:T(8,128)(2,1)S(1)}, u32[]{:S(2)}, u32[]{:S(2)}) async-start(bf16[2,4,72,1152]{3,2,0,1:T(8,128)(2,1)} %copy.125), calls=%async_computation.5 | async-start | bytes 2654208 | tf_op jit(solution)/shard_map/all_to_all | solution.py:115
  184.0 7.2 %copy-start.8 = (bf16[576,2048]{1,0:T(8,128)(2,1)S(1)}, bf16[576,2048]{1,0:T(8,128)(2,1)}, u32[]{:S(2)}) copy-start(bf16[576,2048]{1,0:T(8,128)(2,1)} %get-tuple-element.46) | copy-start | bytes 7077892
  184.0 7.2 %copy-start.12 = (bf16[576,384]{1,0:T(8,128)(2,1)S(1)}, bf16[576,384]{1,0:T(8,128)(2,1)}, u32[]{:S(2)}) copy-start(bf16[576,384]{1,0:T(8,128)(2,1)} %copy-done.11) | copy-start | bytes 1327108
  184.0 7.2 %copy-start.14 = (bf16[576,384]{1,0:T(8,128)(2,1)S(1)}, bf16[576,384]{1,0:T(8,128)(2,1)}, u32[]{:S(2)}) copy-start(bf16[576,384]{1,0:T(8,128)(2,1)} %copy-done.13) | copy-start | bytes 1327108
  189.8 1.4 copy-start.10
  197.1 8.4 %copy-start.16 = (bf16[576,384]{1,0:T(8,128)(2,1)S(1)}, bf16[576,384]{1,0:T(8,128)(2,1)}, u32[]{:S(2)}) copy-start(bf16[576,384]{1,0:T(8,128)(2,1)} %copy-done.15) | copy-start | bytes 1327108
  197.1 8.4 %copy-start.18 = (bf16[576,384]{1,0:T(8,128)(2,1)S(1)}, bf16[576,384]{1,0:T(8,128)(2,1)}, u32[]{:S(2)}) copy-start(bf16[576,384]{1,0:T(8,128)(2,1)} %copy-done.17) | copy-start | bytes 1327108
  200.9 20.5 %all-to-all-start.1 = ((bf16[2,4,72,1152]{3,2,0,1:T(8,128)(2,1)}), bf16[2,4,72,1152]{3,2,0,1:T(8,128)(2,1)}, u32[]{:S(2)}, u32[]{:S(2)}) async-start(bf16[2,4,72,1152]{3,2,0,1:T(8,128)(2,1)} %copy.111), calls=%async_computation.2 | async-start | bytes 2654208 | tf_op jit(solution)/shard_map/all_to_all | solution.py:115
  205.5 6.5 %copy-start.7 = (bf16[576,2048]{1,0:T(8,128)(2,1)S(1)}, bf16[576,2048]{1,0:T(8,128)(2,1)}, u32[]{:S(2)}) copy-start(bf16[576,2048]{1,0:T(8,128)(2,1)} %get-tuple-element.45) | copy-start | bytes 7077892
  205.5 6.5 %copy-start.9 = (bf16[576,2048]{1,0:T(8,128)(2,1)S(1)}, bf16[576,2048]{1,0:T(8,128)(2,1)}, u32[]{:S(2)}) copy-start(bf16[576,2048]{1,0:T(8,128)(2,1)} %get-tuple-element.47) | copy-start | bytes 7077892
  205.5 6.5 %copy-start.22 = (bf16[576,384]{1,0:T(8,128)(2,1)S(1)}, bf16[576,384]{1,0:T(8,128)(2,1)}, u32[]{:S(2)}) copy-start(bf16[576,384]{1,0:T(8,128)(2,1)} %get-tuple-element.55) | copy-start | bytes 1327108
  205.5 6.5 %copy-start.23 = (bf16[576,384]{1,0:T(8,128)(2,1)S(1)}, bf16[576,384]{1,0:T(8,128)(2,1)}, u32[]{:S(2)}) copy-start(bf16[576,384]{1,0:T(8,128)(2,1)} %get-tuple-element.51) | copy-start | bytes 1327108
  215.7 7.4 %copy-start.20 = (bf16[288,128]{1,0:T(8,128)(2,1)S(1)}, bf16[288,128]{1,0:T(8,128)(2,1)}, u32[]{:S(2)}) copy-start(bf16[288,128]{1,0:T(8,128)(2,1)} %copy-done.19) | copy-start | bytes 221188
  225.2 27.3 %copy-start.1 = (bf16[1,384,2048]{2,1,0:T(8,128)(2,1)S(1)}, bf16[1,384,2048]{2,1,0:T(8,128)(2,1)}, u32[]{:S(2)}) copy-start(bf16[1,384,2048]{2,1,0:T(8,128)(2,1)} %param.13) | copy-start | bytes 4718596
  227.1 12.2 %collective-permute-start.5 = (bf16[128,1152]{1,0:T(8,128)(2,1)}, bf16[128,1152]{1,0:T(8,128)(2,1)}, u32[]{:S(2)}, u32[]{:S(2)}) collective-permute-start(bf16[128,1152]{1,0:T(8,128)(2,1)} %fusion.101), channel_id=1, source_target_pairs={{0,8},{8,16},{16,24},{24,0},{1,9},{9,17},{17,25},{25,1},{2,10},{10... | collective-permute-start | bytes 884744 | tf_op jit(solution)/shard_map/ppermute | solution.py:130
  229.9 20.0 %collective-permute-start.4 = (bf16[128,1152]{1,0:T(8,128)(2,1)}, bf16[128,1152]{1,0:T(8,128)(2,1)}, u32[]{:S(2)}, u32[]{:S(2)}) collective-permute-start(bf16[128,1152]{1,0:T(8,128)(2,1)} %fusion.100), channel_id=1, source_target_pairs={{0,16},{8,24},{16,0},{24,8},{1,17},{9,25},{17,1},{25,9},{2,18},{10... | collective-permute-start | bytes 884744 | tf_op jit(solution)/shard_map/ppermute | solution.py:130
  233.1 16.7 %collective-permute-start.1 = (bf16[128,1152]{1,0:T(8,128)(2,1)}, bf16[128,1152]{1,0:T(8,128)(2,1)S(1)}, u32[]{:S(2)}, u32[]{:S(2)}) collective-permute-start(bf16[128,1152]{1,0:T(8,128)(2,1)} %fusion.99), channel_id=1, source_target_pairs={{0,24},{8,0},{16,8},{24,16},{1,25},{9,1},{17,9},{25,17},{2,26},{10... | collective-permute-start | bytes 884744 | tf_op jit(solution)/shard_map/ppermute | solution.py:130
Sparse Core Ops, SparseCore 0:
  98.5 15.4 all-gather.4
  141.4 14.6 all-gather.2
  158.4 14.4 reduce-scatter.4
  175.0 14.5 reduce-scatter.2
where the time goes:
time: 264 us; the launch traced here: 259 us
  waiting for transfers between devices  81.7 us (31%)
  matrix products  42.5 us (16%)
  other arithmetic  33.3 us (13%)
  blocking collectives  32 us (12%)
  local copies, waits for them, and re-layouts  30.2 us (11%)
  starting transfers between devices  24.8 us (9%)
  between operations  14.5 us (5%)
    ppermute x3, waiting for transfers between devices, on_device(): lax.ppermute(ext, 'dp', [(i, (i + s) % n_dp) for i in range(n_dp)])  33.5 us
    all_to_all x1, blocking collectives, on_device(): lax.all_to_all(send.reshape(n_mem, n_ex, capacity, features + lanes), 'ex...  32 us
    all_to_all x1, waiting for transfers between devices, on_device(): lax.all_to_all(send.reshape(n_mem, n_ex, capacity, features + lanes), 'ex...  27 us
    ppermute x3, waiting for transfers between devices, on_device(): part = lax.ppermute(part, 'dp', [(i, (i - s) % n_dp) for i in range(n_dp)])  14 us
    squeeze x2, local copies, waits for them, and re-layouts, on_device(): routed_dy = both[1, :, :features]  11.3 us
    all_to_all x2, starting transfers between devices, on_device(): lax.all_to_all(ret.reshape(n_mem, n_ex, capacity, half + lanes), 'expert'...  8.07 us
    unnamed x55, local copies, waits for them, and re-layouts  7.37 us
    all_to_all x2, waiting for transfers between devices, on_device(): lax.all_to_all(ret.reshape(n_mem, n_ex, capacity, half + lanes), 'expert'...  7.11 us
  transfers between devices with their start and end apart: 13, of which 7 were waited for; matrix products, arithmetic and copies ran while one was open for 31% of the time, Pallas kernels for 0%

commit v1 on v0

--- a/solution.py
+++ b/solution.py
@@ -37,8 +37,7 @@
     rows_x, rows_dy, rows_pre, rows_up, rows_w = [], [], [], [], []
     col_parts = []
     anchors = []
-    pair = 2 if n_dp % 2 == 0 else 1
-    groups_of = [list(range(g, g + pair)) for g in range(0, n_dp, pair)]
+    groups_of = [[0]] + ([list(range(1, n_dp))] if n_dp > 1 else [])
     for gi, members in enumerate(groups_of):
         sends, selects, matches = [], [], []
         for s in members:

time: 264 us -> 263 us (level); the launches traced: 259 us -> 262 us
  waiting for transfers between devices: 81.7 us -> 118 us
  blocking collectives: 32 us -> 0 us
  local copies, waits for them, and re-layouts: 30.2 us -> 25.3 us
  starting transfers between devices: 24.8 us -> 28.9 us
    all_to_all x1 -> x0, blocking collectives: 32 us -> none  [on_device(): lax.all_to_all(send.reshape(n_mem, n_ex, capacity, features + lanes), 'ex...]
    all_gather x2, waiting for transfers between devices: 0.04 us -> 17.4 us  [on_device(): both = lax.all_gather(recv, 'tensor')]
    all_to_all x1 -> x2, waiting for transfers between devices: 27 us -> 42.3 us  [on_device(): lax.all_to_all(send.reshape(n_mem, n_ex, capacity, features + lanes), 'ex...]
    ppermute x3, waiting for transfers between devices: 33.5 us -> 23.2 us  [on_device(): lax.ppermute(ext, 'dp', [(i, (i + s) % n_dp) for i in range(n_dp)])]
    all_to_all x2, waiting for transfers between devices: 7.11 us -> 17.2 us  [on_device(): lax.all_to_all(ret.reshape(n_mem, n_ex, capacity, half + lanes), 'expert'...]
    all_to_all x1 -> x2, starting transfers between devices: 4.55 us -> 8.47 us  [on_device(): lax.all_to_all(send.reshape(n_mem, n_ex, capacity, features + lanes), 'ex...]
    unnamed x55 -> x53, local copies, waits for them, and re-layouts: 7.37 us -> 5.84 us
  transfers between devices with their start and end apart: 13 -> 14, of which waited for: 7 -> 8; matrix products, arithmetic and copies ran while one was open for 31% -> 33% of each run, Pallas kernels for 0% -> 0%
where the time goes in v1:
time: 263 us; the launch traced here: 262 us
  waiting for transfers between devices  118 us (45%)
  matrix products  42.5 us (16%)
  other arithmetic  33 us (13%)
  starting transfers between devices  28.9 us (11%)
  local copies, waits for them, and re-layouts  25.3 us (10%)
  between operations  14.5 us (6%)
    all_to_all x2, waiting for transfers between devices, on_device(): lax.all_to_all(send.reshape(n_mem, n_ex, capacity, features + lanes), 'ex...  42.3 us
    ppermute x3, waiting for transfers between devices, on_device(): lax.ppermute(ext, 'dp', [(i, (i + s) % n_dp) for i in range(n_dp)])  23.2 us
    all_gather x2, waiting for transfers between devices, on_device(): both = lax.all_gather(recv, 'tensor')  17.4 us
    all_to_all x2, waiting for transfers between devices, on_device(): lax.all_to_all(ret.reshape(n_mem, n_ex, capacity, half + lanes), 'expert'...  17.2 us
    ppermute x3, waiting for transfers between devices, on_device(): part = lax.ppermute(part, 'dp', [(i, (i - s) % n_dp) for i in range(n_dp)])  16 us
    squeeze x2, local copies, waits for them, and re-layouts, on_device(): routed_dy = both[1, :, :features]  9.42 us
    all_to_all x2, starting transfers between devices, on_device(): lax.all_to_all(send.reshape(n_mem, n_ex, capacity, features + lanes), 'ex...  8.47 us
    all_to_all x2, starting transfers between devices, on_device(): lax.all_to_all(ret.reshape(n_mem, n_ex, capacity, half + lanes), 'expert'...  8.33 us
  transfers between devices with their start and end apart: 14, of which 8 were waited for; matrix products, arithmetic and copies ran while one was open for 33% of the time, Pallas kernels for 0%

profile of v1, /device:TPU:0, one launch (start us, length us, event | category | flops | bytes accessed | tf_op | source)
XLA Modules:
  0.0 261.8 jit_solution(5930041036359984847)
XLA Ops:
  7.2 1.4 copy.97
  8.6 1.3 copy.98
  10.1 0.8 pad_maximum_fusion.14
  10.9 3.0 %collective-permute-start = (bf16[128,2176]{0,1:T(8,128)(2,1)}, bf16[128,2176]{0,1:T(8,128)(2,1)}, u32[]{:S(2)}, u32[]{:S(2)}) collective-permute-start(bf16[128,2176]{0,1:T(8,128)(2,1)} %pad_maximum_fusion.14), channel_id=1, source_target_pairs={{0,8},{8,16},{16,24},{24,0},{1,9},{9,17},{17,25},{25,1},{2,10},{10... | collective-permute-start | bytes 1671176 | tf_op jit(solution)/shard_map/ppermute | solution.py:25
  13.9 2.6 collective-permute-start.1
  16.5 1.3 collective-permute-start.2
  19.2 1.1 select_reduce_fusion.7
  20.8 1.1 fusion.39
  22.0 3.7 %all-to-all-start = ((bf16[1,4,72,2176]{3,2,0,1:T(8,128)(2,1)}), bf16[1,4,72,2176]{3,2,0,1:T(8,128)(2,1)S(1)}, u32[]{:S(2)}, u32[]{:S(2)}) async-start(bf16[1,4,72,2176]{3,2,0,1:T(8,128)(2,1)} %bitcast.122), calls=%async_computation | async-start | bytes 2506752 | tf_op jit(solution)/shard_map/all_to_all | solution.py:68
  25.7 4.2 %collective-permute-done = bf16[128,2176]{0,1:T(8,128)(2,1)} collective-permute-done((bf16[128,2176]{0,1:T(8,128)(2,1)}, bf16[128,2176]{0,1:T(8,128)(2,1)}, u32[]{:S(2)}, u32[]{:S(2)}) %collective-permute-start) | collective-permute-done | bytes 557088 | tf_op jit(solution)/shard_map/ppermute | solution.py:25
  31.4 0.7 slice_convert_fusion.2
  32.1 0.7 add_select_fusion.2
  32.8 1.1 select_reduce_fusion.5
  33.9 19.0 %collective-permute-done.1 = bf16[128,2176]{0,1:T(8,128)(2,1)} collective-permute-done((bf16[128,2176]{0,1:T(8,128)(2,1)}, bf16[128,2176]{0,1:T(8,128)(2,1)}, u32[]{:S(2)}, u32[]{:S(2)}) %collective-permute-start.1) | collective-permute-done | bytes 557088 | tf_op jit(solution)/shard_map/ppermute | solution.py:25
  54.4 0.7 add_select_fusion.1
  55.8 1.1 select_reduce_fusion.4
  57.8 0.7 convert_subtract_fusion
  59.3 0.7 add_select_fusion
  60.5 1.5 convolution_convert_fusion.2
  62.2 1.5 convolution_convert_fusion.1
  64.5 1.5 convolution_convert_fusion
  66.0 1.1 select_reduce_fusion.3
  67.3 2.1 pad_maximum_fusion.2
  69.4 1.0 copy-done.6
  70.4 4.8 %all-to-all-start.2 = ((bf16[3,4,72,2176]{3,2,0,1:T(8,128)(2,1)}), bf16[3,4,72,2176]{3,2,0,1:T(8,128)(2,1)}, u32[]{:S(2)}, u32[]{:S(2)}) async-start(bf16[3,4,72,2176]{3,2,0,1:T(8,128)(2,1)} %pad_maximum_fusion.2), calls=%async_computation.3 | async-start | bytes 7520256 | tf_op jit(solution)/shard_map/all_to_all | solution.py:68
  75.2 0.7 all-gather.3.cloned.1.call-update
  75.9 42.3 %all-to-all-done.2 = bf16[3,4,72,2176]{3,2,0,1:T(8,128)(2,1)} async-done(((bf16[3,4,72,2176]{3,2,0,1:T(8,128)(2,1)}), bf16[3,4,72,2176]{3,2,0,1:T(8,128)(2,1)}, u32[]{:S(2)}, u32[]{:S(2)}) %all-to-all-start.2) | async-done | bytes 3760160 | tf_op jit(solution)/shard_map/all_to_all | solution.py:68
  118.3 4.2 %copy.116 = bf16[3,4,72,2176]{3,2,1,0:T(8,128)(2,1)} copy(bf16[3,4,72,2176]{3,2,0,1:T(8,128)(2,1)} %all-to-all-done.2) | data formatting | bytes 7520256 | tf_op jit(solution)/shard_map/all_to_all | solution.py:68
  122.7 1.1 convert_reduce_fusion.5
  123.9 2.2 fusion.26
  126.4 0.8 fusion.30
  127.2 1.6 multiply_convert_fusion.4
  131.2 1.7 pad_maximum_fusion.9
  133.0 17.4 %all-gather.5.cloned.1.call-done = bf16[2,864,2176]{2,1,0:T(8,128)(2,1)} async-done(((bf16[1,864,2176]{2,1,0:T(8,128)(2,1)}), bf16[2,864,2176]{2,1,0:T(8,128)(2,1)}) %all-gather.5.cloned.1.call-update) | async-done | bytes 7520272 | tf_op jit(solution)/shard_map/all_gather | solution.py:71
  150.3 1.1 convert_reduce_fusion
  151.4 4.1 %fusion.24 = f32[864,384]{1,0:T(8,128)S(1)} fusion(bf16[1,2048,384]{2,1,0:T(8,128)(2,1)S(1)} %copy-done.3, bf16[2,864,2176]{2,1,0:T(8,128)(2,1)} %all-gather.5.cloned.1.call-done), kind=kOutput, calls=%fused_computation.36 | convolution fusion | flops 1358954496 | bytes 6438912 | tf_op jit(solution)/shard_map/dot_general | solution.py:76
  156.0 2.0 fusion.28
  158.0 3.5 %multiply_convert_fusion.1 = (bf16[864,384]{1,0:T(8,128)(2,1)S(1)}, bf16[864,384]{1,0:T(8,128)(2,1)S(1)}, bf16[864,384]{1,0:T(8,128)(2,1)}, bf16[864,384]{1,0:T(8,128)(2,1)S(1)}, f32[864,384]{1,0:T(8,128)S(1)}) fusion(f32[864]{0:T(1024)S(1)} %convert_reduce_fusion, f32[864,384]{1,0:T(8,128)S(1)} %fusion.24, f32[864,384]{1,0:T(8,128)S(1)} %fusion.28, ...), kind=kOutput, calls=%fused_computation.53 | convolution fusion | flops 1365258240 | bytes 11751424 | tf_op jit(solution)/shard_map/dot_general | solution.py:81
  161.9 1.1 fusion.72
  163.0 1.1 fusion.66
  164.2 1.1 convolution_add_fusion.1
  165.3 1.1 convolution_add_fusion
  166.5 3.5 %pad_maximum_fusion = f32[864,2304]{1,0:T(8,128)} fusion(f32[864,128]{1,0:T(8,128)S(1)} %pad.49, f32[864,1024]{1,0:T(8,128)S(1)} %convolution_add_fusion, f32[864,1024]{1,0:T(8,128)S(1)} %convolution_add_fusion.1), kind=kLoop, calls=%fused_computation | loop fusion | flops 5971968 | bytes 15482880 | tf_op jit(solution)/shard_map/concatenate | solution.py:112
  170.0 2.2 convert_element_type.308
  172.2 3.9 %all-to-all-start.1 = ((bf16[1,4,72,1152]{3,2,0,1:T(8,128)(2,1)}), bf16[1,4,72,1152]{3,2,0,1:T(8,128)(2,1)S(1)}, u32[]{:S(2)}, u32[]{:S(2)}) async-start(bf16[1,4,72,1152]{3,2,0,1:T(8,128)(2,1)} %bitcast.13), calls=%async_computation.2 | async-start | bytes 1327104 | tf_op jit(solution)/shard_map/all_to_all | solution.py:114
  176.1 3.5 %slice_bitcast_fusion.3 = (bf16[288,2048]{1,0:T(8,128)(2,1)S(1)}, bf16[288,2048]{1,0:T(8,128)(2,1)}) fusion(bf16[2,288,2176]{2,1,0:T(8,128)(2,1)} %all-gather.3.cloned.1.call-done), kind=kLoop, calls=%fused_computation.66 | loop fusion | bytes 4718592 | tf_op jit(solution)/shard_map/squeeze | solution.py:73
  179.6 6.5 %all-to-all-done.1 = bf16[1,4,72,1152]{3,2,0,1:T(8,128)(2,1)S(1)} async-done(((bf16[1,4,72,1152]{3,2,0,1:T(8,128)(2,1)}), bf16[1,4,72,1152]{3,2,0,1:T(8,128)(2,1)S(1)}, u32[]{:S(2)}, u32[]{:S(2)}) %all-to-all-start.1) | async-done | bytes 663584 | tf_op jit(solution)/shard_map/all_to_all | solution.py:114
  187.1 0.8 reduce-scatter.5.cloned.1.call-done
  187.8 2.3 convert_element_type.342
  190.2 1.4 copy.118
  191.6 4.4 %all-to-all-start.3 = ((bf16[3,4,72,1152]{3,2,0,1:T(8,128)(2,1)}), bf16[3,4,72,1152]{3,2,0,1:T(8,128)(2,1)}, u32[]{:S(2)}, u32[]{:S(2)}) async-start(bf16[3,4,72,1152]{3,2,0,1:T(8,128)(2,1)} %copy.118), calls=%async_computation.5 | async-start | bytes 3981312 | tf_op jit(solution)/shard_map/all_to_all | solution.py:114
  196.1 6.0 %slice_bitcast_fusion.1 = (bf16[864,2048]{1,0:T(8,128)(2,1)}, bf16[864,2048]{1,0:T(8,128)(2,1)S(1)}) fusion(bf16[2,864,2176]{2,1,0:T(8,128)(2,1)} %all-gather.5.cloned.1.call-done), kind=kLoop, calls=%fused_computation.13 | loop fusion | bytes 14155776 | tf_op jit(solution)/shard_map/squeeze | solution.py:73
  202.1 4.0 %fusion.18 = bf16[1,2048,384]{2,1,0:T(8,128)(2,1)} fusion(bf16[864,2048]{1,0:T(8,128)(2,1)S(1)} %get-tuple-element.45, bf16[288,2048]{1,0:T(8,128)(2,1)S(1)} %copy-done.12, bf16[864,384]{1,0:T(8,128)(2,1)S(1)} %copy-done.8, bf16[288,384]{1,0:T(8,128)(2,1)S(1)} %copy-done.14), kind=kOutput, calls=%fused_computation.25 | convolution fusion | flops 1823932416 | bytes 7176192 | tf_op jit(solution)/shard_map/dot_general | solution.py:142
  206.0 3.9 %fusion.19 = bf16[1,2048,384]{2,1,0:T(8,128)(2,1)} fusion(bf16[864,2048]{1,0:T(8,128)(2,1)S(1)} %get-tuple-element.45, bf16[288,2048]{1,0:T(8,128)(2,1)S(1)} %copy-done.12, bf16[864,384]{1,0:T(8,128)(2,1)S(1)} %copy-done.10, bf16[288,384]{1,0:T(8,128)(2,1)S(1)} %get-tuple-element.53), kind=kOutput, calls=%fused_computation.26 | convolution fusion | flops 1823932416 | bytes 7176192 | tf_op jit(solution)/shard_map/dot_general | solution.py:138
  209.9 10.7 %all-to-all-done.3 = bf16[3,4,72,1152]{3,2,0,1:T(8,128)(2,1)} async-done(((bf16[3,4,72,1152]{3,2,0,1:T(8,128)(2,1)}), bf16[3,4,72,1152]{3,2,0,1:T(8,128)(2,1)}, u32[]{:S(2)}, u32[]{:S(2)}) %all-to-all-start.3) | async-done | bytes 1990688 | tf_op jit(solution)/shard_map/all_to_all | solution.py:114
  220.6 1.7 copy.119
  224.1 3.6 %collective-permute-start.3 = (bf16[128,1152]{1,0:T(8,128)(2,1)S(1)}, bf16[128,1152]{1,0:T(8,128)(2,1)}, u32[]{:S(2)}, u32[]{:S(2)}) collective-permute-start(bf16[128,1152]{1,0:T(8,128)(2,1)S(1)} %fusion.99), channel_id=1, source_target_pairs={{0,24},{8,0},{16,8},{24,16},{1,25},{9,1},{17,9},{25,17},{2,26},{10... | collective-permute-start | bytes 884744 | tf_op jit(solution)/shard_map/ppermute | solution.py:129
  227.7 1.1 select_reduce_fusion
  228.9 0.7 fusion.100
  229.7 1.2 collective-permute-start.5
  230.9 5.8 %fusion.15 = bf16[1,384,2048]{2,1,0:T(8,128)(2,1)} fusion(bf16[864,2048]{1,0:T(8,128)(2,1)} %get-tuple-element.44, bf16[288,2048]{1,0:T(8,128)(2,1)S(1)} %get-tuple-element.50, bf16[864,384]{1,0:T(8,128)(2,1)} %get-tuple-element.48, bf16[288,384]{1,0:T(8,128)(2,1)} %get-tuple-element.54), kind=kOutput, calls=%fused_computation.24 | convolution fusion | flops 1823932416 | bytes 7176192 | tf_op jit(solution)/shard_map/dot_general | solution.py:146
  236.7 15.9 %collective-permute-done.4 = bf16[128,1152]{1,0:T(8,128)(2,1)} collective-permute-done((bf16[128,1152]{1,0:T(8,128)(2,1)}, bf16[128,1152]{1,0:T(8,128)(2,1)}, u32[]{:S(2)}, u32[]{:S(2)}) %collective-permute-start.4) | collective-permute-done | bytes 294944 | tf_op jit(solution)/shard_map/ppermute | solution.py:129
  252.6 1.2 add_convert_fusion
  253.8 0.7 slice.165
  (130 shorter events, 16.5 us)
Async XLA Ops:
  7.2 120.0 %copy-start = (bf16[1,384,2048]{2,1,0:T(8,128)(2,1)S(1)}, bf16[1,384,2048]{2,1,0:T(8,128)(2,1)}, u32[]{:S(2)}) copy-start(bf16[1,384,2048]{2,1,0:T(8,128)(2,1)} %param.13) | copy-start | bytes 4718596
  7.2 2.8 %copy-start.22 = (s32[128,8]{0,1:T(8,128)S(1)}, s32[128,8]{0,1:T(8,128)}, u32[]{:S(2)}) copy-start(s32[128,8]{0,1:T(8,128)} %param.9) | copy-start | bytes 12292
  7.2 2.8 %copy-start.21 = (bf16[128,8]{0,1:T(8,128)(2,1)S(1)}, bf16[128,8]{0,1:T(8,128)(2,1)}, u32[]{:S(2)}) copy-start(bf16[128,8]{0,1:T(8,128)(2,1)} %param.10) | copy-start | bytes 6148
  10.9 19.0 %collective-permute-start = (bf16[128,2176]{0,1:T(8,128)(2,1)}, bf16[128,2176]{0,1:T(8,128)(2,1)}, u32[]{:S(2)}, u32[]{:S(2)}) collective-permute-start(bf16[128,2176]{0,1:T(8,128)(2,1)} %pad_maximum_fusion.14), channel_id=1, source_target_pairs={{0,8},{8,16},{16,24},{24,0},{1,9},{9,17},{17,25},{25,1},{2,10},{10... | collective-permute-start | bytes 1671176 | tf_op jit(solution)/shard_map/ppermute | solution.py:25
  13.9 39.0 %collective-permute-start.1 = (bf16[128,2176]{0,1:T(8,128)(2,1)}, bf16[128,2176]{0,1:T(8,128)(2,1)}, u32[]{:S(2)}, u32[]{:S(2)}) collective-permute-start(bf16[128,2176]{0,1:T(8,128)(2,1)} %pad_maximum_fusion.14), channel_id=1, source_target_pairs={{0,16},{8,24},{16,0},{24,8},{1,17},{9,25},{17,1},{25,9},{2,18},{10... | collective-permute-start | bytes 1671176 | tf_op jit(solution)/shard_map/ppermute | solution.py:25
  16.5 41.3 %collective-permute-start.2 = (bf16[128,2176]{0,1:T(8,128)(2,1)}, bf16[128,2176]{0,1:T(8,128)(2,1)}, u32[]{:S(2)}, u32[]{:S(2)}) collective-permute-start(bf16[128,2176]{0,1:T(8,128)(2,1)} %pad_maximum_fusion.14), channel_id=1, source_target_pairs={{0,24},{8,0},{16,8},{24,16},{1,25},{9,1},{17,9},{25,17},{2,26},{10... | collective-permute-start | bytes 1671176 | tf_op jit(solution)/shard_map/ppermute | solution.py:25
  22.0 47.4 %all-to-all-start = ((bf16[1,4,72,2176]{3,2,0,1:T(8,128)(2,1)}), bf16[1,4,72,2176]{3,2,0,1:T(8,128)(2,1)S(1)}, u32[]{:S(2)}, u32[]{:S(2)}) async-start(bf16[1,4,72,2176]{3,2,0,1:T(8,128)(2,1)} %bitcast.122), calls=%async_computation | async-start | bytes 2506752 | tf_op jit(solution)/shard_map/all_to_all | solution.py:68
  57.4 4.7 %copy-start.15 = (bf16[288,128]{1,0:T(8,128)(2,1)}, bf16[288,128]{1,0:T(8,128)(2,1)S(1)}, u32[]{:S(2)}) copy-start(bf16[288,128]{1,0:T(8,128)(2,1)S(1)} %fusion.85) | copy-start | bytes 221188
  60.1 5.9 %copy-start.19 = (s32[128,8]{0,1:T(8,128)}, s32[128,8]{0,1:T(8,128)S(1)}, u32[]{:S(2)}) copy-start(s32[128,8]{0,1:T(8,128)S(1)} %add_select_fusion) | copy-start | bytes 12292
  60.5 4.0 %copy-start.17 = (bf16[288,128]{1,0:T(8,128)(2,1)}, bf16[288,128]{1,0:T(8,128)(2,1)S(1)}, u32[]{:S(2)}) copy-start(bf16[288,128]{1,0:T(8,128)(2,1)S(1)} %fusion.87) | copy-start | bytes 221188
  69.4 1.0 copy-start.6
  70.4 47.9 %all-to-all-start.2 = ((bf16[3,4,72,2176]{3,2,0,1:T(8,128)(2,1)}), bf16[3,4,72,2176]{3,2,0,1:T(8,128)(2,1)}, u32[]{:S(2)}, u32[]{:S(2)}) async-start(bf16[3,4,72,2176]{3,2,0,1:T(8,128)(2,1)} %pad_maximum_fusion.2), calls=%async_computation.3 | async-start | bytes 7520256 | tf_op jit(solution)/shard_map/all_to_all | solution.py:68
  75.2 47.6 %all-gather.3.cloned.1.call-start = ((), (), s32[]{:S(2)}) async-start(), calls=%async_computation.6 | async-start | bytes 3760128 | tf_op jit(solution)/shard_map/all_gather | solution.py:71
  75.9 74.4 %all-gather.5.cloned.1.call-start = ((), (), s32[]{:S(2)}) async-start(), calls=%async_computation.8 | async-start | bytes 11280384 | tf_op jit(solution)/shard_map/all_gather | solution.py:71
  122.4 1.4 copy-start.3
  122.5 47.5 %reduce-scatter.3.cloned.1.call-start = ((), (), s32[]{:S(2)}) async-start(), calls=%async_computation.7 | async-start | bytes 3981312 | tf_op jit(solution)/shard_map/reduce_scatter | solution.py:111
  123.9 2.2 copy-start.4
  123.9 2.5 copy-start.11
  128.8 1.8 copy-start.13
  132.9 54.9 %reduce-scatter.5.cloned.1.call-start = ((), (), s32[]{:S(2)}) async-start(), calls=%async_computation.9 | async-start | bytes 11943936 | tf_op jit(solution)/shard_map/reduce_scatter | solution.py:111
  151.4 4.2 %copy-start.2 = (bf16[2,864,2176]{2,1,0:T(8,128)(2,1)S(1)}, bf16[2,864,2176]{2,1,0:T(8,128)(2,1)}, u32[]{:S(2)}) copy-start(bf16[2,864,2176]{2,1,0:T(8,128)(2,1)} %all-gather.5.cloned.1.call-done) | copy-start | bytes 22560772
  151.4 4.6 %copy-start.5 = (bf16[1,2048,384]{2,1,0:T(8,128)(2,1)S(1)}, bf16[1,2048,384]{2,1,0:T(8,128)(2,1)}, u32[]{:S(2)}) copy-start(bf16[1,2048,384]{2,1,0:T(8,128)(2,1)} %param.12) | copy-start | bytes 4718596
  161.5 1.6 copy-start.9
  161.5 3.8 %copy-start.7 = (bf16[864,384]{1,0:T(8,128)(2,1)}, bf16[864,384]{1,0:T(8,128)(2,1)S(1)}, u32[]{:S(2)}) copy-start(bf16[864,384]{1,0:T(8,128)(2,1)S(1)} %get-tuple-element.46) | copy-start | bytes 1990660
  172.2 13.9 %all-to-all-start.1 = ((bf16[1,4,72,1152]{3,2,0,1:T(8,128)(2,1)}), bf16[1,4,72,1152]{3,2,0,1:T(8,128)(2,1)S(1)}, u32[]{:S(2)}, u32[]{:S(2)}) async-start(bf16[1,4,72,1152]{3,2,0,1:T(8,128)(2,1)} %bitcast.13), calls=%async_computation.2 | async-start | bytes 1327104 | tf_op jit(solution)/shard_map/all_to_all | solution.py:114
  191.6 29.0 %all-to-all-start.3 = ((bf16[3,4,72,1152]{3,2,0,1:T(8,128)(2,1)}), bf16[3,4,72,1152]{3,2,0,1:T(8,128)(2,1)}, u32[]{:S(2)}, u32[]{:S(2)}) async-start(bf16[3,4,72,1152]{3,2,0,1:T(8,128)(2,1)} %copy.118), calls=%async_computation.5 | async-start | bytes 3981312 | tf_op jit(solution)/shard_map/all_to_all | solution.py:114
  196.0 6.0 %copy-start.8 = (bf16[864,384]{1,0:T(8,128)(2,1)S(1)}, bf16[864,384]{1,0:T(8,128)(2,1)}, u32[]{:S(2)}) copy-start(bf16[864,384]{1,0:T(8,128)(2,1)} %copy-done.7) | copy-start | bytes 1990660
  196.1 6.0 %copy-start.12 = (bf16[288,2048]{1,0:T(8,128)(2,1)S(1)}, bf16[288,2048]{1,0:T(8,128)(2,1)}, u32[]{:S(2)}) copy-start(bf16[288,2048]{1,0:T(8,128)(2,1)} %get-tuple-element.51) | copy-start | bytes 3538948
  196.1 6.0 %copy-start.14 = (bf16[288,384]{1,0:T(8,128)(2,1)S(1)}, bf16[288,384]{1,0:T(8,128)(2,1)}, u32[]{:S(2)}) copy-start(bf16[288,384]{1,0:T(8,128)(2,1)} %copy-done.13) | copy-start | bytes 663556
  202.0 4.0 %copy-start.10 = (bf16[864,384]{1,0:T(8,128)(2,1)S(1)}, bf16[864,384]{1,0:T(8,128)(2,1)}, u32[]{:S(2)}) copy-start(bf16[864,384]{1,0:T(8,128)(2,1)} %copy-done.9) | copy-start | bytes 1990660
  209.9 12.4 %copy-start.16 = (bf16[288,128]{1,0:T(8,128)(2,1)S(1)}, bf16[288,128]{1,0:T(8,128)(2,1)}, u32[]{:S(2)}) copy-start(bf16[288,128]{1,0:T(8,128)(2,1)} %copy-done.15) | copy-start | bytes 221188
  222.3 0.9 copy-start.18
  222.7 5.0 %copy-start.20 = (s32[128,8]{0,1:T(8,128)S(1)}, s32[128,8]{0,1:T(8,128)}, u32[]{:S(2)}) copy-start(s32[128,8]{0,1:T(8,128)} %copy-done.19) | copy-start | bytes 12292
  224.1 12.6 %collective-permute-start.3 = (bf16[128,1152]{1,0:T(8,128)(2,1)S(1)}, bf16[128,1152]{1,0:T(8,128)(2,1)}, u32[]{:S(2)}, u32[]{:S(2)}) collective-permute-start(bf16[128,1152]{1,0:T(8,128)(2,1)S(1)} %fusion.99), channel_id=1, source_target_pairs={{0,24},{8,0},{16,8},{24,16},{1,25},{9,1},{17,9},{25,17},{2,26},{10... | collective-permute-start | bytes 884744 | tf_op jit(solution)/shard_map/ppermute | solution.py:129
  229.6 23.0 %collective-permute-start.4 = (bf16[128,1152]{1,0:T(8,128)(2,1)}, bf16[128,1152]{1,0:T(8,128)(2,1)}, u32[]{:S(2)}, u32[]{:S(2)}) collective-permute-start(bf16[128,1152]{1,0:T(8,128)(2,1)} %fusion.100), channel_id=1, source_target_pairs={{0,16},{8,24},{16,0},{24,8},{1,17},{9,25},{17,1},{25,9},{2,18},{10... | collective-permute-start | bytes 884744 | tf_op jit(solution)/shard_map/ppermute | solution.py:129
  229.7 22.9 %collective-permute-start.5 = (bf16[128,1152]{1,0:T(8,128)(2,1)S(1)}, bf16[128,1152]{1,0:T(8,128)(2,1)S(1)}, u32[]{:S(2)}, u32[]{:S(2)}) collective-permute-start(bf16[128,1152]{1,0:T(8,128)(2,1)S(1)} %fusion.101), channel_id=1, source_target_pairs={{0,8},{8,16},{16,24},{24,0},{1,9},{9,17},{17,25},{25,1},{2,10},{10... | collective-permute-start | bytes 884744 | tf_op jit(solution)/shard_map/ppermute | solution.py:129
  230.9 24.3 %copy-start.1 = (bf16[1,384,2048]{2,1,0:T(8,128)(2,1)S(1)}, bf16[1,384,2048]{2,1,0:T(8,128)(2,1)}, u32[]{:S(2)}) copy-start(bf16[1,384,2048]{2,1,0:T(8,128)(2,1)} %param.13) | copy-start | bytes 4718596
Sparse Core Ops, SparseCore 0:
  78.1 22.6 all-gather.2
  122.6 27.7 all-gather.4
  152.6 11.3 reduce-scatter.2
  170.1 17.7 reduce-scatter.4

commit v2 on v1

--- a/solution.py
+++ b/solution.py
@@ -54,7 +54,13 @@
             key = jnp.where(in_plane, local_ex * capacity + position, -1).reshape(tok_rows, top_count)
             match = key[None, :, :] == q_iota[:, None, None]
             select = jnp.sum(match.astype(jnp.bfloat16), axis=2)
-            send_rows = jnp.dot(select, carried_b, preferred_element_type=jnp.float32).astype(tokens.dtype)
+            if s == 0:
+                send_rows = jnp.concatenate([
+                    jnp.dot(select, tokens, preferred_element_type=jnp.float32).astype(tokens.dtype),
+                    jnp.dot(select, grad_out, preferred_element_type=jnp.float32).astype(tokens.dtype),
+                ], axis=1)
+            else:
+                send_rows = jnp.dot(select, carried_b, preferred_element_type=jnp.float32).astype(tokens.dtype)
             send_gate = jnp.sum(jnp.where(match, gates_b[None, :, :], 0.0), axis=(1, 2))
             gate_cols = jnp.pad(send_gate.astype(tokens.dtype)[:, None], ((0, 0), (0, lanes - 1)))
             sends.append(jnp.concatenate([send_rows, gate_cols], axis=1))
@@ -65,13 +71,19 @@
 
         if gi >= 2:
             send = lax.optimization_barrier((send, anchors[gi - 2]))[0]
+        width = send.shape[-1]
         recv = lax.all_to_all(
-            send.reshape(n_mem, n_ex, capacity, features + lanes), "expert", split_axis=1, concat_axis=1, tiled=True
-        ).reshape(n_mem * block_slots, features + lanes)
-        both = lax.all_gather(recv, "tensor")
-        routed_x = both[0, :, :features]
-        routed_dy = both[1, :, :features]
-        routed_gate = both[0, :, features]
+            send.reshape(n_mem, n_ex, capacity, width), "expert", split_axis=1, concat_axis=1, tiled=True
+        ).reshape(n_mem * block_slots, width)
+        if members == [0]:
+            routed_x = recv[:, :features]
+            routed_dy = recv[:, features:2 * features]
+            routed_gate = recv[:, 2 * features]
+        else:
+            both = lax.all_gather(recv, "tensor")
+            routed_x = both[0, :, :features]
+            routed_dy = both[1, :, :features]
+            routed_gate = both[0, :, features]
 
         gate_pre = jnp.dot(routed_x, weight_g, preferred_element_type=jnp.float32)
         up_pre = jnp.dot(routed_x, weight_u, preferred_element_type=jnp.float32)

time: 263 us -> 270 us (1.027)
  blocking collectives: 0 us -> 77.6 us
  waiting for transfers between devices: 118 us -> 71.7 us
  starting transfers between devices: 28.9 us -> 19.6 us
  other arithmetic: 33 us -> 24.8 us
  local copies, waits for them, and re-layouts: 25.3 us -> 21.4 us
  matrix products: 42.5 us -> 39.4 us
    all_to_all x0 -> x2, blocking collectives: none -> 77.6 us  [on_device(): lax.all_to_all(send.reshape(n_mem, n_ex, capacity, width), 'expert', spli...]
    all_to_all x2 -> x0, waiting for transfers between devices: 42.3 us -> none  [on_device(): lax.all_to_all(send.reshape(n_mem, n_ex, capacity, features + lanes), 'ex...]
    all_gather x2 -> x1, waiting for transfers between devices: 17.4 us -> 0.02 us  [on_device(): both = lax.all_gather(recv, 'tensor')]
    all_to_all x2 -> x0, starting transfers between devices: 8.47 us -> none  [on_device(): lax.all_to_all(send.reshape(n_mem, n_ex, capacity, features + lanes), 'ex...]
    reduce_scatter x2, waiting for transfers between devices: 0.78 us -> 8.87 us  [on_device(): lax.psum_scatter(jnp.concatenate(pieces, axis=1), 'tensor', scatter_dimen...]
    ppermute x3, waiting for transfers between devices: 23.2 us -> 30.5 us  [on_device(): lax.ppermute(ext, 'dp', [(i, (i + s) % n_dp) for i in range(n_dp)])]
    squeeze x2 -> x1, local copies, waits for them, and re-layouts: 9.42 us -> 5.96 us  [on_device(): routed_dy = both[1, :, :features]]
    unnamed x53 -> x77, local copies, waits for them, and re-layouts: 5.84 us -> 7.27 us
  transfers between devices with their start and end apart: 14 -> 11, of which waited for: 8 -> 6; matrix products, arithmetic and copies ran while one was open for 33% -> 23% of each run, Pallas kernels for 0% -> 0%
where the time goes in v2:
time: 270 us; the launch traced here: 269 us
  blocking collectives  77.6 us (29%)
  waiting for transfers between devices  71.7 us (27%)
  matrix products  39.4 us (15%)
  other arithmetic  24.8 us (9%)
  local copies, waits for them, and re-layouts  21.4 us (8%)
  starting transfers between devices  19.6 us (7%)
  between operations  14.6 us (5%)
    all_to_all x2, blocking collectives, on_device(): lax.all_to_all(send.reshape(n_mem, n_ex, capacity, width), 'expert', spli...  77.6 us
    ppermute x3, waiting for transfers between devices, on_device(): lax.ppermute(ext, 'dp', [(i, (i + s) % n_dp) for i in range(n_dp)])  30.5 us
    all_to_all x2, waiting for transfers between devices, on_device(): lax.all_to_all(ret.reshape(n_mem, n_ex, capacity, half + lanes), 'expert'...  16.4 us
    ppermute x3, waiting for transfers between devices, on_device(): part = lax.ppermute(part, 'dp', [(i, (i - s) % n_dp) for i in range(n_dp)])  15.8 us
    reduce_scatter x2, waiting for transfers between devices, on_device(): lax.psum_scatter(jnp.concatenate(pieces, axis=1), 'tensor', scatter_dimen...  8.87 us
    all_to_all x2, starting transfers between devices, on_device(): lax.all_to_all(ret.reshape(n_mem, n_ex, capacity, half + lanes), 'expert'...  7.75 us
    unnamed x77, local copies, waits for them, and re-layouts  7.27 us
    ppermute x3, starting transfers between devices, on_device(): lax.ppermute(ext, 'dp', [(i, (i + s) % n_dp) for i in range(n_dp)])  7.01 us
  transfers between devices with their start and end apart: 11, of which 6 were waited for; matrix products, arithmetic and copies ran while one was open for 23% of the time, Pallas kernels for 0%

profile of v2, /device:TPU:0, one launch (start us, length us, event | category | flops | bytes accessed | tf_op | source)
XLA Modules:
  0.0 269.1 jit_solution(15057076781015515071)
XLA Ops:
  7.3 1.4 copy.102
  8.7 1.3 copy.103
  10.0 0.6 convert_subtract_fusion.3
  10.7 3.1 %collective-permute-start = (bf16[128,2176]{0,1:T(8,128)(2,1)S(1)}, bf16[128,2176]{0,1:T(8,128)(2,1)S(1)}, u32[]{:S(2)}, u32[]{:S(2)}) collective-permute-start(bf16[128,2176]{0,1:T(8,128)(2,1)S(1)} %pad_maximum_fusion.14), channel_id=1, source_target_pairs={{0,8},{8,16},{16,24},{24,0},{1,9},{9,17},{17,25},{25,1},{2,10},{10... | collective-permute-start | bytes 1671176 | tf_op jit(solution)/shard_map/ppermute | solution.py:25
  13.8 2.6 collective-permute-start.1
  16.4 1.3 collective-permute-start.2
  17.7 11.7 %collective-permute-done = bf16[128,2176]{0,1:T(8,128)(2,1)S(1)} collective-permute-done((bf16[128,2176]{0,1:T(8,128)(2,1)S(1)}, bf16[128,2176]{0,1:T(8,128)(2,1)S(1)}, u32[]{:S(2)}, u32[]{:S(2)}) %collective-permute-start) | collective-permute-done | bytes 557088 | tf_op jit(solution)/shard_map/ppermute | solution.py:25
  29.4 0.8 copy-done.24
  30.4 0.5 fusion.53
  31.1 0.7 slice_convert_fusion.2
  31.8 0.7 add_select_fusion.2
  32.5 1.1 select_reduce_fusion.5
  33.6 18.8 %collective-permute-done.1 = bf16[128,2176]{0,1:T(8,128)(2,1)S(1)} collective-permute-done((bf16[128,2176]{0,1:T(8,128)(2,1)S(1)}, bf16[128,2176]{0,1:T(8,128)(2,1)S(1)}, u32[]{:S(2)}, u32[]{:S(2)}) %collective-permute-start.1) | collective-permute-done | bytes 557088 | tf_op jit(solution)/shard_map/ppermute | solution.py:25
  52.7 0.5 fusion.52
  53.3 1.1 select_reduce_fusion.4
  55.6 0.5 fusion.51
  56.7 1.1 select_reduce_fusion.3
  57.9 1.5 convolution_convert_fusion.2
  60.7 0.5 pad_maximum_fusion.2
  61.3 46.9 %all_to_all.20 = bf16[3,4,72,2176]{3,2,0,1:T(8,128)(2,1)S(1)} all-to-all(bf16[3,4,72,2176]{3,2,0,1:T(8,128)(2,1)S(1)} %pad_maximum_fusion.2), channel_id=1, replica_groups=mesh['dp'=4,'expert'=4,'tensor'=2] {'expert'}, dimensions={1} | all-to-all | bytes 7520256 | tf_op jit(solution)/shard_map/all_to_all | solution.py:75
  108.2 2.1 copy.116
  110.4 0.6 copy-done.33
  111.2 0.5 fusion.54
  111.8 1.1 select_reduce_fusion.7
  114.6 30.7 %all_to_all.21 = bf16[1,4,72,4224]{3,2,0,1:T(8,128)(2,1)S(1)} all-to-all(bf16[1,4,72,4224]{3,2,0,1:T(8,128)(2,1)S(1)} %bitcast.111), channel_id=1, replica_groups=mesh['dp'=4,'expert'=4,'tensor'=2] {'expert'}, dimensions={1} | all-to-all | bytes 4866048 | tf_op jit(solution)/shard_map/all_to_all | solution.py:75
  145.4 0.8 fusion.27
  146.2 1.4 copy-done.6
  147.6 0.8 fusion.31
  148.4 1.6 multiply_convert_fusion.4
  150.3 0.5 fusion.68
  150.8 0.5 fusion.74
  151.3 0.5 convolution_add_fusion.2
  151.8 0.5 convolution_add_fusion.3
  152.4 1.7 pad_maximum_fusion.9
  154.2 1.1 convert_reduce_fusion
  155.3 4.1 %fusion.25 = f32[864,384]{1,0:T(8,128)S(1)} fusion(bf16[1,2048,384]{2,1,0:T(8,128)(2,1)S(1)} %copy-done.5, bf16[2,864,2176]{2,1,0:T(8,128)(2,1)} %all-gather.2.cloned.1.call-done), kind=kOutput, calls=%fused_computation.39 | convolution fusion | flops 1358954496 | bytes 6438912 | tf_op jit(solution)/shard_map/dot_general | solution.py:88
  159.9 2.0 fusion.29
  161.9 3.5 %multiply_convert_fusion.1 = (bf16[864,384]{1,0:T(8,128)(2,1)S(1)}, bf16[864,384]{1,0:T(8,128)(2,1)S(1)}, bf16[864,384]{1,0:T(8,128)(2,1)}, bf16[864,384]{1,0:T(8,128)(2,1)S(1)}, f32[864,384]{1,0:T(8,128)S(1)}) fusion(f32[864]{0:T(1024)S(1)} %convert_reduce_fusion, f32[864,384]{1,0:T(8,128)S(1)} %fusion.25, f32[864,384]{1,0:T(8,128)S(1)} %fusion.29, ...), kind=kOutput, calls=%fused_computation.56 | convolution fusion | flops 1365258240 | bytes 11751424 | tf_op jit(solution)/shard_map/dot_general | solution.py:93
  165.8 1.1 fusion.72
  166.9 1.1 fusion.66
  168.0 1.1 convolution_add_fusion.1
  169.2 1.1 convolution_add_fusion
  170.3 3.5 %pad_maximum_fusion = f32[864,2304]{1,0:T(8,128)} fusion(f32[864,128]{1,0:T(8,128)S(1)} %pad.49, f32[864,1024]{1,0:T(8,128)S(1)} %convolution_add_fusion, f32[864,1024]{1,0:T(8,128)S(1)} %convolution_add_fusion.1), kind=kLoop, calls=%fused_computation | loop fusion | flops 5971968 | bytes 15482880 | tf_op jit(solution)/shard_map/concatenate | solution.py:124
  173.9 2.4 convert_element_type.302
  176.3 3.7 %all-to-all-start.1 = ((bf16[1,4,72,1152]{3,2,0,1:T(8,128)(2,1)}), bf16[1,4,72,1152]{3,2,0,1:T(8,128)(2,1)S(1)}, u32[]{:S(2)}, u32[]{:S(2)}) async-start(bf16[1,4,72,1152]{3,2,0,1:T(8,128)(2,1)} %bitcast.122), calls=%async_computation.2 | async-start | bytes 1327104 | tf_op jit(solution)/shard_map/all_to_all | solution.py:126
  180.0 1.7 fusion.115
  181.7 6.1 %all-to-all-done.1 = bf16[1,4,72,1152]{3,2,0,1:T(8,128)(2,1)S(1)} async-done(((bf16[1,4,72,1152]{3,2,0,1:T(8,128)(2,1)}), bf16[1,4,72,1152]{3,2,0,1:T(8,128)(2,1)S(1)}, u32[]{:S(2)}, u32[]{:S(2)}) %all-to-all-start.1) | async-done | bytes 663584 | tf_op jit(solution)/shard_map/all_to_all | solution.py:126
  188.8 8.8 %reduce-scatter.5.cloned.1.call-done = f32[864,1152]{1,0:T(8,128)} async-done(((f32[864,2304]{1,0:T(8,128)}), f32[864,1152]{1,0:T(8,128)}) %reduce-scatter.5.cloned.1.call-update) | async-done | bytes 3981328 | tf_op jit(solution)/shard_map/reduce_scatter | solution.py:123
  197.7 2.3 convert_element_type.336
  200.0 1.5 copy.118
  201.4 4.0 %all-to-all-start.3 = ((bf16[3,4,72,1152]{3,2,0,1:T(8,128)(2,1)}), bf16[3,4,72,1152]{3,2,0,1:T(8,128)(2,1)S(1)}, u32[]{:S(2)}, u32[]{:S(2)}) async-start(bf16[3,4,72,1152]{3,2,0,1:T(8,128)(2,1)} %copy.118), calls=%async_computation.5 | async-start | bytes 3981312 | tf_op jit(solution)/shard_map/all_to_all | solution.py:126
  205.5 6.0 %slice_bitcast_fusion.1 = (bf16[864,2048]{1,0:T(8,128)(2,1)}, bf16[864,2048]{1,0:T(8,128)(2,1)S(1)}) fusion(bf16[2,864,2176]{2,1,0:T(8,128)(2,1)} %all-gather.2.cloned.1.call-done), kind=kLoop, calls=%fused_computation.15 | loop fusion | bytes 14155776 | tf_op jit(solution)/shard_map/squeeze | solution.py:85
  211.5 3.9 %fusion.19 = bf16[1,2048,384]{2,1,0:T(8,128)(2,1)} fusion(bf16[864,2048]{1,0:T(8,128)(2,1)S(1)} %get-tuple-element.45, bf16[288,2048]{1,0:T(8,128)(2,1)S(1)} %copy-done.15, bf16[864,384]{1,0:T(8,128)(2,1)S(1)} %copy-done.9, bf16[288,384]{1,0:T(8,128)(2,1)S(1)} %copy-done.19), kind=kOutput, calls=%fused_computation.28 | convolution fusion | flops 1823932416 | bytes 7176192 | tf_op jit(solution)/shard_map/dot_general | solution.py:154
  215.4 3.9 %fusion.20 = bf16[1,2048,384]{2,1,0:T(8,128)(2,1)} fusion(bf16[864,2048]{1,0:T(8,128)(2,1)S(1)} %get-tuple-element.45, bf16[288,2048]{1,0:T(8,128)(2,1)S(1)} %copy-done.15, bf16[864,384]{1,0:T(8,128)(2,1)S(1)} %copy-done.11, bf16[288,384]{1,0:T(8,128)(2,1)S(1)} %copy-done.17), kind=kOutput, calls=%fused_computation.29 | convolution fusion | flops 1823932416 | bytes 7176192 | tf_op jit(solution)/shard_map/dot_general | solution.py:150
  219.4 10.3 %all-to-all-done.3 = bf16[3,4,72,1152]{3,2,0,1:T(8,128)(2,1)S(1)} async-done(((bf16[3,4,72,1152]{3,2,0,1:T(8,128)(2,1)}), bf16[3,4,72,1152]{3,2,0,1:T(8,128)(2,1)S(1)}, u32[]{:S(2)}, u32[]{:S(2)}) %all-to-all-start.3) | async-done | bytes 1990688 | tf_op jit(solution)/shard_map/all_to_all | solution.py:126
  231.6 3.5 %collective-permute-start.3 = (bf16[128,1152]{1,0:T(8,128)(2,1)S(1)}, bf16[128,1152]{1,0:T(8,128)(2,1)}, u32[]{:S(2)}, u32[]{:S(2)}) collective-permute-start(bf16[128,1152]{1,0:T(8,128)(2,1)S(1)} %fusion.99), channel_id=1, source_target_pairs={{0,24},{8,0},{16,8},{24,16},{1,25},{9,1},{17,9},{25,17},{2,26},{10... | collective-permute-start | bytes 884744 | tf_op jit(solution)/shard_map/ppermute | solution.py:141
  235.1 1.1 select_reduce_fusion
  236.3 0.7 fusion.100
  237.2 1.2 collective-permute-start.5
  238.4 5.8 %fusion.16 = bf16[1,384,2048]{2,1,0:T(8,128)(2,1)} fusion(bf16[864,2048]{1,0:T(8,128)(2,1)} %get-tuple-element.44, bf16[288,2048]{1,0:T(8,128)(2,1)S(1)} %copy-done.14, bf16[864,384]{1,0:T(8,128)(2,1)} %get-tuple-element.48, bf16[288,384]{1,0:T(8,128)(2,1)} %get-tuple-element.54), kind=kOutput, calls=%fused_computation.27 | convolution fusion | flops 1823932416 | bytes 7176192 | tf_op jit(solution)/shard_map/dot_general | solution.py:158
  244.2 15.8 %collective-permute-done.4 = bf16[128,1152]{1,0:T(8,128)(2,1)} collective-permute-done((bf16[128,1152]{1,0:T(8,128)(2,1)}, bf16[128,1152]{1,0:T(8,128)(2,1)}, u32[]{:S(2)}, u32[]{:S(2)}) %collective-permute-start.4) | collective-permute-done | bytes 294944 | tf_op jit(solution)/shard_map/ppermute | solution.py:141
  260.0 1.2 add_convert_fusion
  261.2 0.7 slice.165
  262.0 0.7 copy.123
  (150 shorter events, 10.6 us)
Async XLA Ops:
  7.2 141.2 %copy-start = (bf16[1,384,2048]{2,1,0:T(8,128)(2,1)S(1)}, bf16[1,384,2048]{2,1,0:T(8,128)(2,1)}, u32[]{:S(2)}) copy-start(bf16[1,384,2048]{2,1,0:T(8,128)(2,1)} %param.13) | copy-start | bytes 4718596
  7.2 2.8 %copy-start.34 = (s32[128,8]{0,1:T(8,128)S(1)}, s32[128,8]{0,1:T(8,128)}, u32[]{:S(2)}) copy-start(s32[128,8]{0,1:T(8,128)} %param.9) | copy-start | bytes 12292
  7.2 3.4 %copy-start.32 = (bf16[128,8]{0,1:T(8,128)(2,1)S(1)}, bf16[128,8]{0,1:T(8,128)(2,1)}, u32[]{:S(2)}) copy-start(bf16[128,8]{0,1:T(8,128)(2,1)} %param.10) | copy-start | bytes 6148
  7.2 147.0 %all-gather.2.cloned.1.call-start = ((), (), s32[]{:S(2)}) async-start(), calls=%async_computation.7 | async-start | bytes 11280384 | tf_op jit(solution)/shard_map/all_gather | solution.py:83
  10.7 18.7 %collective-permute-start = (bf16[128,2176]{0,1:T(8,128)(2,1)S(1)}, bf16[128,2176]{0,1:T(8,128)(2,1)S(1)}, u32[]{:S(2)}, u32[]{:S(2)}) collective-permute-start(bf16[128,2176]{0,1:T(8,128)(2,1)S(1)} %pad_maximum_fusion.14), channel_id=1, source_target_pairs={{0,8},{8,16},{16,24},{24,0},{1,9},{9,17},{17,25},{25,1},{2,10},{10... | collective-permute-start | bytes 1671176 | tf_op jit(solution)/shard_map/ppermute | solution.py:25
  13.8 38.7 %collective-permute-start.1 = (bf16[128,2176]{0,1:T(8,128)(2,1)S(1)}, bf16[128,2176]{0,1:T(8,128)(2,1)S(1)}, u32[]{:S(2)}, u32[]{:S(2)}) collective-permute-start(bf16[128,2176]{0,1:T(8,128)(2,1)S(1)} %pad_maximum_fusion.14), channel_id=1, source_target_pairs={{0,16},{8,24},{16,0},{24,8},{1,17},{9,25},{17,1},{25,9},{2,18},{10... | collective-permute-start | bytes 1671176 | tf_op jit(solution)/shard_map/ppermute | solution.py:25
  16.4 39.0 %collective-permute-start.2 = (bf16[128,2176]{0,1:T(8,128)(2,1)S(1)}, bf16[128,2176]{0,1:T(8,128)(2,1)S(1)}, u32[]{:S(2)}, u32[]{:S(2)}) collective-permute-start(bf16[128,2176]{0,1:T(8,128)(2,1)S(1)} %pad_maximum_fusion.14), channel_id=1, source_target_pairs={{0,24},{8,0},{16,8},{24,16},{1,25},{9,1},{17,9},{25,17},{2,26},{10... | collective-permute-start | bytes 1671176 | tf_op jit(solution)/shard_map/ppermute | solution.py:25
  29.4 0.8 copy-start.24
  32.5 24.2 %copy-start.25 = (s32[128,8]{0,1:T(8,128)}, s32[128,8]{0,1:T(8,128)S(1)}, u32[]{:S(2)}) copy-start(s32[128,8]{0,1:T(8,128)S(1)} %add_select_fusion.2) | copy-start | bytes 12292
  53.3 6.1 %copy-start.27 = (s32[128,8]{0,1:T(8,128)}, s32[128,8]{0,1:T(8,128)S(1)}, u32[]{:S(2)}) copy-start(s32[128,8]{0,1:T(8,128)S(1)} %add_select_fusion.1) | copy-start | bytes 12292
  54.9 4.5 %copy-start.20 = (bf16[288,128]{1,0:T(8,128)(2,1)}, bf16[288,128]{1,0:T(8,128)(2,1)S(1)}, u32[]{:S(2)}) copy-start(bf16[288,128]{1,0:T(8,128)(2,1)S(1)} %fusion.85) | copy-start | bytes 221188
  56.3 3.3 %copy-start.29 = (s32[128,8]{0,1:T(8,128)}, s32[128,8]{0,1:T(8,128)S(1)}, u32[]{:S(2)}) copy-start(s32[128,8]{0,1:T(8,128)S(1)} %add_select_fusion) | copy-start | bytes 12292
  56.7 3.4 %copy-start.22 = (bf16[288,128]{1,0:T(8,128)(2,1)}, bf16[288,128]{1,0:T(8,128)(2,1)S(1)}, u32[]{:S(2)}) copy-start(bf16[288,128]{1,0:T(8,128)(2,1)S(1)} %fusion.87) | copy-start | bytes 221188
  110.3 0.7 copy-start.33
  110.3 0.7 copy-start.31
  110.3 3.2 %copy-start.12 = (bf16[128,2048]{1,0:T(8,128)(2,1)S(1)}, bf16[128,2048]{1,0:T(8,128)(2,1)}, u32[]{:S(2)}) copy-start(bf16[128,2048]{1,0:T(8,128)(2,1)} %param.8) | copy-start | bytes 1572868
  110.3 63.6 %reduce-scatter.3.cloned.1.call-start = ((), (), s32[]{:S(2)}) async-start(), calls=%async_computation.6 | async-start | bytes 3981312 | tf_op jit(solution)/shard_map/reduce_scatter | solution.py:123
  111.2 2.8 %copy-start.13 = (bf16[128,2048]{1,0:T(8,128)(2,1)S(1)}, bf16[128,2048]{1,0:T(8,128)(2,1)}, u32[]{:S(2)}) copy-start(bf16[128,2048]{1,0:T(8,128)(2,1)} %param.7) | copy-start | bytes 1572868
  114.6 30.8 %copy-start.5 = (bf16[1,2048,384]{2,1,0:T(8,128)(2,1)S(1)}, bf16[1,2048,384]{2,1,0:T(8,128)(2,1)}, u32[]{:S(2)}) copy-start(bf16[1,2048,384]{2,1,0:T(8,128)(2,1)} %param.11) | copy-start | bytes 4718596
  145.3 3.1 %copy-start.2 = (bf16[1,4,72,4224]{3,2,0,1:T(8,128)(2,1)}, bf16[1,4,72,4224]{3,2,0,1:T(8,128)(2,1)S(1)}, u32[]{:S(2)}) copy-start(bf16[1,4,72,4224]{3,2,0,1:T(8,128)(2,1)S(1)} %all_to_all.21) | copy-start | bytes 7299076
  145.4 2.2 copy-start.6
  150.0 0.8 copy-start.16
  150.0 1.8 copy-start.18
  154.1 43.5 %reduce-scatter.5.cloned.1.call-start = ((), (), s32[]{:S(2)}) async-start(), calls=%async_computation.8 | async-start | bytes 11943936 | tf_op jit(solution)/shard_map/reduce_scatter | solution.py:123
  155.3 4.2 %copy-start.4 = (bf16[2,864,2176]{2,1,0:T(8,128)(2,1)S(1)}, bf16[2,864,2176]{2,1,0:T(8,128)(2,1)}, u32[]{:S(2)}) copy-start(bf16[2,864,2176]{2,1,0:T(8,128)(2,1)} %all-gather.2.cloned.1.call-done) | copy-start | bytes 22560772
  155.3 4.6 %copy-start.7 = (bf16[1,2048,384]{2,1,0:T(8,128)(2,1)S(1)}, bf16[1,2048,384]{2,1,0:T(8,128)(2,1)}, u32[]{:S(2)}) copy-start(bf16[1,2048,384]{2,1,0:T(8,128)(2,1)} %param.12) | copy-start | bytes 4718596
  165.4 1.6 copy-start.10
  165.4 3.8 %copy-start.8 = (bf16[864,384]{1,0:T(8,128)(2,1)}, bf16[864,384]{1,0:T(8,128)(2,1)S(1)}, u32[]{:S(2)}) copy-start(bf16[864,384]{1,0:T(8,128)(2,1)S(1)} %get-tuple-element.46) | copy-start | bytes 1990660
  173.9 6.1 %copy-start.3 = (bf16[1,4,72,4224]{3,2,0,1:T(8,128)(2,1)S(1)}, bf16[1,4,72,4224]{3,2,0,1:T(8,128)(2,1)}, u32[]{:S(2)}) copy-start(bf16[1,4,72,4224]{3,2,0,1:T(8,128)(2,1)} %copy-done.2) | copy-start | bytes 7299076
  176.3 11.6 %all-to-all-start.1 = ((bf16[1,4,72,1152]{3,2,0,1:T(8,128)(2,1)}), bf16[1,4,72,1152]{3,2,0,1:T(8,128)(2,1)S(1)}, u32[]{:S(2)}, u32[]{:S(2)}) async-start(bf16[1,4,72,1152]{3,2,0,1:T(8,128)(2,1)} %bitcast.122), calls=%async_computation.2 | async-start | bytes 1327104 | tf_op jit(solution)/shard_map/all_to_all | solution.py:126
  201.4 28.2 %all-to-all-start.3 = ((bf16[3,4,72,1152]{3,2,0,1:T(8,128)(2,1)}), bf16[3,4,72,1152]{3,2,0,1:T(8,128)(2,1)S(1)}, u32[]{:S(2)}, u32[]{:S(2)}) async-start(bf16[3,4,72,1152]{3,2,0,1:T(8,128)(2,1)} %copy.118), calls=%async_computation.5 | async-start | bytes 3981312 | tf_op jit(solution)/shard_map/all_to_all | solution.py:126
  205.5 6.0 %copy-start.9 = (bf16[864,384]{1,0:T(8,128)(2,1)S(1)}, bf16[864,384]{1,0:T(8,128)(2,1)}, u32[]{:S(2)}) copy-start(bf16[864,384]{1,0:T(8,128)(2,1)} %copy-done.8) | copy-start | bytes 1990660
  205.5 6.0 %copy-start.15 = (bf16[288,2048]{1,0:T(8,128)(2,1)S(1)}, bf16[288,2048]{1,0:T(8,128)(2,1)}, u32[]{:S(2)}) copy-start(bf16[288,2048]{1,0:T(8,128)(2,1)} %get-tuple-element.51) | copy-start | bytes 3538948
  205.5 6.0 %copy-start.19 = (bf16[288,384]{1,0:T(8,128)(2,1)S(1)}, bf16[288,384]{1,0:T(8,128)(2,1)}, u32[]{:S(2)}) copy-start(bf16[288,384]{1,0:T(8,128)(2,1)} %copy-done.18) | copy-start | bytes 663556
  211.5 4.0 %copy-start.11 = (bf16[864,384]{1,0:T(8,128)(2,1)S(1)}, bf16[864,384]{1,0:T(8,128)(2,1)}, u32[]{:S(2)}) copy-start(bf16[864,384]{1,0:T(8,128)(2,1)} %copy-done.10) | copy-start | bytes 1990660
  211.5 4.0 %copy-start.17 = (bf16[288,384]{1,0:T(8,128)(2,1)S(1)}, bf16[288,384]{1,0:T(8,128)(2,1)}, u32[]{:S(2)}) copy-start(bf16[288,384]{1,0:T(8,128)(2,1)} %copy-done.16) | copy-start | bytes 663556
  219.4 10.5 %copy-start.21 = (bf16[288,128]{1,0:T(8,128)(2,1)S(1)}, bf16[288,128]{1,0:T(8,128)(2,1)}, u32[]{:S(2)}) copy-start(bf16[288,128]{1,0:T(8,128)(2,1)} %copy-done.20) | copy-start | bytes 221188
  229.8 0.9 copy-start.23
  229.8 1.2 copy-start.26
  230.1 5.0 %copy-start.28 = (s32[128,8]{0,1:T(8,128)S(1)}, s32[128,8]{0,1:T(8,128)}, u32[]{:S(2)}) copy-start(s32[128,8]{0,1:T(8,128)} %copy-done.27) | copy-start | bytes 12292
  230.1 5.0 %copy-start.30 = (s32[128,8]{0,1:T(8,128)S(1)}, s32[128,8]{0,1:T(8,128)}, u32[]{:S(2)}) copy-start(s32[128,8]{0,1:T(8,128)} %copy-done.29) | copy-start | bytes 12292
  230.7 7.7 %copy-start.14 = (bf16[288,2048]{1,0:T(8,128)(2,1)S(1)}, bf16[288,2048]{1,0:T(8,128)(2,1)}, u32[]{:S(2)}) copy-start(bf16[288,2048]{1,0:T(8,128)(2,1)} %get-tuple-element.50) | copy-start | bytes 3538948
  231.6 12.6 %collective-permute-start.3 = (bf16[128,1152]{1,0:T(8,128)(2,1)S(1)}, bf16[128,1152]{1,0:T(8,128)(2,1)}, u32[]{:S(2)}, u32[]{:S(2)}) collective-permute-start(bf16[128,1152]{1,0:T(8,128)(2,1)S(1)} %fusion.99), channel_id=1, source_target_pairs={{0,24},{8,0},{16,8},{24,16},{1,25},{9,1},{17,9},{25,17},{2,26},{10... | collective-permute-start | bytes 884744 | tf_op jit(solution)/shard_map/ppermute | solution.py:141
  237.0 23.0 %collective-permute-start.4 = (bf16[128,1152]{1,0:T(8,128)(2,1)}, bf16[128,1152]{1,0:T(8,128)(2,1)}, u32[]{:S(2)}, u32[]{:S(2)}) collective-permute-start(bf16[128,1152]{1,0:T(8,128)(2,1)} %fusion.100), channel_id=1, source_target_pairs={{0,16},{8,24},{16,0},{24,8},{1,17},{9,25},{17,1},{25,9},{2,18},{10... | collective-permute-start | bytes 884744 | tf_op jit(solution)/shard_map/ppermute | solution.py:141
  237.2 22.8 %collective-permute-start.5 = (bf16[128,1152]{1,0:T(8,128)(2,1)S(1)}, bf16[128,1152]{1,0:T(8,128)(2,1)S(1)}, u32[]{:S(2)}, u32[]{:S(2)}) collective-permute-start(bf16[128,1152]{1,0:T(8,128)(2,1)S(1)} %fusion.101), channel_id=1, source_target_pairs={{0,8},{8,16},{16,24},{24,0},{1,9},{9,17},{17,25},{25,1},{2,10},{10... | collective-permute-start | bytes 884744 | tf_op jit(solution)/shard_map/ppermute | solution.py:141
  238.4 24.2 %copy-start.1 = (bf16[1,384,2048]{2,1,0:T(8,128)(2,1)S(1)}, bf16[1,384,2048]{2,1,0:T(8,128)(2,1)}, u32[]{:S(2)}) copy-start(bf16[1,384,2048]{2,1,0:T(8,128)(2,1)} %param.13) | copy-start | bytes 4718596
Sparse Core Ops, SparseCore 0:
  110.4 27.0 all-gather.1
  154.2 17.3 reduce-scatter.2
  174.0 23.6 reduce-scatter.4

commit v3 on v1

--- a/solution.py
+++ b/solution.py
@@ -42,6 +42,8 @@
         sends, selects, matches = [], [], []
         for s in members:
             blk = blocks[s]
+            if gi:
+                blk = lax.optimization_barrier((blk, anchors[0]))[0]
             carried_b = blk[:, :features]
             ids_b = blk[:, features:features + top_count].astype(jnp.int32)
             gates_b = blk[:, features + top_count:features + 2 * top_count].astype(jnp.float32)

time: 263 us -> 284 us (1.080); the launches traced: 262 us -> 279 us
  blocking collectives: 0 us -> 65.4 us
  waiting for transfers between devices: 118 us -> 82.9 us
  starting transfers between devices: 28.9 us -> 17.6 us
    all_to_all x0 -> x2, blocking collectives: none -> 65.4 us  [on_device(): lax.all_to_all(send.reshape(n_mem, n_ex, capacity, features + lanes), 'ex...]
    all_to_all x2 -> x0, waiting for transfers between devices: 42.3 us -> none  [on_device(): lax.all_to_all(send.reshape(n_mem, n_ex, capacity, features + lanes), 'ex...]
    ppermute x3, waiting for transfers between devices: 23.2 us -> 34.6 us  [on_device(): lax.ppermute(ext, 'dp', [(i, (i + s) % n_dp) for i in range(n_dp)])]
    all_to_all x2 -> x0, starting transfers between devices: 8.47 us -> none  [on_device(): lax.all_to_all(send.reshape(n_mem, n_ex, capacity, features + lanes), 'ex...]
    ppermute x3, waiting for transfers between devices: 16 us -> 12.4 us  [on_device(): part = lax.ppermute(part, 'dp', [(i, (i - s) % n_dp) for i in range(n_dp)])]
    unnamed x53 -> x69, local copies, waits for them, and re-layouts: 5.84 us -> 5.32 us
  transfers between devices with their start and end apart: 14 -> 12, of which waited for: 8 -> 8; matrix products, arithmetic and copies ran while one was open for 33% -> 22% of each run, Pallas kernels for 0% -> 0%
where the time goes in v3:
time: 284 us; the launch traced here: 279 us
  waiting for transfers between devices  82.9 us (29%)
  blocking collectives  65.4 us (23%)
  matrix products  42.7 us (15%)
  other arithmetic  31 us (11%)
  local copies, waits for them, and re-layouts  24.6 us (9%)
  starting transfers between devices  17.6 us (6%)
  between operations  14.6 us (5%)
    all_to_all x2, blocking collectives, on_device(): lax.all_to_all(send.reshape(n_mem, n_ex, capacity, features + lanes), 'ex...  65.4 us
    ppermute x3, waiting for transfers between devices, on_device(): lax.ppermute(ext, 'dp', [(i, (i + s) % n_dp) for i in range(n_dp)])  34.6 us
    all_gather x2, waiting for transfers between devices, on_device(): both = lax.all_gather(recv, 'tensor')  18.5 us
    all_to_all x2, waiting for transfers between devices, on_device(): lax.all_to_all(ret.reshape(n_mem, n_ex, capacity, half + lanes), 'expert'...  16.5 us
    ppermute x3, waiting for transfers between devices, on_device(): part = lax.ppermute(part, 'dp', [(i, (i - s) % n_dp) for i in range(n_dp)])  12.4 us
    squeeze x2, local copies, waits for them, and re-layouts, on_device(): routed_dy = both[1, :, :features]  9.87 us
    all_to_all x2, starting transfers between devices, on_device(): lax.all_to_all(ret.reshape(n_mem, n_ex, capacity, half + lanes), 'expert'...  7.93 us
    dot_general x2, matrix products, on_device(): gate_pre = jnp.dot(routed_x, weight_g, preferred_element_type=jnp.float32)  6.31 us
  transfers between devices with their start and end apart: 12, of which 8 were waited for; matrix products, arithmetic and copies ran while one was open for 22% of the time, Pallas kernels for 0%

profile of v3, /device:TPU:0, one launch (start us, length us, event | category | flops | bytes accessed | tf_op | source)
XLA Modules:
  0.0 278.6 jit_solution(15724868959616891965)
XLA Ops:
  7.2 0.8 convert_element_type.299
  8.1 0.7 convert_subtract_fusion.3
  10.1 1.1 select_reduce_fusion.7
  11.5 1.3 copy.98
  12.9 0.8 copy-done.7
  14.3 21.6 %all_to_all.20 = bf16[1,4,72,2176]{3,2,0,1:T(8,128)(2,1)} all-to-all(bf16[1,4,72,2176]{3,2,0,1:T(8,128)(2,1)S(1)} %bitcast.122), channel_id=1, replica_groups=mesh['dp'=4,'expert'=4,'tensor'=2] {'expert'}, dimensions={1} | all-to-all | bytes 2506752 | tf_op jit(solution)/shard_map/all_to_all | solution.py:70
  36.0 2.0 pad_maximum_fusion.14
  37.9 3.6 %collective-permute-start.2 = (bf16[128,2176]{0,1:T(8,128)(2,1)}, bf16[128,2176]{0,1:T(8,128)(2,1)}, u32[]{:S(2)}, u32[]{:S(2)}) collective-permute-start(bf16[128,2176]{0,1:T(8,128)(2,1)} %pad_maximum_fusion.14), channel_id=1, source_target_pairs={{0,24},{8,0},{16,8},{24,16},{1,25},{9,1},{17,9},{25,17},{2,26},{10... | collective-permute-start | bytes 1671176 | tf_op jit(solution)/shard_map/ppermute | solution.py:25
  41.6 1.0 collective-permute-start
  42.6 4.2 %all-gather.3.cloned.1.call-done = bf16[2,288,2176]{2,1,0:T(8,128)(2,1)} async-done(((bf16[1,288,2176]{2,1,0:T(8,128)(2,1)}), bf16[2,288,2176]{2,1,0:T(8,128)(2,1)}) %all-gather.3.cloned.1.call-update) | async-done | bytes 2506768 | tf_op jit(solution)/shard_map/all_gather | solution.py:73
  46.8 2.2 fusion.26
  49.3 0.8 fusion.30
  50.3 1.8 multiply_convert_fusion.4
  52.1 25.1 %collective-permute-done = bf16[128,2176]{0,1:T(8,128)(2,1)} collective-permute-done((bf16[128,2176]{0,1:T(8,128)(2,1)}, bf16[128,2176]{0,1:T(8,128)(2,1)}, u32[]{:S(2)}, u32[]{:S(2)}) %collective-permute-start) | collective-permute-done | bytes 557088 | tf_op jit(solution)/shard_map/ppermute | solution.py:25
  77.9 0.7 convert_subtract_fusion.2
  78.6 9.5 %collective-permute-done.1 = bf16[128,2176]{0,1:T(8,128)(2,1)} collective-permute-done((bf16[128,2176]{0,1:T(8,128)(2,1)}, bf16[128,2176]{0,1:T(8,128)(2,1)}, u32[]{:S(2)}, u32[]{:S(2)}) %collective-permute-start.1) | collective-permute-done | bytes 557088 | tf_op jit(solution)/shard_map/ppermute | solution.py:25
  88.1 0.7 slice_convert_fusion.1
  88.7 0.7 convert_subtract_fusion.1
  89.4 0.7 slice_convert_fusion
  92.4 0.7 add_select_fusion
  93.6 1.1 select_reduce_fusion.4
  94.6 1.0 fusion.87
  95.7 1.1 select_reduce_fusion.3
  96.7 0.7 copy.104
  97.5 0.9 sub.65
  98.9 0.7 convert_element_type.314
  99.6 0.9 copy.105
  100.5 0.7 add_select_fusion.2
  101.7 1.1 select_reduce_fusion.5
  103.1 1.5 convolution_convert_fusion.1
  104.6 1.5 convolution_convert_fusion
  106.1 1.5 convolution_convert_fusion.2
  108.5 43.8 %all_to_all.21 = bf16[3,4,72,2176]{3,2,0,1:T(8,128)(2,1)S(1)} all-to-all(bf16[3,4,72,2176]{3,2,0,1:T(8,128)(2,1)S(1)} %pad_maximum_fusion.2), channel_id=1, replica_groups=mesh['dp'=4,'expert'=4,'tensor'=2] {'expert'}, dimensions={1} | all-to-all | bytes 7520256 | tf_op jit(solution)/shard_map/all_to_all | solution.py:70
  152.3 2.1 copy.116
  154.5 1.2 fusion.95
  156.9 0.9 copy-done.5
  158.8 1.7 pad_maximum_fusion.9
  160.8 14.2 %all-gather.5.cloned.1.call-done = bf16[2,864,2176]{2,1,0:T(8,128)(2,1)} async-done(((bf16[1,864,2176]{2,1,0:T(8,128)(2,1)}), bf16[2,864,2176]{2,1,0:T(8,128)(2,1)}) %all-gather.5.cloned.1.call-update) | async-done | bytes 7520272 | tf_op jit(solution)/shard_map/all_gather | solution.py:73
  175.0 1.1 convert_reduce_fusion
  176.1 4.1 %fusion.24 = f32[864,384]{1,0:T(8,128)S(1)} fusion(bf16[1,2048,384]{2,1,0:T(8,128)(2,1)S(1)} %copy-done.3, bf16[2,864,2176]{2,1,0:T(8,128)(2,1)} %all-gather.5.cloned.1.call-done), kind=kOutput, calls=%fused_computation.36 | convolution fusion | flops 1358954496 | bytes 6438912 | tf_op jit(solution)/shard_map/dot_general | solution.py:78
  180.7 2.0 fusion.28
  182.7 3.5 %multiply_convert_fusion.1 = (bf16[864,384]{1,0:T(8,128)(2,1)S(1)}, bf16[864,384]{1,0:T(8,128)(2,1)S(1)}, bf16[864,384]{1,0:T(8,128)(2,1)}, bf16[864,384]{1,0:T(8,128)(2,1)S(1)}, f32[864,384]{1,0:T(8,128)S(1)}) fusion(f32[864]{0:T(1024)S(1)} %convert_reduce_fusion, f32[864,384]{1,0:T(8,128)S(1)} %fusion.24, f32[864,384]{1,0:T(8,128)S(1)} %fusion.28, ...), kind=kOutput, calls=%fused_computation.53 | convolution fusion | flops 1365258240 | bytes 11751424 | tf_op jit(solution)/shard_map/dot_general | solution.py:83
  186.6 1.1 fusion.66
  187.7 1.1 fusion.72
  188.9 1.1 convolution_add_fusion
  190.0 1.1 convolution_add_fusion.1
  191.2 3.5 %pad_maximum_fusion = f32[864,2304]{1,0:T(8,128)} fusion(f32[864,128]{1,0:T(8,128)S(1)} %pad.49, f32[864,1024]{1,0:T(8,128)S(1)} %convolution_add_fusion, f32[864,1024]{1,0:T(8,128)S(1)} %convolution_add_fusion.1), kind=kLoop, calls=%fused_computation | loop fusion | flops 5971968 | bytes 15482880 | tf_op jit(solution)/shard_map/concatenate | solution.py:114
  194.7 2.2 convert_element_type.308
  196.9 3.9 %all-to-all-start.1 = ((bf16[1,4,72,1152]{3,2,0,1:T(8,128)(2,1)}), bf16[1,4,72,1152]{3,2,0,1:T(8,128)(2,1)S(1)}, u32[]{:S(2)}, u32[]{:S(2)}) async-start(bf16[1,4,72,1152]{3,2,0,1:T(8,128)(2,1)} %bitcast.13), calls=%async_computation.2 | async-start | bytes 1327104 | tf_op jit(solution)/shard_map/all_to_all | solution.py:116
  200.8 3.9 %slice_bitcast_fusion.3 = (bf16[288,2048]{1,0:T(8,128)(2,1)}, bf16[288,2048]{1,0:T(8,128)(2,1)}) fusion(bf16[2,288,2176]{2,1,0:T(8,128)(2,1)} %all-gather.3.cloned.1.call-done), kind=kLoop, calls=%fused_computation.66 | loop fusion | bytes 4718592 | tf_op jit(solution)/shard_map/squeeze | solution.py:75
  204.7 6.1 %all-to-all-done.1 = bf16[1,4,72,1152]{3,2,0,1:T(8,128)(2,1)S(1)} async-done(((bf16[1,4,72,1152]{3,2,0,1:T(8,128)(2,1)}), bf16[1,4,72,1152]{3,2,0,1:T(8,128)(2,1)S(1)}, u32[]{:S(2)}, u32[]{:S(2)}) %all-to-all-start.1) | async-done | bytes 663584 | tf_op jit(solution)/shard_map/all_to_all | solution.py:116
  211.7 0.8 reduce-scatter.5.cloned.1.call-done
  212.5 2.3 convert_element_type.342
  214.9 1.5 copy.118
  216.3 4.0 %all-to-all-start.3 = ((bf16[3,4,72,1152]{3,2,0,1:T(8,128)(2,1)}), bf16[3,4,72,1152]{3,2,0,1:T(8,128)(2,1)S(1)}, u32[]{:S(2)}, u32[]{:S(2)}) async-start(bf16[3,4,72,1152]{3,2,0,1:T(8,128)(2,1)} %copy.118), calls=%async_computation.5 | async-start | bytes 3981312 | tf_op jit(solution)/shard_map/all_to_all | solution.py:116
  220.3 6.0 %slice_bitcast_fusion.1 = (bf16[864,2048]{1,0:T(8,128)(2,1)}, bf16[864,2048]{1,0:T(8,128)(2,1)S(1)}) fusion(bf16[2,864,2176]{2,1,0:T(8,128)(2,1)} %all-gather.5.cloned.1.call-done), kind=kLoop, calls=%fused_computation.13 | loop fusion | bytes 14155776 | tf_op jit(solution)/shard_map/squeeze | solution.py:75
  226.3 3.9 %fusion.18 = bf16[1,2048,384]{2,1,0:T(8,128)(2,1)} fusion(bf16[864,2048]{1,0:T(8,128)(2,1)S(1)} %get-tuple-element.51, bf16[288,2048]{1,0:T(8,128)(2,1)S(1)} %copy-done.14, bf16[864,384]{1,0:T(8,128)(2,1)S(1)} %copy-done.9, bf16[288,384]{1,0:T(8,128)(2,1)S(1)} %copy-done.18), kind=kOutput, calls=%fused_computation.25 | convolution fusion | flops 1823932416 | bytes 7176192 | tf_op jit(solution)/shard_map/dot_general | solution.py:144
  230.3 3.9 %fusion.19 = bf16[1,2048,384]{2,1,0:T(8,128)(2,1)} fusion(bf16[864,2048]{1,0:T(8,128)(2,1)S(1)} %get-tuple-element.51, bf16[288,2048]{1,0:T(8,128)(2,1)S(1)} %copy-done.14, bf16[864,384]{1,0:T(8,128)(2,1)S(1)} %copy-done.11, bf16[288,384]{1,0:T(8,128)(2,1)S(1)} %copy-done.16), kind=kOutput, calls=%fused_computation.26 | convolution fusion | flops 1823932416 | bytes 7176192 | tf_op jit(solution)/shard_map/dot_general | solution.py:140
  234.2 10.4 %all-to-all-done.3 = bf16[3,4,72,1152]{3,2,0,1:T(8,128)(2,1)S(1)} async-done(((bf16[3,4,72,1152]{3,2,0,1:T(8,128)(2,1)}), bf16[3,4,72,1152]{3,2,0,1:T(8,128)(2,1)S(1)}, u32[]{:S(2)}, u32[]{:S(2)}) %all-to-all-start.3) | async-done | bytes 1990688 | tf_op jit(solution)/shard_map/all_to_all | solution.py:116
  247.6 2.5 collective-permute-start.4
  250.1 1.5 collective-permute-start.3
  252.3 5.8 %fusion.15 = bf16[1,384,2048]{2,1,0:T(8,128)(2,1)} fusion(bf16[864,2048]{1,0:T(8,128)(2,1)} %get-tuple-element.50, bf16[288,2048]{1,0:T(8,128)(2,1)S(1)} %copy-done.13, bf16[864,384]{1,0:T(8,128)(2,1)} %get-tuple-element.54, bf16[288,384]{1,0:T(8,128)(2,1)} %get-tuple-element.60), kind=kOutput, calls=%fused_computation.24 | convolution fusion | flops 1823932416 | bytes 7176192 | tf_op jit(solution)/shard_map/dot_general | solution.py:148
  258.0 12.4 %collective-permute-done.4 = bf16[128,1152]{1,0:T(8,128)(2,1)S(1)} collective-permute-done((bf16[128,1152]{1,0:T(8,128)(2,1)S(1)}, bf16[128,1152]{1,0:T(8,128)(2,1)S(1)}, u32[]{:S(2)}, u32[]{:S(2)}) %collective-permute-start.4) | collective-permute-done | bytes 294944 | tf_op jit(solution)/shard_map/ppermute | solution.py:131
  270.7 0.7 slice.156
  (144 shorter events, 16.9 us)
Async XLA Ops:
  7.2 43.1 %copy-start = (bf16[1,384,2048]{2,1,0:T(8,128)(2,1)S(1)}, bf16[1,384,2048]{2,1,0:T(8,128)(2,1)}, u32[]{:S(2)}) copy-start(bf16[1,384,2048]{2,1,0:T(8,128)(2,1)} %param.13) | copy-start | bytes 4718596
  7.2 4.1 %copy-start.23 = (bf16[128,2048]{1,0:T(8,128)(2,1)S(1)}, bf16[128,2048]{1,0:T(8,128)(2,1)}, u32[]{:S(2)}) copy-start(bf16[128,2048]{1,0:T(8,128)(2,1)} %param.7) | copy-start | bytes 1572868
  7.2 39.6 %all-gather.3.cloned.1.call-start = ((), (), s32[]{:S(2)}) async-start(), calls=%async_computation.6 | async-start | bytes 3760128 | tf_op jit(solution)/shard_map/all_gather | solution.py:73
  12.9 0.8 copy-start.7
  14.3 21.6 %copy-start.30 = (bf16[128,8]{0,1:T(8,128)(2,1)S(1)}, bf16[128,8]{0,1:T(8,128)(2,1)}, u32[]{:S(2)}) copy-start(bf16[128,8]{0,1:T(8,128)(2,1)} %param.10) | copy-start | bytes 6148
  35.9 10.9 %copy-start.3 = (bf16[1,2048,384]{2,1,0:T(8,128)(2,1)S(1)}, bf16[1,2048,384]{2,1,0:T(8,128)(2,1)}, u32[]{:S(2)}) copy-start(bf16[1,2048,384]{2,1,0:T(8,128)(2,1)} %param.11) | copy-start | bytes 4718596
  35.9 139.1 %all-gather.5.cloned.1.call-start = ((), (), s32[]{:S(2)}) async-start(), calls=%async_computation.8 | async-start | bytes 11280384 | tf_op jit(solution)/shard_map/all_gather | solution.py:73
  37.9 51.5 %collective-permute-start.2 = (bf16[128,2176]{0,1:T(8,128)(2,1)}, bf16[128,2176]{0,1:T(8,128)(2,1)}, u32[]{:S(2)}, u32[]{:S(2)}) collective-permute-start(bf16[128,2176]{0,1:T(8,128)(2,1)} %pad_maximum_fusion.14), channel_id=1, source_target_pairs={{0,24},{8,0},{16,8},{24,16},{1,25},{9,1},{17,9},{25,17},{2,26},{10... | collective-permute-start | bytes 1671176 | tf_op jit(solution)/shard_map/ppermute | solution.py:25
  41.6 46.5 %collective-permute-start.1 = (bf16[128,2176]{0,1:T(8,128)(2,1)}, bf16[128,2176]{0,1:T(8,128)(2,1)}, u32[]{:S(2)}, u32[]{:S(2)}) collective-permute-start(bf16[128,2176]{0,1:T(8,128)(2,1)} %pad_maximum_fusion.14), channel_id=1, source_target_pairs={{0,16},{8,24},{16,0},{24,8},{1,17},{9,25},{17,1},{25,9},{2,18},{10... | collective-permute-start | bytes 1671176 | tf_op jit(solution)/shard_map/ppermute | solution.py:25
  41.6 35.7 %collective-permute-start = (bf16[128,2176]{0,1:T(8,128)(2,1)}, bf16[128,2176]{0,1:T(8,128)(2,1)}, u32[]{:S(2)}, u32[]{:S(2)}) collective-permute-start(bf16[128,2176]{0,1:T(8,128)(2,1)} %pad_maximum_fusion.14), channel_id=1, source_target_pairs={{0,8},{8,16},{16,24},{24,0},{1,9},{9,17},{17,25},{25,1},{2,10},{10... | collective-permute-start | bytes 1671176 | tf_op jit(solution)/shard_map/ppermute | solution.py:25
  46.8 2.2 copy-start.4
  46.8 2.5 copy-start.12
  52.1 104.3 %copy-start.15 = (bf16[288,384]{1,0:T(8,128)(2,1)}, bf16[288,384]{1,0:T(8,128)(2,1)S(1)}, u32[]{:S(2)}) copy-start(bf16[288,384]{1,0:T(8,128)(2,1)S(1)} %get-tuple-element.59) | copy-start | bytes 663556
  93.1 6.5 %copy-start.26 = (s32[128,8]{0,1:T(8,128)}, s32[128,8]{0,1:T(8,128)S(1)}, u32[]{:S(2)}) copy-start(s32[128,8]{0,1:T(8,128)S(1)} %get-tuple-element.64) | copy-start | bytes 12292
  93.1 11.5 %copy-start.28 = (s32[128,8]{0,1:T(8,128)}, s32[128,8]{0,1:T(8,128)S(1)}, u32[]{:S(2)}) copy-start(s32[128,8]{0,1:T(8,128)S(1)} %get-tuple-element.65) | copy-start | bytes 12292
  100.5 4.1 %copy-start.19 = (bf16[288,128]{1,0:T(8,128)(2,1)S(1)}, bf16[288,128]{1,0:T(8,128)(2,1)}, u32[]{:S(2)}) copy-start(bf16[288,128]{1,0:T(8,128)(2,1)} %fusion.87) | copy-start | bytes 221188
  101.2 4.9 %copy-start.24 = (s32[128,8]{0,1:T(8,128)}, s32[128,8]{0,1:T(8,128)S(1)}, u32[]{:S(2)}) copy-start(s32[128,8]{0,1:T(8,128)S(1)} %add_select_fusion.2) | copy-start | bytes 12292
  101.7 4.5 %copy-start.21 = (bf16[288,128]{1,0:T(8,128)(2,1)}, bf16[288,128]{1,0:T(8,128)(2,1)S(1)}, u32[]{:S(2)}) copy-start(bf16[288,128]{1,0:T(8,128)(2,1)S(1)} %fusion.85) | copy-start | bytes 221188
  154.4 40.2 %reduce-scatter.3.cloned.1.call-start = ((), (), s32[]{:S(2)}) async-start(), calls=%async_computation.7 | async-start | bytes 3981312 | tf_op jit(solution)/shard_map/reduce_scatter | solution.py:113
  156.4 1.4 copy-start.5
  156.4 1.4 copy-start.17
  160.5 52.0 %reduce-scatter.5.cloned.1.call-start = ((), (), s32[]{:S(2)}) async-start(), calls=%async_computation.9 | async-start | bytes 11943936 | tf_op jit(solution)/shard_map/reduce_scatter | solution.py:113
  176.1 4.2 %copy-start.2 = (bf16[2,864,2176]{2,1,0:T(8,128)(2,1)S(1)}, bf16[2,864,2176]{2,1,0:T(8,128)(2,1)}, u32[]{:S(2)}) copy-start(bf16[2,864,2176]{2,1,0:T(8,128)(2,1)} %all-gather.5.cloned.1.call-done) | copy-start | bytes 22560772
  176.1 4.6 %copy-start.6 = (bf16[1,2048,384]{2,1,0:T(8,128)(2,1)S(1)}, bf16[1,2048,384]{2,1,0:T(8,128)(2,1)}, u32[]{:S(2)}) copy-start(bf16[1,2048,384]{2,1,0:T(8,128)(2,1)} %param.12) | copy-start | bytes 4718596
  186.2 1.6 copy-start.10
  186.2 3.8 %copy-start.8 = (bf16[864,384]{1,0:T(8,128)(2,1)}, bf16[864,384]{1,0:T(8,128)(2,1)S(1)}, u32[]{:S(2)}) copy-start(bf16[864,384]{1,0:T(8,128)(2,1)S(1)} %get-tuple-element.52) | copy-start | bytes 1990660
  196.9 13.9 %all-to-all-start.1 = ((bf16[1,4,72,1152]{3,2,0,1:T(8,128)(2,1)}), bf16[1,4,72,1152]{3,2,0,1:T(8,128)(2,1)S(1)}, u32[]{:S(2)}, u32[]{:S(2)}) async-start(bf16[1,4,72,1152]{3,2,0,1:T(8,128)(2,1)} %bitcast.13), calls=%async_computation.2 | async-start | bytes 1327104 | tf_op jit(solution)/shard_map/all_to_all | solution.py:116
  216.3 28.3 %all-to-all-start.3 = ((bf16[3,4,72,1152]{3,2,0,1:T(8,128)(2,1)}), bf16[3,4,72,1152]{3,2,0,1:T(8,128)(2,1)S(1)}, u32[]{:S(2)}, u32[]{:S(2)}) async-start(bf16[3,4,72,1152]{3,2,0,1:T(8,128)(2,1)} %copy.118), calls=%async_computation.5 | async-start | bytes 3981312 | tf_op jit(solution)/shard_map/all_to_all | solution.py:116
  220.3 6.0 %copy-start.9 = (bf16[864,384]{1,0:T(8,128)(2,1)S(1)}, bf16[864,384]{1,0:T(8,128)(2,1)}, u32[]{:S(2)}) copy-start(bf16[864,384]{1,0:T(8,128)(2,1)} %copy-done.8) | copy-start | bytes 1990660
  220.3 6.0 %copy-start.14 = (bf16[288,2048]{1,0:T(8,128)(2,1)S(1)}, bf16[288,2048]{1,0:T(8,128)(2,1)}, u32[]{:S(2)}) copy-start(bf16[288,2048]{1,0:T(8,128)(2,1)} %get-tuple-element.57) | copy-start | bytes 3538948
  220.3 6.0 %copy-start.18 = (bf16[288,384]{1,0:T(8,128)(2,1)S(1)}, bf16[288,384]{1,0:T(8,128)(2,1)}, u32[]{:S(2)}) copy-start(bf16[288,384]{1,0:T(8,128)(2,1)} %get-tuple-element.58) | copy-start | bytes 663556
  226.3 4.0 %copy-start.11 = (bf16[864,384]{1,0:T(8,128)(2,1)S(1)}, bf16[864,384]{1,0:T(8,128)(2,1)}, u32[]{:S(2)}) copy-start(bf16[864,384]{1,0:T(8,128)(2,1)} %copy-done.10) | copy-start | bytes 1990660
  226.3 3.9 %copy-start.16 = (bf16[288,384]{1,0:T(8,128)(2,1)S(1)}, bf16[288,384]{1,0:T(8,128)(2,1)}, u32[]{:S(2)}) copy-start(bf16[288,384]{1,0:T(8,128)(2,1)} %copy-done.15) | copy-start | bytes 663556
  234.2 10.8 %copy-start.20 = (bf16[288,128]{1,0:T(8,128)(2,1)S(1)}, bf16[288,128]{1,0:T(8,128)(2,1)}, u32[]{:S(2)}) copy-start(bf16[288,128]{1,0:T(8,128)(2,1)} %fusion.87) | copy-start | bytes 221188
  244.8 0.9 copy-start.22
  244.8 1.2 copy-start.29
  244.8 1.6 copy-start.25
  244.8 2.0 copy-start.27
  245.7 6.6 %copy-start.13 = (bf16[288,2048]{1,0:T(8,128)(2,1)S(1)}, bf16[288,2048]{1,0:T(8,128)(2,1)}, u32[]{:S(2)}) copy-start(bf16[288,2048]{1,0:T(8,128)(2,1)} %get-tuple-element.56) | copy-start | bytes 3538948
  247.6 22.9 %collective-permute-start.4 = (bf16[128,1152]{1,0:T(8,128)(2,1)S(1)}, bf16[128,1152]{1,0:T(8,128)(2,1)S(1)}, u32[]{:S(2)}, u32[]{:S(2)}) collective-permute-start(bf16[128,1152]{1,0:T(8,128)(2,1)S(1)} %fusion.100), channel_id=1, source_target_pairs={{0,16},{8,24},{16,0},{24,8},{1,17},{9,25},{17,1},{25,9},{2,18},{10... | collective-permute-start | bytes 884744 | tf_op jit(solution)/shard_map/ppermute | solution.py:131
  250.1 20.4 %collective-permute-start.3 = (bf16[128,1152]{1,0:T(8,128)(2,1)S(1)}, bf16[128,1152]{1,0:T(8,128)(2,1)S(1)}, u32[]{:S(2)}, u32[]{:S(2)}) collective-permute-start(bf16[128,1152]{1,0:T(8,128)(2,1)S(1)} %fusion.99), channel_id=1, source_target_pairs={{0,24},{8,0},{16,8},{24,16},{1,25},{9,1},{17,9},{25,17},{2,26},{10... | collective-permute-start | bytes 884744 | tf_op jit(solution)/shard_map/ppermute | solution.py:131
  251.6 18.9 %collective-permute-start.5 = (bf16[128,1152]{1,0:T(8,128)(2,1)S(1)}, bf16[128,1152]{1,0:T(8,128)(2,1)S(1)}, u32[]{:S(2)}, u32[]{:S(2)}) collective-permute-start(bf16[128,1152]{1,0:T(8,128)(2,1)S(1)} %fusion.101), channel_id=1, source_target_pairs={{0,8},{8,16},{16,24},{24,0},{1,9},{9,17},{17,25},{25,1},{2,10},{10... | collective-permute-start | bytes 884744 | tf_op jit(solution)/shard_map/ppermute | solution.py:131
  252.3 19.8 %copy-start.1 = (bf16[1,384,2048]{2,1,0:T(8,128)(2,1)S(1)}, bf16[1,384,2048]{2,1,0:T(8,128)(2,1)}, u32[]{:S(2)}) copy-start(bf16[1,384,2048]{2,1,0:T(8,128)(2,1)} %param.13) | copy-start | bytes 4718596
Sparse Core Ops, SparseCore 0:
  36.0 10.7 all-gather.2
  154.6 20.4 all-gather.4
  177.3 11.3 reduce-scatter.2
  194.8 17.7 reduce-scatter.4

commit v4 on v1

--- a/solution.py
+++ b/solution.py
@@ -39,29 +39,28 @@
     anchors = []
     groups_of = [[0]] + ([list(range(1, n_dp))] if n_dp > 1 else [])
     for gi, members in enumerate(groups_of):
-        sends, selects, matches = [], [], []
-        for s in members:
-            blk = blocks[s]
-            carried_b = blk[:, :features]
-            ids_b = blk[:, features:features + top_count].astype(jnp.int32)
-            gates_b = blk[:, features + top_count:features + 2 * top_count].astype(jnp.float32)
+        n_mem = len(members)
+        stacked = jnp.stack([blocks[s] for s in members])
+        carried_m = stacked[:, :, :features]
+        ids_m = stacked[:, :, features:features + top_count].astype(jnp.int32)
+        gates_m = stacked[:, :, features + top_count:features + 2 * top_count].astype(jnp.float32)
 
-            local_ex = ids_b.reshape(routes) - plane * n_ex
-            in_plane = (local_ex >= 0) & (local_ex < n_ex)
-            one_hot = local_ex[:, None] == e_iota[None, :]
-            running = jnp.dot(earlier, one_hot.astype(jnp.bfloat16), preferred_element_type=jnp.float32)
-            position = jnp.sum(running * one_hot.astype(jnp.float32), axis=1).astype(jnp.int32)
-            key = jnp.where(in_plane, local_ex * capacity + position, -1).reshape(tok_rows, top_count)
-            match = key[None, :, :] == q_iota[:, None, None]
-            select = jnp.sum(match.astype(jnp.bfloat16), axis=2)
-            send_rows = jnp.dot(select, carried_b, preferred_element_type=jnp.float32).astype(tokens.dtype)
-            send_gate = jnp.sum(jnp.where(match, gates_b[None, :, :], 0.0), axis=(1, 2))
-            gate_cols = jnp.pad(send_gate.astype(tokens.dtype)[:, None], ((0, 0), (0, lanes - 1)))
-            sends.append(jnp.concatenate([send_rows, gate_cols], axis=1))
-            selects.append(select)
-            matches.append(match)
-        send = jnp.stack(sends)
-        n_mem = len(members)
+        local_ex = ids_m.reshape(n_mem, routes) - plane * n_ex
+        in_plane = (local_ex >= 0) & (local_ex < n_ex)
+        one_hot = local_ex[:, :, None] == e_iota[None, None, :]
+        running = jnp.einsum(
+            "ab,mbe->mae", earlier, one_hot.astype(jnp.bfloat16), preferred_element_type=jnp.float32
+        )
+        position = jnp.sum(running * one_hot.astype(jnp.float32), axis=2).astype(jnp.int32)
+        key = jnp.where(in_plane, local_ex * capacity + position, -1).reshape(n_mem, tok_rows, top_count)
+        match = key[:, None, :, :] == q_iota[None, :, None, None]
+        select = jnp.sum(match.astype(jnp.bfloat16), axis=3)
+        send_rows = jnp.einsum(
+            "mqt,mtf->mqf", select, carried_m, preferred_element_type=jnp.float32
+        ).astype(tokens.dtype)
+        send_gate = jnp.sum(jnp.where(match, gates_m[:, None, :, :], 0.0), axis=(2, 3))
+        gate_cols = jnp.pad(send_gate.astype(tokens.dtype)[:, :, None], ((0, 0), (0, 0), (0, lanes - 1)))
+        send = jnp.concatenate([send_rows, gate_cols], axis=2)
 
         if gi >= 2:
             send = lax.optimization_barrier((send, anchors[gi - 2]))[0]
@@ -115,16 +114,17 @@
             ret.reshape(n_mem, n_ex, capacity, half + lanes), "expert", split_axis=1, concat_axis=1, tiled=True
         ).reshape(n_mem, block_slots, half + lanes)
 
+        col_grad = jnp.einsum(
+            "mqt,mqf->mtf", select, back[:, :, :half], preferred_element_type=jnp.float32
+        )
+        col_gate = jnp.sum(
+            jnp.where(match, back[:, :, half].astype(jnp.float32)[:, :, None, None], 0.0), axis=1
+        )
+        parts = jnp.concatenate(
+            [col_grad, jnp.pad(col_gate, ((0, 0), (0, 0), (0, lanes - top_count)))], axis=2
+        ).astype(jnp.bfloat16)
         for m, s in enumerate(members):
-            col_grad = lax.dot_general(
-                selects[m], back[m, :, :half], (((0,), (0,)), ((), ())), preferred_element_type=jnp.float32
-            )
-            col_gate = jnp.sum(
-                jnp.where(matches[m], back[m, :, half].astype(jnp.float32)[:, None, None], 0.0), axis=0
-            )
-            part = jnp.concatenate(
-                [col_grad, jnp.pad(col_gate, ((0, 0), (0, lanes - top_count)))], axis=1
-            ).astype(jnp.bfloat16)
+            part = parts[m]
             if s:
                 part = lax.ppermute(part, "dp", [(i, (i - s) % n_dp) for i in range(n_dp)])
             col_parts.append(part.astype(jnp.float32))

time: 263 us -> 259 us (0.985)
  other arithmetic: 33 us -> 27.2 us
  waiting for transfers between devices: 118 us -> 121 us
    ppermute x3, waiting for transfers between devices: 16 us -> 19.1 us  [on_device(): part = lax.ppermute(part, 'dp', [(i, (i - s) % n_dp) for i in range(n_dp)])]
    all_gather x2, waiting for transfers between devices: 17.4 us -> 20.2 us  [on_device(): both = lax.all_gather(recv, 'tensor')]
    reduce_sum x11 -> x6, other arithmetic: 7.77 us -> 6.15 us  [the longest x2 2.71 us: on_device(): jnp.sum(jnp.where(match, gates_m[:, None, :, :], 0.0), axis=(2, 3))]
    unnamed x53 -> x42, local copies, waits for them, and re-layouts: 5.84 us -> 4.33 us
    dot_general x12 -> x6, matrix products: 8.23 us -> 7.22 us  [the longest x2 4.09 us: on_device(): jnp.einsum('mqt,mtf->mqf', select, carried_m, preferred_element_type=jnp....]
  transfers between devices with their start and end apart: 14 -> 14, of which waited for: 8 -> 10; matrix products, arithmetic and copies ran while one was open for 33% -> 29% of each run, Pallas kernels for 0% -> 0%
where the time goes in v4:
time: 259 us
  waiting for transfers between devices  121 us (47%)
  matrix products  40.4 us (16%)
  starting transfers between devices  30.3 us (12%)
  other arithmetic  27.2 us (11%)
  local copies, waits for them, and re-layouts  25.5 us (10%)
  between operations  14.3 us (6%)
    all_to_all x2, waiting for transfers between devices, on_device(): lax.all_to_all(send.reshape(n_mem, n_ex, capacity, features + lanes), 'ex...  40.2 us
    ppermute x3, waiting for transfers between devices, on_device(): lax.ppermute(ext, 'dp', [(i, (i + s) % n_dp) for i in range(n_dp)])  22.7 us
    all_gather x2, waiting for transfers between devices, on_device(): both = lax.all_gather(recv, 'tensor')  20.2 us
    ppermute x3, waiting for transfers between devices, on_device(): part = lax.ppermute(part, 'dp', [(i, (i - s) % n_dp) for i in range(n_dp)])  19.1 us
    all_to_all x2, waiting for transfers between devices, on_device(): lax.all_to_all(ret.reshape(n_mem, n_ex, capacity, half + lanes), 'expert'...  17.2 us
    squeeze x2, local copies, waits for them, and re-layouts, on_device(): routed_dy = both[1, :, :features]  9.41 us
    all_to_all x2, starting transfers between devices, on_device(): lax.all_to_all(send.reshape(n_mem, n_ex, capacity, features + lanes), 'ex...  9.06 us
    all_to_all x2, starting transfers between devices, on_device(): lax.all_to_all(ret.reshape(n_mem, n_ex, capacity, half + lanes), 'expert'...  8.34 us
  transfers between devices with their start and end apart: 14, of which 10 were waited for; matrix products, arithmetic and copies ran while one was open for 29% of the time, Pallas kernels for 0%

profile of v4, /device:TPU:0, one launch (start us, length us, event | category | flops | bytes accessed | tf_op | source)
XLA Modules:
  0.0 258.6 jit_solution(11480117046381044526)
XLA Ops:
  7.2 0.8 convert_element_type.213
  8.0 1.3 copy.64
  9.3 1.3 copy.65
  10.7 1.1 fusion.105
  11.8 4.0 %collective-permute-start.1 = (bf16[128,2176]{0,1:T(8,128)(2,1)}, bf16[128,2176]{0,1:T(8,128)(2,1)S(1)}, u32[]{:S(2)}, u32[]{:S(2)}) collective-permute-start(bf16[128,2176]{0,1:T(8,128)(2,1)} %get-tuple-element.55), channel_id=1, source_target_pairs={{0,16},{8,24},{16,0},{24,8},{1,17},{9,25},{17,1},{25,9},{2,18},{10... | collective-permute-start | bytes 1671176 | tf_op jit(solution)/shard_map/ppermute | solution.py:25
  15.8 1.6 collective-permute-start
  17.4 2.2 collective-permute-start.2
  19.7 0.7 fusion.101
  20.3 0.7 convert_subtract_fusion.1
  21.2 0.8 fusion.58
  22.2 0.7 fusion.100
  23.3 1.1 select_reduce_fusion.3
  24.5 1.5 convolution_convert_fusion.1
  26.0 1.2 pad_maximum_fusion.14
  27.2 4.3 %all-to-all-start = ((bf16[1,4,72,2176]{3,2,0,1:T(8,128)(2,1)}), bf16[1,4,72,2176]{3,2,0,1:T(8,128)(2,1)}, u32[]{:S(2)}, u32[]{:S(2)}) async-start(bf16[1,4,72,2176]{3,2,0,1:T(8,128)(2,1)} %pad_maximum_fusion.14), calls=%async_computation | async-start | bytes 2506752 | tf_op jit(solution)/shard_map/all_to_all | solution.py:67
  31.5 22.0 %collective-permute-done.1 = bf16[128,2176]{0,1:T(8,128)(2,1)S(1)} collective-permute-done((bf16[128,2176]{0,1:T(8,128)(2,1)}, bf16[128,2176]{0,1:T(8,128)(2,1)S(1)}, u32[]{:S(2)}, u32[]{:S(2)}) %collective-permute-start.1) | collective-permute-done | bytes 557088 | tf_op jit(solution)/shard_map/ppermute | solution.py:25
  53.4 0.7 collective-permute-done.2
  54.2 1.4 pad_maximum_fusion.13
  56.6 1.7 select_reduce_fusion.1
  58.5 1.6 fusion.23
  60.1 2.6 convolution_convert_fusion
  63.0 2.1 copy.78
  65.1 4.8 %all-to-all-start.2 = ((bf16[3,4,72,2176]{3,2,0,1:T(8,128)(2,1)}), bf16[3,4,72,2176]{3,2,0,1:T(8,128)(2,1)}, u32[]{:S(2)}, u32[]{:S(2)}) async-start(bf16[3,4,72,2176]{3,2,0,1:T(8,128)(2,1)} %copy.78), calls=%async_computation.3 | async-start | bytes 7520256 | tf_op jit(solution)/shard_map/all_to_all | solution.py:67
  69.9 0.7 all-gather.3.cloned.1.call-update
  70.7 40.2 %all-to-all-done.2 = bf16[3,4,72,2176]{3,2,0,1:T(8,128)(2,1)} async-done(((bf16[3,4,72,2176]{3,2,0,1:T(8,128)(2,1)}), bf16[3,4,72,2176]{3,2,0,1:T(8,128)(2,1)}, u32[]{:S(2)}, u32[]{:S(2)}) %all-to-all-start.2) | async-done | bytes 3760160 | tf_op jit(solution)/shard_map/all_to_all | solution.py:67
  110.8 4.2 %copy.79 = bf16[3,4,72,2176]{3,2,1,0:T(8,128)(2,1)} copy(bf16[3,4,72,2176]{3,2,0,1:T(8,128)(2,1)} %all-to-all-done.2) | data formatting | bytes 7520256 | tf_op jit(solution)/shard_map/all_to_all | solution.py:67
  115.3 1.1 convert_reduce_fusion.3
  116.4 2.2 fusion.30
  119.0 0.8 fusion.34
  119.8 1.6 multiply_convert_fusion.4
  123.7 1.7 pad_maximum_fusion.8
  125.5 20.1 %all-gather.5.cloned.1.call-done = bf16[2,864,2176]{2,1,0:T(8,128)(2,1)} async-done(((bf16[1,864,2176]{2,1,0:T(8,128)(2,1)}), bf16[2,864,2176]{2,1,0:T(8,128)(2,1)}) %all-gather.5.cloned.1.call-update) | async-done | bytes 7520272 | tf_op jit(solution)/shard_map/all_gather | solution.py:70
  145.7 1.1 convert_reduce_fusion.1
  146.8 4.1 %fusion.28 = f32[864,384]{1,0:T(8,128)S(1)} fusion(bf16[1,2048,384]{2,1,0:T(8,128)(2,1)S(1)} %copy-done.3, bf16[2,864,2176]{2,1,0:T(8,128)(2,1)} %all-gather.5.cloned.1.call-done), kind=kOutput, calls=%fused_computation.41 | convolution fusion | flops 1358954496 | bytes 6438912 | tf_op jit(solution)/shard_map/dot_general | solution.py:75
  151.4 2.0 fusion.32
  153.4 3.5 %multiply_convert_fusion.1 = (bf16[864,384]{1,0:T(8,128)(2,1)S(1)}, bf16[864,384]{1,0:T(8,128)(2,1)S(1)}, bf16[864,384]{1,0:T(8,128)(2,1)}, bf16[864,384]{1,0:T(8,128)(2,1)S(1)}, f32[864,384]{1,0:T(8,128)S(1)}) fusion(f32[864]{0:T(1024)S(1)} %convert_reduce_fusion.1, f32[864,384]{1,0:T(8,128)S(1)} %fusion.28, f32[864,384]{1,0:T(8,128)S(1)} %fusion.32, ...), kind=kOutput, calls=%fused_computation.59 | convolution fusion | flops 1365258240 | bytes 11751424 | tf_op jit(solution)/shard_map/dot_general | solution.py:80
  157.3 1.1 fusion.71
  158.4 1.1 fusion.77
  159.5 1.1 convolution_add_fusion
  160.7 1.1 convolution_add_fusion.1
  161.8 3.4 %pad_maximum_fusion = f32[864,2304]{1,0:T(8,128)} fusion(f32[864,128]{1,0:T(8,128)S(1)} %pad.35, f32[864,1024]{1,0:T(8,128)S(1)} %convolution_add_fusion, f32[864,1024]{1,0:T(8,128)S(1)} %convolution_add_fusion.1), kind=kLoop, calls=%fused_computation | loop fusion | flops 5971968 | bytes 15482880 | tf_op jit(solution)/shard_map/concatenate | solution.py:111
  165.3 2.2 convert_element_type.227
  167.5 3.9 %all-to-all-start.1 = ((bf16[1,4,72,1152]{3,2,0,1:T(8,128)(2,1)}), bf16[1,4,72,1152]{3,2,0,1:T(8,128)(2,1)S(1)}, u32[]{:S(2)}, u32[]{:S(2)}) async-start(bf16[1,4,72,1152]{3,2,0,1:T(8,128)(2,1)} %bitcast.22), calls=%async_computation.2 | async-start | bytes 1327104 | tf_op jit(solution)/shard_map/all_to_all | solution.py:113
  171.4 3.5 %slice_bitcast_fusion.3 = (bf16[288,2048]{1,0:T(8,128)(2,1)S(1)}, bf16[288,2048]{1,0:T(8,128)(2,1)}) fusion(bf16[2,288,2176]{2,1,0:T(8,128)(2,1)} %all-gather.3.cloned.1.call-done), kind=kLoop, calls=%fused_computation.66 | loop fusion | bytes 4718592 | tf_op jit(solution)/shard_map/squeeze | solution.py:72
  174.9 6.5 %all-to-all-done.1 = bf16[1,4,72,1152]{3,2,0,1:T(8,128)(2,1)S(1)} async-done(((bf16[1,4,72,1152]{3,2,0,1:T(8,128)(2,1)}), bf16[1,4,72,1152]{3,2,0,1:T(8,128)(2,1)S(1)}, u32[]{:S(2)}, u32[]{:S(2)}) %all-to-all-start.1) | async-done | bytes 663584 | tf_op jit(solution)/shard_map/all_to_all | solution.py:113
  182.4 0.7 reduce-scatter.5.cloned.1.call-done
  183.2 2.3 convert_element_type.245
  185.5 1.5 copy.81
  186.9 4.4 %all-to-all-start.3 = ((bf16[3,4,72,1152]{3,2,0,1:T(8,128)(2,1)}), bf16[3,4,72,1152]{3,2,0,1:T(8,128)(2,1)}, u32[]{:S(2)}, u32[]{:S(2)}) async-start(bf16[3,4,72,1152]{3,2,0,1:T(8,128)(2,1)} %copy.81), calls=%async_computation.5 | async-start | bytes 3981312 | tf_op jit(solution)/shard_map/all_to_all | solution.py:113
  191.4 5.9 %slice_bitcast_fusion.1 = (bf16[864,2048]{1,0:T(8,128)(2,1)}, bf16[864,2048]{1,0:T(8,128)(2,1)S(1)}) fusion(bf16[2,864,2176]{2,1,0:T(8,128)(2,1)} %all-gather.5.cloned.1.call-done), kind=kLoop, calls=%fused_computation.14 | loop fusion | bytes 14155776 | tf_op jit(solution)/shard_map/squeeze | solution.py:72
  197.4 4.0 %fusion.21 = bf16[1,2048,384]{2,1,0:T(8,128)(2,1)} fusion(bf16[864,2048]{1,0:T(8,128)(2,1)S(1)} %get-tuple-element.40, bf16[288,2048]{1,0:T(8,128)(2,1)S(1)} %copy-done.12, bf16[864,384]{1,0:T(8,128)(2,1)S(1)} %copy-done.8, bf16[288,384]{1,0:T(8,128)(2,1)S(1)} %copy-done.14), kind=kOutput, calls=%fused_computation.28 | convolution fusion | flops 1823932416 | bytes 7176192 | tf_op jit(solution)/shard_map/dot_general | solution.py:142
  201.3 3.9 %fusion.22 = bf16[1,2048,384]{2,1,0:T(8,128)(2,1)} fusion(bf16[864,2048]{1,0:T(8,128)(2,1)S(1)} %get-tuple-element.40, bf16[288,2048]{1,0:T(8,128)(2,1)S(1)} %copy-done.12, bf16[864,384]{1,0:T(8,128)(2,1)S(1)} %copy-done.10, bf16[288,384]{1,0:T(8,128)(2,1)S(1)} %get-tuple-element.48), kind=kOutput, calls=%fused_computation.29 | convolution fusion | flops 1823932416 | bytes 7176192 | tf_op jit(solution)/shard_map/dot_general | solution.py:138
  205.3 10.7 %all-to-all-done.3 = bf16[3,4,72,1152]{3,2,0,1:T(8,128)(2,1)} async-done(((bf16[3,4,72,1152]{3,2,0,1:T(8,128)(2,1)}), bf16[3,4,72,1152]{3,2,0,1:T(8,128)(2,1)}, u32[]{:S(2)}, u32[]{:S(2)}) %all-to-all-start.3) | async-done | bytes 1990688 | tf_op jit(solution)/shard_map/all_to_all | solution.py:113
  215.9 1.7 copy.82
  217.9 1.5 fusion.40
  219.4 1.1 select_reduce_fusion
  220.6 1.4 fusion.59
  222.0 3.6 %collective-permute-start.3 = (bf16[128,1152]{1,0:T(8,128)(2,1)S(1)}, bf16[128,1152]{1,0:T(8,128)(2,1)S(1)}, u32[]{:S(2)}, u32[]{:S(2)}) collective-permute-start(bf16[128,1152]{1,0:T(8,128)(2,1)S(1)} %get-tuple-element.51), channel_id=1, source_target_pairs={{0,24},{8,0},{16,8},{24,16},{1,25},{9,1},{17,9},{25,17},{2,26},{10... | collective-permute-start | bytes 884744 | tf_op jit(solution)/shard_map/ppermute | solution.py:129
  225.7 1.1 collective-permute-start.4
  226.8 4.6 %fusion.18 = bf16[1,384,2048]{2,1,0:T(8,128)(2,1)} fusion(bf16[864,2048]{1,0:T(8,128)(2,1)S(1)} %copy-done.6, bf16[288,2048]{1,0:T(8,128)(2,1)S(1)} %get-tuple-element.45, bf16[864,384]{1,0:T(8,128)(2,1)} %get-tuple-element.43, bf16[288,384]{1,0:T(8,128)(2,1)S(1)} %copy-done.18), kind=kOutput, calls=%fused_computation.27 | convolution fusion | flops 1823932416 | bytes 7176192 | tf_op jit(solution)/shard_map/dot_general | solution.py:146
  231.4 1.8 collective-permute-done.3
  233.1 7.4 %collective-permute-done.5 = bf16[128,1152]{1,0:T(8,128)(2,1)S(1)} collective-permute-done((bf16[128,1152]{1,0:T(8,128)(2,1)S(1)}, bf16[128,1152]{1,0:T(8,128)(2,1)S(1)}, u32[]{:S(2)}, u32[]{:S(2)}) %collective-permute-start.5) | collective-permute-done | bytes 294944 | tf_op jit(solution)/shard_map/ppermute | solution.py:129
  240.5 10.0 %collective-permute-done.4 = bf16[128,1152]{1,0:T(8,128)(2,1)S(1)} collective-permute-done((bf16[128,1152]{1,0:T(8,128)(2,1)S(1)}, bf16[128,1152]{1,0:T(8,128)(2,1)S(1)}, u32[]{:S(2)}, u32[]{:S(2)}) %collective-permute-start.4) | collective-permute-done | bytes 294944 | tf_op jit(solution)/shard_map/ppermute | solution.py:129
  250.7 0.7 slice.139
  (92 shorter events, 8.7 us)
Async XLA Ops:
  7.2 112.6 %copy-start = (bf16[1,384,2048]{2,1,0:T(8,128)(2,1)S(1)}, bf16[1,384,2048]{2,1,0:T(8,128)(2,1)}, u32[]{:S(2)}) copy-start(bf16[1,384,2048]{2,1,0:T(8,128)(2,1)} %param.13) | copy-start | bytes 4718596
  7.2 3.5 %copy-start.17 = (bf16[128,8]{0,1:T(8,128)(2,1)S(1)}, bf16[128,8]{0,1:T(8,128)(2,1)}, u32[]{:S(2)}) copy-start(bf16[128,8]{0,1:T(8,128)(2,1)} %param.10) | copy-start | bytes 6148
  11.8 41.6 %collective-permute-start.1 = (bf16[128,2176]{0,1:T(8,128)(2,1)}, bf16[128,2176]{0,1:T(8,128)(2,1)S(1)}, u32[]{:S(2)}, u32[]{:S(2)}) collective-permute-start(bf16[128,2176]{0,1:T(8,128)(2,1)} %get-tuple-element.55), channel_id=1, source_target_pairs={{0,16},{8,24},{16,0},{24,8},{1,17},{9,25},{17,1},{25,9},{2,18},{10... | collective-permute-start | bytes 1671176 | tf_op jit(solution)/shard_map/ppermute | solution.py:25
  15.8 37.6 %collective-permute-start = (bf16[128,2176]{0,1:T(8,128)(2,1)}, bf16[128,2176]{0,1:T(8,128)(2,1)S(1)}, u32[]{:S(2)}, u32[]{:S(2)}) collective-permute-start(bf16[128,2176]{0,1:T(8,128)(2,1)} %get-tuple-element.55), channel_id=1, source_target_pairs={{0,8},{8,16},{16,24},{24,0},{1,9},{9,17},{17,25},{25,1},{2,10},{10... | collective-permute-start | bytes 1671176 | tf_op jit(solution)/shard_map/ppermute | solution.py:25
  17.4 36.7 %collective-permute-start.2 = (bf16[128,2176]{0,1:T(8,128)(2,1)}, bf16[128,2176]{0,1:T(8,128)(2,1)S(1)}, u32[]{:S(2)}, u32[]{:S(2)}) collective-permute-start(bf16[128,2176]{0,1:T(8,128)(2,1)} %get-tuple-element.55), channel_id=1, source_target_pairs={{0,24},{8,0},{16,8},{24,16},{1,25},{9,1},{17,9},{25,17},{2,26},{10... | collective-permute-start | bytes 1671176 | tf_op jit(solution)/shard_map/ppermute | solution.py:25
  27.2 37.9 %all-to-all-start = ((bf16[1,4,72,2176]{3,2,0,1:T(8,128)(2,1)}), bf16[1,4,72,2176]{3,2,0,1:T(8,128)(2,1)}, u32[]{:S(2)}, u32[]{:S(2)}) async-start(bf16[1,4,72,2176]{3,2,0,1:T(8,128)(2,1)} %pad_maximum_fusion.14), calls=%async_computation | async-start | bytes 2506752 | tf_op jit(solution)/shard_map/all_to_all | solution.py:67
  60.1 2.6 %copy-start.15 = (bf16[3,288,128]{2,1,0:T(8,128)(2,1)}, bf16[3,288,128]{2,1,0:T(8,128)(2,1)S(1)}, u32[]{:S(2)}) copy-start(bf16[3,288,128]{2,1,0:T(8,128)(2,1)S(1)} %fusion.23) | copy-start | bytes 663556
  65.1 45.7 %all-to-all-start.2 = ((bf16[3,4,72,2176]{3,2,0,1:T(8,128)(2,1)}), bf16[3,4,72,2176]{3,2,0,1:T(8,128)(2,1)}, u32[]{:S(2)}, u32[]{:S(2)}) async-start(bf16[3,4,72,2176]{3,2,0,1:T(8,128)(2,1)} %copy.78), calls=%async_computation.3 | async-start | bytes 7520256 | tf_op jit(solution)/shard_map/all_to_all | solution.py:67
  69.9 45.4 %all-gather.3.cloned.1.call-start = ((), (), s32[]{:S(2)}) async-start(), calls=%async_computation.6 | async-start | bytes 3760128 | tf_op jit(solution)/shard_map/all_gather | solution.py:70
  70.6 75.1 %all-gather.5.cloned.1.call-start = ((), (), s32[]{:S(2)}) async-start(), calls=%async_computation.8 | async-start | bytes 11280384 | tf_op jit(solution)/shard_map/all_gather | solution.py:70
  115.0 1.4 copy-start.3
  115.0 50.3 %reduce-scatter.3.cloned.1.call-start = ((), (), s32[]{:S(2)}) async-start(), calls=%async_computation.7 | async-start | bytes 3981312 | tf_op jit(solution)/shard_map/reduce_scatter | solution.py:110
  116.4 2.2 copy-start.4
  116.4 2.5 copy-start.11
  121.4 1.8 copy-start.13
  125.5 57.7 %reduce-scatter.5.cloned.1.call-start = ((), (), s32[]{:S(2)}) async-start(), calls=%async_computation.9 | async-start | bytes 11943936 | tf_op jit(solution)/shard_map/reduce_scatter | solution.py:110
  146.8 4.2 %copy-start.2 = (bf16[2,864,2176]{2,1,0:T(8,128)(2,1)S(1)}, bf16[2,864,2176]{2,1,0:T(8,128)(2,1)}, u32[]{:S(2)}) copy-start(bf16[2,864,2176]{2,1,0:T(8,128)(2,1)} %all-gather.5.cloned.1.call-done) | copy-start | bytes 22560772
  146.8 4.6 %copy-start.5 = (bf16[1,2048,384]{2,1,0:T(8,128)(2,1)S(1)}, bf16[1,2048,384]{2,1,0:T(8,128)(2,1)}, u32[]{:S(2)}) copy-start(bf16[1,2048,384]{2,1,0:T(8,128)(2,1)} %param.12) | copy-start | bytes 4718596
  156.8 1.6 copy-start.9
  156.8 3.8 %copy-start.7 = (bf16[864,384]{1,0:T(8,128)(2,1)}, bf16[864,384]{1,0:T(8,128)(2,1)S(1)}, u32[]{:S(2)}) copy-start(bf16[864,384]{1,0:T(8,128)(2,1)S(1)} %get-tuple-element.41) | copy-start | bytes 1990660
  167.5 13.9 %all-to-all-start.1 = ((bf16[1,4,72,1152]{3,2,0,1:T(8,128)(2,1)}), bf16[1,4,72,1152]{3,2,0,1:T(8,128)(2,1)S(1)}, u32[]{:S(2)}, u32[]{:S(2)}) async-start(bf16[1,4,72,1152]{3,2,0,1:T(8,128)(2,1)} %bitcast.22), calls=%async_computation.2 | async-start | bytes 1327104 | tf_op jit(solution)/shard_map/all_to_all | solution.py:113
  186.9 29.0 %all-to-all-start.3 = ((bf16[3,4,72,1152]{3,2,0,1:T(8,128)(2,1)}), bf16[3,4,72,1152]{3,2,0,1:T(8,128)(2,1)}, u32[]{:S(2)}, u32[]{:S(2)}) async-start(bf16[3,4,72,1152]{3,2,0,1:T(8,128)(2,1)} %copy.81), calls=%async_computation.5 | async-start | bytes 3981312 | tf_op jit(solution)/shard_map/all_to_all | solution.py:113
  191.4 6.0 %copy-start.8 = (bf16[864,384]{1,0:T(8,128)(2,1)S(1)}, bf16[864,384]{1,0:T(8,128)(2,1)}, u32[]{:S(2)}) copy-start(bf16[864,384]{1,0:T(8,128)(2,1)} %copy-done.7) | copy-start | bytes 1990660
  191.4 6.0 %copy-start.12 = (bf16[288,2048]{1,0:T(8,128)(2,1)S(1)}, bf16[288,2048]{1,0:T(8,128)(2,1)}, u32[]{:S(2)}) copy-start(bf16[288,2048]{1,0:T(8,128)(2,1)} %get-tuple-element.46) | copy-start | bytes 3538948
  191.4 6.0 %copy-start.14 = (bf16[288,384]{1,0:T(8,128)(2,1)S(1)}, bf16[288,384]{1,0:T(8,128)(2,1)}, u32[]{:S(2)}) copy-start(bf16[288,384]{1,0:T(8,128)(2,1)} %copy-done.13) | copy-start | bytes 663556
  197.4 4.0 %copy-start.10 = (bf16[864,384]{1,0:T(8,128)(2,1)S(1)}, bf16[864,384]{1,0:T(8,128)(2,1)}, u32[]{:S(2)}) copy-start(bf16[864,384]{1,0:T(8,128)(2,1)} %copy-done.9) | copy-start | bytes 1990660
  205.3 12.6 %copy-start.16 = (bf16[3,288,128]{2,1,0:T(8,128)(2,1)S(1)}, bf16[3,288,128]{2,1,0:T(8,128)(2,1)}, u32[]{:S(2)}) copy-start(bf16[3,288,128]{2,1,0:T(8,128)(2,1)} %copy-done.15) | copy-start | bytes 663556
  217.8 8.9 %copy-start.18 = (bf16[288,384]{1,0:T(8,128)(2,1)S(1)}, bf16[288,384]{1,0:T(8,128)(2,1)}, u32[]{:S(2)}) copy-start(bf16[288,384]{1,0:T(8,128)(2,1)} %get-tuple-element.49) | copy-start | bytes 663556
  220.6 6.2 %copy-start.6 = (bf16[864,2048]{1,0:T(8,128)(2,1)S(1)}, bf16[864,2048]{1,0:T(8,128)(2,1)}, u32[]{:S(2)}) copy-start(bf16[864,2048]{1,0:T(8,128)(2,1)} %get-tuple-element.39) | copy-start | bytes 10616836
  222.0 11.1 %collective-permute-start.3 = (bf16[128,1152]{1,0:T(8,128)(2,1)S(1)}, bf16[128,1152]{1,0:T(8,128)(2,1)S(1)}, u32[]{:S(2)}, u32[]{:S(2)}) collective-permute-start(bf16[128,1152]{1,0:T(8,128)(2,1)S(1)} %get-tuple-element.51), channel_id=1, source_target_pairs={{0,24},{8,0},{16,8},{24,16},{1,25},{9,1},{17,9},{25,17},{2,26},{10... | collective-permute-start | bytes 884744 | tf_op jit(solution)/shard_map/ppermute | solution.py:129
  225.7 14.9 %collective-permute-start.5 = (bf16[128,1152]{1,0:T(8,128)(2,1)S(1)}, bf16[128,1152]{1,0:T(8,128)(2,1)S(1)}, u32[]{:S(2)}, u32[]{:S(2)}) collective-permute-start(bf16[128,1152]{1,0:T(8,128)(2,1)S(1)} %get-tuple-element.52), channel_id=1, source_target_pairs={{0,8},{8,16},{16,24},{24,0},{1,9},{9,17},{17,25},{25,1},{2,10},{10... | collective-permute-start | bytes 884744 | tf_op jit(solution)/shard_map/ppermute | solution.py:129
  225.7 24.8 %collective-permute-start.4 = (bf16[128,1152]{1,0:T(8,128)(2,1)S(1)}, bf16[128,1152]{1,0:T(8,128)(2,1)S(1)}, u32[]{:S(2)}, u32[]{:S(2)}) collective-permute-start(bf16[128,1152]{1,0:T(8,128)(2,1)S(1)} %get-tuple-element.53), channel_id=1, source_target_pairs={{0,16},{8,24},{16,0},{24,8},{1,17},{9,25},{17,1},{25,9},{2,18},{10... | collective-permute-start | bytes 884744 | tf_op jit(solution)/shard_map/ppermute | solution.py:129
  226.8 25.3 %copy-start.1 = (bf16[1,384,2048]{2,1,0:T(8,128)(2,1)S(1)}, bf16[1,384,2048]{2,1,0:T(8,128)(2,1)}, u32[]{:S(2)}) copy-start(bf16[1,384,2048]{2,1,0:T(8,128)(2,1)} %param.13) | copy-start | bytes 4718596
Sparse Core Ops, SparseCore 0:
  72.3 22.2 all-gather.2
  115.1 30.4 all-gather.4
  147.9 11.3 reduce-scatter.2
  165.4 17.7 reduce-scatter.4

commit v5 on v4

--- a/solution.py
+++ b/solution.py
@@ -67,10 +67,11 @@
         recv = lax.all_to_all(
             send.reshape(n_mem, n_ex, capacity, features + lanes), "expert", split_axis=1, concat_axis=1, tiled=True
         ).reshape(n_mem * block_slots, features + lanes)
-        both = lax.all_gather(recv, "tensor")
-        routed_x = both[0, :, :features]
-        routed_dy = both[1, :, :features]
-        routed_gate = both[0, :, features]
+        other = lax.ppermute(recv, "tensor", [(0, 1), (1, 0)])
+        mine_x = core == 0
+        routed_x = jnp.where(mine_x, recv[:, :features], other[:, :features])
+        routed_dy = jnp.where(mine_x, other[:, :features], recv[:, :features])
+        routed_gate = jnp.where(mine_x, recv[:, features], other[:, features])
 
         gate_pre = jnp.dot(routed_x, weight_g, preferred_element_type=jnp.float32)
         up_pre = jnp.dot(routed_x, weight_u, preferred_element_type=jnp.float32)

time: 259 us -> 253 us (0.977)
  local copies, waits for them, and re-layouts: 25.5 us -> 17.9 us
  other arithmetic: 27.2 us -> 32.2 us
  matrix products: 40.4 us -> 37.1 us
    reduce_scatter x2, waiting for transfers between devices: 0.75 us -> 22.6 us  [on_device(): lax.psum_scatter(jnp.concatenate(pieces, axis=1), 'tensor', scatter_dimen...]
    all_gather x2 -> x0, waiting for transfers between devices: 20.2 us -> none  [on_device(): both = lax.all_gather(recv, 'tensor')]
    squeeze x2 -> x0, local copies, waits for them, and re-layouts: 9.41 us -> none  [on_device(): routed_dy = both[1, :, :features]]
    all_to_all x2, waiting for transfers between devices: 17.2 us -> 10.2 us  [on_device(): lax.all_to_all(ret.reshape(n_mem, n_ex, capacity, half + lanes), 'expert'...]
    select_n x0 -> x2, other arithmetic: none -> 4.77 us  [on_device(): routed_x = jnp.where(mine_x, recv[:, :features], other[:, :features])]
    ppermute x3, waiting for transfers between devices: 19.1 us -> 23.4 us  [on_device(): part = lax.ppermute(part, 'dp', [(i, (i - s) % n_dp) for i in range(n_dp)])]
    unnamed x42 -> x44, local copies, waits for them, and re-layouts: 4.33 us -> 6.14 us
  transfers between devices with their start and end apart: 14 -> 14, of which waited for: 10 -> 9; matrix products, arithmetic and copies ran while one was open for 29% -> 30% of each run, Pallas kernels for 0% -> 0%
where the time goes in v5:
time: 253 us; the launch traced here: 252 us
  waiting for transfers between devices  120 us (47%)
  matrix products  37.1 us (15%)
  other arithmetic  32.2 us (13%)
  starting transfers between devices  30.6 us (12%)
  local copies, waits for them, and re-layouts  17.9 us (7%)
  between operations  14.7 us (6%)
    all_to_all x2, waiting for transfers between devices, on_device(): lax.all_to_all(send.reshape(n_mem, n_ex, capacity, features + lanes), 'ex...  40.6 us
    ppermute x3, waiting for transfers between devices, on_device(): part = lax.ppermute(part, 'dp', [(i, (i - s) % n_dp) for i in range(n_dp)])  23.4 us
    ppermute x3, waiting for transfers between devices, on_device(): lax.ppermute(ext, 'dp', [(i, (i + s) % n_dp) for i in range(n_dp)])  22.7 us
    reduce_scatter x2, waiting for transfers between devices, on_device(): lax.psum_scatter(jnp.concatenate(pieces, axis=1), 'tensor', scatter_dimen...  22.6 us
    all_to_all x2, waiting for transfers between devices, on_device(): lax.all_to_all(ret.reshape(n_mem, n_ex, capacity, half + lanes), 'expert'...  10.2 us
    all_to_all x2, starting transfers between devices, on_device(): lax.all_to_all(send.reshape(n_mem, n_ex, capacity, features + lanes), 'ex...  9.03 us
    all_to_all x2, starting transfers between devices, on_device(): lax.all_to_all(ret.reshape(n_mem, n_ex, capacity, half + lanes), 'expert'...  8.76 us
    ppermute x3, starting transfers between devices, on_device(): lax.ppermute(ext, 'dp', [(i, (i + s) % n_dp) for i in range(n_dp)])  7.86 us
  transfers between devices with their start and end apart: 14, of which 9 were waited for; matrix products, arithmetic and copies ran while one was open for 30% of the time, Pallas kernels for 0%

profile of v5, /device:TPU:0, one launch (start us, length us, event | category | flops | bytes accessed | tf_op | source)
XLA Modules:
  0.0 251.9 jit_solution(15046514839338501418)
XLA Ops:
  7.2 0.8 convert_element_type.197
  8.0 1.3 copy.64
  9.3 1.3 copy.65
  10.7 1.1 fusion.105
  11.8 4.0 %collective-permute-start.2 = (bf16[128,2176]{0,1:T(8,128)(2,1)}, bf16[128,2176]{0,1:T(8,128)(2,1)S(1)}, u32[]{:S(2)}, u32[]{:S(2)}) collective-permute-start(bf16[128,2176]{0,1:T(8,128)(2,1)} %get-tuple-element.55), channel_id=1, source_target_pairs={{0,16},{8,24},{16,0},{24,8},{1,17},{9,25},{17,1},{25,9},{2,18},{10... | collective-permute-start | bytes 1671176 | tf_op jit(solution)/shard_map/ppermute | solution.py:25
  15.8 1.6 collective-permute-start.1
  17.4 2.2 collective-permute-start.3
  19.7 0.7 fusion.101
  20.3 0.7 convert_subtract_fusion.1
  21.2 0.8 fusion.58
  22.2 0.7 fusion.100
  23.3 1.1 select_reduce_fusion.3
  24.5 1.5 convolution_convert_fusion.1
  26.0 1.2 pad_maximum_fusion.14
  27.2 4.3 %all-to-all-start = ((bf16[1,4,72,2176]{3,2,0,1:T(8,128)(2,1)}), bf16[1,4,72,2176]{3,2,0,1:T(8,128)(2,1)}, u32[]{:S(2)}, u32[]{:S(2)}) async-start(bf16[1,4,72,2176]{3,2,0,1:T(8,128)(2,1)} %pad_maximum_fusion.14), calls=%async_computation | async-start | bytes 2506752 | tf_op jit(solution)/shard_map/all_to_all | solution.py:67
  31.5 22.0 %collective-permute-done.2 = bf16[128,2176]{0,1:T(8,128)(2,1)S(1)} collective-permute-done((bf16[128,2176]{0,1:T(8,128)(2,1)}, bf16[128,2176]{0,1:T(8,128)(2,1)S(1)}, u32[]{:S(2)}, u32[]{:S(2)}) %collective-permute-start.2) | collective-permute-done | bytes 557088 | tf_op jit(solution)/shard_map/ppermute | solution.py:25
  53.4 0.7 collective-permute-done.3
  54.1 0.6 maximum_convert_fusion
  54.7 1.4 pad_maximum_fusion.13
  57.2 2.4 select_reduce_fusion.1
  59.8 1.6 fusion.23
  61.4 2.6 %convolution_convert_fusion = bf16[3,288,2048]{2,1,0:T(8,128)(2,1)S(1)} fusion(bf16[3,288,128]{2,1,0:T(8,128)(2,1)S(1)} %fusion.23, bf16[3,128,2176]{1,2,0:T(8,128)(2,1)} %pad_maximum_fusion.13), kind=kOutput, calls=%fused_computation.19 | convolution fusion | flops 454754304 | bytes 5332992 | tf_op jit(solution)/shard_map/mqt,mtf->mqf/dot_general | solution.py:58
  64.3 2.1 copy.78
  66.4 4.8 %all-to-all-start.2 = ((bf16[3,4,72,2176]{3,2,0,1:T(8,128)(2,1)}), bf16[3,4,72,2176]{3,2,0,1:T(8,128)(2,1)}, u32[]{:S(2)}, u32[]{:S(2)}) async-start(bf16[3,4,72,2176]{3,2,0,1:T(8,128)(2,1)} %copy.78), calls=%async_computation.3 | async-start | bytes 7520256 | tf_op jit(solution)/shard_map/all_to_all | solution.py:67
  71.5 40.6 %all-to-all-done.2 = bf16[3,4,72,2176]{3,2,0,1:T(8,128)(2,1)} async-done(((bf16[3,4,72,2176]{3,2,0,1:T(8,128)(2,1)}), bf16[3,4,72,2176]{3,2,0,1:T(8,128)(2,1)}, u32[]{:S(2)}, u32[]{:S(2)}) %all-to-all-start.2) | async-done | bytes 3760160 | tf_op jit(solution)/shard_map/all_to_all | solution.py:67
  112.1 4.2 %copy.79 = bf16[3,4,72,2176]{3,2,1,0:T(8,128)(2,1)} copy(bf16[3,4,72,2176]{3,2,0,1:T(8,128)(2,1)} %all-to-all-done.2) | data formatting | bytes 7520256 | tf_op jit(solution)/shard_map/all_to_all | solution.py:67
  116.3 1.0 convert_reduce_fusion.3
  117.3 1.4 broadcast_select_fusion.2
  118.8 0.8 fusion.38
  119.7 1.3 copy-done.3
  121.0 0.8 fusion.34
  122.4 1.7 multiply_convert_fusion.4
  126.4 1.7 pad_maximum_fusion.8
  128.2 1.2 convert_reduce_fusion.1
  129.4 3.3 %broadcast_select_fusion = (bf16[864,2048]{1,0:T(8,128)(2,1)S(1)}, bf16[864,2048]{1,0:T(8,128)(2,1)S(1)}) fusion(pred[]{:T(512)S(6)} %eq.88, bf16[864,2176]{1,0:T(8,128)(2,1)} %bitcast.32, bf16[864,2176]{1,0:T(8,128)(2,1)} %collective-permute-done.4), kind=kLoop, calls=%fused_computation.17 | loop fusion | flops 3538944 | bytes 14155777 | tf_op jit(solution)/shard_map/jit(_where)/select_n | solution.py:72
  132.8 2.0 fusion.36
  135.4 2.0 fusion.32
  137.4 3.4 %multiply_convert_fusion.1 = (bf16[864,384]{1,0:T(8,128)(2,1)S(1)}, bf16[864,384]{1,0:T(8,128)(2,1)S(1)}, bf16[864,384]{1,0:T(8,128)(2,1)}, bf16[864,384]{1,0:T(8,128)(2,1)S(1)}) fusion(f32[864,384]{1,0:T(8,128)S(1)} %fusion.36, f32[864]{0:T(1024)S(1)} %convert_reduce_fusion.1, f32[864,384]{1,0:T(8,128)S(1)} %fusion.32, ...), kind=kOutput, calls=%fused_computation.59 | convolution fusion | flops 1365258240 | bytes 10423680 | tf_op jit(solution)/shard_map/dot_general | solution.py:76
  141.3 1.1 fusion.71
  142.4 1.1 fusion.77
  143.5 1.1 convolution_add_fusion
  144.6 1.1 convolution_add_fusion.1
  145.8 3.6 %pad_maximum_fusion = f32[864,2304]{1,0:T(8,128)} fusion(f32[864,128]{1,0:T(8,128)S(1)} %pad.35, f32[864,1024]{1,0:T(8,128)S(1)} %convolution_add_fusion, f32[864,1024]{1,0:T(8,128)S(1)} %convolution_add_fusion.1), kind=kLoop, calls=%fused_computation | loop fusion | flops 5971968 | bytes 15482880 | tf_op jit(solution)/shard_map/concatenate | solution.py:112
  149.4 1.3 reduce-scatter.3.cloned.1.call-done
  150.6 2.2 convert_element_type.209
  152.9 4.0 %all-to-all-start.1 = ((bf16[1,4,72,1152]{3,2,0,1:T(8,128)(2,1)}), bf16[1,4,72,1152]{3,2,0,1:T(8,128)(2,1)S(1)}, u32[]{:S(2)}, u32[]{:S(2)}) async-start(bf16[1,4,72,1152]{3,2,0,1:T(8,128)(2,1)} %bitcast.20), calls=%async_computation.2 | async-start | bytes 1327104 | tf_op jit(solution)/shard_map/all_to_all | solution.py:114
  156.9 21.3 %reduce-scatter.5.cloned.1.call-done = f32[864,1152]{1,0:T(8,128)} async-done(((f32[864,2304]{1,0:T(8,128)}), f32[864,1152]{1,0:T(8,128)}) %reduce-scatter.5.cloned.1.call-update) | async-done | bytes 3981328 | tf_op jit(solution)/shard_map/reduce_scatter | solution.py:111
  178.1 2.3 convert_element_type.225
  180.5 1.5 copy.81
  181.9 4.8 %all-to-all-start.3 = ((bf16[3,4,72,1152]{3,2,0,1:T(8,128)(2,1)}), bf16[3,4,72,1152]{3,2,0,1:T(8,128)(2,1)}, u32[]{:S(2)}, u32[]{:S(2)}) async-start(bf16[3,4,72,1152]{3,2,0,1:T(8,128)(2,1)} %copy.81), calls=%async_computation.5 | async-start | bytes 3981312 | tf_op jit(solution)/shard_map/all_to_all | solution.py:114
  186.8 5.7 %fusion.18 = bf16[1,384,2048]{2,1,0:T(8,128)(2,1)} fusion(bf16[864,2048]{1,0:T(8,128)(2,1)} %copy-done.7, bf16[288,2048]{1,0:T(8,128)(2,1)S(1)} %copy-done.11, bf16[864,384]{1,0:T(8,128)(2,1)} %get-tuple-element.43, bf16[288,384]{1,0:T(8,128)(2,1)S(1)} %copy-done.19), kind=kOutput, calls=%fused_computation.27 | convolution fusion | flops 1823932416 | bytes 7176192 | tf_op jit(solution)/shard_map/dot_general | solution.py:147
  192.6 3.9 %fusion.21 = bf16[1,2048,384]{2,1,0:T(8,128)(2,1)} fusion(bf16[864,2048]{1,0:T(8,128)(2,1)S(1)} %copy-done.6, bf16[288,2048]{1,0:T(8,128)(2,1)S(1)} %copy-done.9, bf16[864,384]{1,0:T(8,128)(2,1)S(1)} %get-tuple-element.41, bf16[288,384]{1,0:T(8,128)(2,1)S(1)} %copy-done.15), kind=kOutput, calls=%fused_computation.28 | convolution fusion | flops 1823932416 | bytes 7176192 | tf_op jit(solution)/shard_map/dot_general | solution.py:143
  196.5 3.9 %fusion.22 = bf16[1,2048,384]{2,1,0:T(8,128)(2,1)} fusion(bf16[864,2048]{1,0:T(8,128)(2,1)S(1)} %copy-done.6, bf16[288,2048]{1,0:T(8,128)(2,1)S(1)} %copy-done.9, bf16[864,384]{1,0:T(8,128)(2,1)S(1)} %get-tuple-element.42, bf16[288,384]{1,0:T(8,128)(2,1)S(1)} %copy-done.13), kind=kOutput, calls=%fused_computation.29 | convolution fusion | flops 1823932416 | bytes 7176192 | tf_op jit(solution)/shard_map/dot_general | solution.py:139
  201.0 10.2 %all-to-all-done.3 = bf16[3,4,72,1152]{3,2,0,1:T(8,128)(2,1)} async-done(((bf16[3,4,72,1152]{3,2,0,1:T(8,128)(2,1)}), bf16[3,4,72,1152]{3,2,0,1:T(8,128)(2,1)}, u32[]{:S(2)}, u32[]{:S(2)}) %all-to-all-start.3) | async-done | bytes 1990688 | tf_op jit(solution)/shard_map/all_to_all | solution.py:114
  211.2 1.7 copy.82
  213.1 0.6 fusion.40
  213.8 1.1 select_reduce_fusion
  215.2 3.4 %collective-permute-start.5 = (bf16[128,1152]{1,0:T(8,128)(2,1)S(1)}, bf16[128,1152]{1,0:T(8,128)(2,1)S(1)}, u32[]{:S(2)}, u32[]{:S(2)}) collective-permute-start(bf16[128,1152]{1,0:T(8,128)(2,1)S(1)} %get-tuple-element.51), channel_id=1, source_target_pairs={{0,24},{8,0},{16,8},{24,16},{1,25},{9,1},{17,9},{25,17},{2,26},{10... | collective-permute-start | bytes 884744 | tf_op jit(solution)/shard_map/ppermute | solution.py:130
  218.6 1.2 collective-permute-start.6
  220.1 6.0 %collective-permute-done.5 = bf16[128,1152]{1,0:T(8,128)(2,1)S(1)} collective-permute-done((bf16[128,1152]{1,0:T(8,128)(2,1)S(1)}, bf16[128,1152]{1,0:T(8,128)(2,1)S(1)}, u32[]{:S(2)}, u32[]{:S(2)}) %collective-permute-start.5) | collective-permute-done | bytes 294944 | tf_op jit(solution)/shard_map/ppermute | solution.py:130
  226.1 7.5 %collective-permute-done.7 = bf16[128,1152]{1,0:T(8,128)(2,1)S(1)} collective-permute-done((bf16[128,1152]{1,0:T(8,128)(2,1)S(1)}, bf16[128,1152]{1,0:T(8,128)(2,1)S(1)}, u32[]{:S(2)}, u32[]{:S(2)}) %collective-permute-start.7) | collective-permute-done | bytes 294944 | tf_op jit(solution)/shard_map/ppermute | solution.py:130
  233.6 9.9 %collective-permute-done.6 = bf16[128,1152]{1,0:T(8,128)(2,1)S(1)} collective-permute-done((bf16[128,1152]{1,0:T(8,128)(2,1)S(1)}, bf16[128,1152]{1,0:T(8,128)(2,1)S(1)}, u32[]{:S(2)}, u32[]{:S(2)}) %collective-permute-start.6) | collective-permute-done | bytes 294944 | tf_op jit(solution)/shard_map/ppermute | solution.py:130
  243.7 0.7 slice.153
  244.4 0.7 copy.84
  (92 shorter events, 8.7 us)
Async XLA Ops:
  7.2 111.6 %copy-start = (bf16[1,384,2048]{2,1,0:T(8,128)(2,1)S(1)}, bf16[1,384,2048]{2,1,0:T(8,128)(2,1)}, u32[]{:S(2)}) copy-start(bf16[1,384,2048]{2,1,0:T(8,128)(2,1)} %param.13) | copy-start | bytes 4718596
  7.2 3.5 %copy-start.18 = (bf16[128,8]{0,1:T(8,128)(2,1)S(1)}, bf16[128,8]{0,1:T(8,128)(2,1)}, u32[]{:S(2)}) copy-start(bf16[128,8]{0,1:T(8,128)(2,1)} %param.10) | copy-start | bytes 6148
  11.8 41.6 %collective-permute-start.2 = (bf16[128,2176]{0,1:T(8,128)(2,1)}, bf16[128,2176]{0,1:T(8,128)(2,1)S(1)}, u32[]{:S(2)}, u32[]{:S(2)}) collective-permute-start(bf16[128,2176]{0,1:T(8,128)(2,1)} %get-tuple-element.55), channel_id=1, source_target_pairs={{0,16},{8,24},{16,0},{24,8},{1,17},{9,25},{17,1},{25,9},{2,18},{10... | collective-permute-start | bytes 1671176 | tf_op jit(solution)/shard_map/ppermute | solution.py:25
  15.8 37.6 %collective-permute-start.1 = (bf16[128,2176]{0,1:T(8,128)(2,1)}, bf16[128,2176]{0,1:T(8,128)(2,1)S(1)}, u32[]{:S(2)}, u32[]{:S(2)}) collective-permute-start(bf16[128,2176]{0,1:T(8,128)(2,1)} %get-tuple-element.55), channel_id=1, source_target_pairs={{0,8},{8,16},{16,24},{24,0},{1,9},{9,17},{17,25},{25,1},{2,10},{10... | collective-permute-start | bytes 1671176 | tf_op jit(solution)/shard_map/ppermute | solution.py:25
  17.4 36.7 %collective-permute-start.3 = (bf16[128,2176]{0,1:T(8,128)(2,1)}, bf16[128,2176]{0,1:T(8,128)(2,1)S(1)}, u32[]{:S(2)}, u32[]{:S(2)}) collective-permute-start(bf16[128,2176]{0,1:T(8,128)(2,1)} %get-tuple-element.55), channel_id=1, source_target_pairs={{0,24},{8,0},{16,8},{24,16},{1,25},{9,1},{17,9},{25,17},{2,26},{10... | collective-permute-start | bytes 1671176 | tf_op jit(solution)/shard_map/ppermute | solution.py:25
  27.2 39.2 %all-to-all-start = ((bf16[1,4,72,2176]{3,2,0,1:T(8,128)(2,1)}), bf16[1,4,72,2176]{3,2,0,1:T(8,128)(2,1)}, u32[]{:S(2)}, u32[]{:S(2)}) async-start(bf16[1,4,72,2176]{3,2,0,1:T(8,128)(2,1)} %pad_maximum_fusion.14), calls=%async_computation | async-start | bytes 2506752 | tf_op jit(solution)/shard_map/all_to_all | solution.py:67
  61.4 2.6 %copy-start.16 = (bf16[3,288,128]{2,1,0:T(8,128)(2,1)}, bf16[3,288,128]{2,1,0:T(8,128)(2,1)S(1)}, u32[]{:S(2)}) copy-start(bf16[3,288,128]{2,1,0:T(8,128)(2,1)S(1)} %fusion.23) | copy-start | bytes 663556
  66.4 45.7 %all-to-all-start.2 = ((bf16[3,4,72,2176]{3,2,0,1:T(8,128)(2,1)}), bf16[3,4,72,2176]{3,2,0,1:T(8,128)(2,1)}, u32[]{:S(2)}, u32[]{:S(2)}) async-start(bf16[3,4,72,2176]{3,2,0,1:T(8,128)(2,1)} %copy.78), calls=%async_computation.3 | async-start | bytes 7520256 | tf_op jit(solution)/shard_map/all_to_all | solution.py:67
  71.2 79.5 %reduce-scatter.3.cloned.1.call-start = ((), (), s32[]{:S(2)}) async-start(), calls=%async_computation.6 | async-start | bytes 3981312 | tf_op jit(solution)/shard_map/reduce_scatter | solution.py:111
  71.4 44.9 %collective-permute-start = (bf16[288,2176]{1,0:T(8,128)(2,1)}, bf16[288,2176]{1,0:T(8,128)(2,1)S(1)}, u32[]{:S(2)}, u32[]{:S(2)}) collective-permute-start(bf16[288,2176]{1,0:T(8,128)(2,1)} %bitcast.11), channel_id=1, source_target_pairs={{0,1},{1,0},{2,3},{3,2},{4,5},{5,4},{6,7},{7,6},{8,9},{9,8},{10,11... | collective-permute-start | bytes 3760136 | tf_op jit(solution)/shard_map/ppermute | solution.py:70
  116.3 11.9 %collective-permute-start.4 = (bf16[864,2176]{1,0:T(8,128)(2,1)}, bf16[864,2176]{1,0:T(8,128)(2,1)}, u32[]{:S(2)}, u32[]{:S(2)}) collective-permute-start(bf16[864,2176]{1,0:T(8,128)(2,1)} %bitcast.32), channel_id=1, source_target_pairs={{0,1},{1,0},{2,3},{3,2},{4,5},{5,4},{6,7},{7,6},{8,9},{9,8},{10,11... | collective-permute-start | bytes 11280392 | tf_op jit(solution)/shard_map/ppermute | solution.py:70
  118.7 1.0 copy-start.10
  118.7 3.1 %copy-start.8 = (bf16[288,2048]{1,0:T(8,128)(2,1)}, bf16[288,2048]{1,0:T(8,128)(2,1)S(1)}, u32[]{:S(2)}) copy-start(bf16[288,2048]{1,0:T(8,128)(2,1)S(1)} %get-tuple-element.45) | copy-start | bytes 3538948
  118.7 2.2 copy-start.3
  121.0 1.4 copy-start.2
  124.1 1.3 copy-start.12
  124.1 1.8 copy-start.14
  128.2 50.0 %reduce-scatter.5.cloned.1.call-start = ((), (), s32[]{:S(2)}) async-start(), calls=%async_computation.7 | async-start | bytes 11943936 | tf_op jit(solution)/shard_map/reduce_scatter | solution.py:111
  132.8 2.0 copy-start.7
  132.8 4.6 %copy-start.5 = (bf16[864,2048]{1,0:T(8,128)(2,1)}, bf16[864,2048]{1,0:T(8,128)(2,1)S(1)}, u32[]{:S(2)}) copy-start(bf16[864,2048]{1,0:T(8,128)(2,1)S(1)} %get-tuple-element.39) | copy-start | bytes 10616836
  132.8 2.6 %copy-start.4 = (bf16[1,2048,384]{2,1,0:T(8,128)(2,1)S(1)}, bf16[1,2048,384]{2,1,0:T(8,128)(2,1)}, u32[]{:S(2)}) copy-start(bf16[1,2048,384]{2,1,0:T(8,128)(2,1)} %param.12) | copy-start | bytes 4718596
  152.9 29.1 %all-to-all-start.1 = ((bf16[1,4,72,1152]{3,2,0,1:T(8,128)(2,1)}), bf16[1,4,72,1152]{3,2,0,1:T(8,128)(2,1)S(1)}, u32[]{:S(2)}, u32[]{:S(2)}) async-start(bf16[1,4,72,1152]{3,2,0,1:T(8,128)(2,1)} %bitcast.20), calls=%async_computation.2 | async-start | bytes 1327104 | tf_op jit(solution)/shard_map/all_to_all | solution.py:114
  181.9 4.8 %copy-start.11 = (bf16[288,2048]{1,0:T(8,128)(2,1)S(1)}, bf16[288,2048]{1,0:T(8,128)(2,1)}, u32[]{:S(2)}) copy-start(bf16[288,2048]{1,0:T(8,128)(2,1)} %copy-done.10) | copy-start | bytes 3538948
  181.9 4.8 %copy-start.19 = (bf16[288,384]{1,0:T(8,128)(2,1)S(1)}, bf16[288,384]{1,0:T(8,128)(2,1)}, u32[]{:S(2)}) copy-start(bf16[288,384]{1,0:T(8,128)(2,1)} %get-tuple-element.49) | copy-start | bytes 663556
  181.9 29.3 %all-to-all-start.3 = ((bf16[3,4,72,1152]{3,2,0,1:T(8,128)(2,1)}), bf16[3,4,72,1152]{3,2,0,1:T(8,128)(2,1)}, u32[]{:S(2)}, u32[]{:S(2)}) async-start(bf16[3,4,72,1152]{3,2,0,1:T(8,128)(2,1)} %copy.81), calls=%async_computation.5 | async-start | bytes 3981312 | tf_op jit(solution)/shard_map/all_to_all | solution.py:114
  186.8 5.8 %copy-start.6 = (bf16[864,2048]{1,0:T(8,128)(2,1)S(1)}, bf16[864,2048]{1,0:T(8,128)(2,1)}, u32[]{:S(2)}) copy-start(bf16[864,2048]{1,0:T(8,128)(2,1)} %copy-done.5) | copy-start | bytes 10616836
  186.8 5.8 %copy-start.9 = (bf16[288,2048]{1,0:T(8,128)(2,1)S(1)}, bf16[288,2048]{1,0:T(8,128)(2,1)}, u32[]{:S(2)}) copy-start(bf16[288,2048]{1,0:T(8,128)(2,1)} %copy-done.8) | copy-start | bytes 3538948
  186.8 5.8 %copy-start.15 = (bf16[288,384]{1,0:T(8,128)(2,1)S(1)}, bf16[288,384]{1,0:T(8,128)(2,1)}, u32[]{:S(2)}) copy-start(bf16[288,384]{1,0:T(8,128)(2,1)} %copy-done.14) | copy-start | bytes 663556
  192.5 3.9 %copy-start.13 = (bf16[288,384]{1,0:T(8,128)(2,1)S(1)}, bf16[288,384]{1,0:T(8,128)(2,1)}, u32[]{:S(2)}) copy-start(bf16[288,384]{1,0:T(8,128)(2,1)} %copy-done.12) | copy-start | bytes 663556
  201.0 12.1 %copy-start.17 = (bf16[3,288,128]{2,1,0:T(8,128)(2,1)S(1)}, bf16[3,288,128]{2,1,0:T(8,128)(2,1)}, u32[]{:S(2)}) copy-start(bf16[3,288,128]{2,1,0:T(8,128)(2,1)} %copy-done.16) | copy-start | bytes 663556
  215.1 30.0 %copy-start.1 = (bf16[1,384,2048]{2,1,0:T(8,128)(2,1)S(1)}, bf16[1,384,2048]{2,1,0:T(8,128)(2,1)}, u32[]{:S(2)}) copy-start(bf16[1,384,2048]{2,1,0:T(8,128)(2,1)} %param.13) | copy-start | bytes 4718596
  215.2 10.9 %collective-permute-start.5 = (bf16[128,1152]{1,0:T(8,128)(2,1)S(1)}, bf16[128,1152]{1,0:T(8,128)(2,1)S(1)}, u32[]{:S(2)}, u32[]{:S(2)}) collective-permute-start(bf16[128,1152]{1,0:T(8,128)(2,1)S(1)} %get-tuple-element.51), channel_id=1, source_target_pairs={{0,24},{8,0},{16,8},{24,16},{1,25},{9,1},{17,9},{25,17},{2,26},{10... | collective-permute-start | bytes 884744 | tf_op jit(solution)/shard_map/ppermute | solution.py:130
  218.6 14.9 %collective-permute-start.7 = (bf16[128,1152]{1,0:T(8,128)(2,1)S(1)}, bf16[128,1152]{1,0:T(8,128)(2,1)S(1)}, u32[]{:S(2)}, u32[]{:S(2)}) collective-permute-start(bf16[128,1152]{1,0:T(8,128)(2,1)S(1)} %get-tuple-element.52), channel_id=1, source_target_pairs={{0,8},{8,16},{16,24},{24,0},{1,9},{9,17},{17,25},{25,1},{2,10},{10... | collective-permute-start | bytes 884744 | tf_op jit(solution)/shard_map/ppermute | solution.py:130
  218.6 24.9 %collective-permute-start.6 = (bf16[128,1152]{1,0:T(8,128)(2,1)S(1)}, bf16[128,1152]{1,0:T(8,128)(2,1)S(1)}, u32[]{:S(2)}, u32[]{:S(2)}) collective-permute-start(bf16[128,1152]{1,0:T(8,128)(2,1)S(1)} %get-tuple-element.53), channel_id=1, source_target_pairs={{0,16},{8,24},{16,0},{24,8},{1,17},{9,25},{17,1},{25,9},{2,18},{10... | collective-permute-start | bytes 884744 | tf_op jit(solution)/shard_map/ppermute | solution.py:130
Sparse Core Ops, SparseCore 0:
  128.3 22.3 reduce-scatter.2
  152.9 25.1 reduce-scatter.4

commit v6 on v5

--- a/solution.py
+++ b/solution.py
@@ -96,21 +96,22 @@
         rows_up.append(up_grad)
         rows_w.append(weighted)
         gate_col = jnp.pad(gate_terms[:, None], ((0, 0), (0, lanes - 1)))
-        pieces = []
         half = features // 2
-        for h in range(2):
-            rows = slice(h * half, (h + 1) * half)
-            pieces.append(
+
+        def hidden_part(c):
+            w_g = lax.dynamic_slice_in_dim(weight_g, c * half, half, axis=0)
+            w_u = lax.dynamic_slice_in_dim(weight_u, c * half, half, axis=0)
+            return jnp.concatenate([
                 lax.dot_general(
-                    pre_grad, weight_g[rows], (((1,), (1,)), ((), ())), preferred_element_type=jnp.float32
+                    pre_grad, w_g, (((1,), (1,)), ((), ())), preferred_element_type=jnp.float32
                 ) + lax.dot_general(
-                    up_grad, weight_u[rows], (((1,), (1,)), ((), ())), preferred_element_type=jnp.float32
-                )
-            )
-            pieces.append(gate_col)
-        ret = lax.psum_scatter(
-            jnp.concatenate(pieces, axis=1), "tensor", scatter_dimension=1, tiled=True
-        ).astype(jnp.bfloat16)
+                    up_grad, w_u, (((1,), (1,)), ((), ())), preferred_element_type=jnp.float32
+                ),
+                gate_col,
+            ], axis=1)
+
+        theirs = lax.ppermute(hidden_part(1 - core), "tensor", [(0, 1), (1, 0)])
+        ret = (hidden_part(core) + theirs).astype(jnp.bfloat16)
         back = lax.all_to_all(
             ret.reshape(n_mem, n_ex, capacity, half + lanes), "expert", split_axis=1, concat_axis=1, tiled=True
         ).reshape(n_mem, block_slots, half + lanes)

time: 253 us -> 257 us (1.016)
  blocking collectives: 0 us -> 19.9 us
  between operations: 14.7 us -> 1.29 us
  waiting for transfers between devices: 120 us -> 109 us
  starting transfers between devices: 30.6 us -> 39.4 us
  other arithmetic: 32.2 us -> 28.6 us
    reduce_scatter x2 -> x0, waiting for transfers between devices: 22.6 us -> none  [on_device(): lax.psum_scatter(jnp.concatenate(pieces, axis=1), 'tensor', scatter_dimen...]
    all_to_all x0 -> x1, blocking collectives: none -> 19.9 us  [on_device(): lax.all_to_all(send.reshape(n_mem, n_ex, capacity, features + lanes), 'ex...]
    ppermute x3, starting transfers between devices: 4.59 us -> 17.3 us  [on_device(): part = lax.ppermute(part, 'dp', [(i, (i - s) % n_dp) for i in range(n_dp)])]
    ppermute x3, waiting for transfers between devices: 22.7 us -> 34.5 us  [on_device(): lax.ppermute(ext, 'dp', [(i, (i + s) % n_dp) for i in range(n_dp)])]
    ppermute x3, waiting for transfers between devices: 23.4 us -> 18.6 us  [on_device(): part = lax.ppermute(part, 'dp', [(i, (i - s) % n_dp) for i in range(n_dp)])]
    all_to_all x2 -> x1, starting transfers between devices: 9.03 us -> 4.9 us  [on_device(): lax.all_to_all(send.reshape(n_mem, n_ex, capacity, features + lanes), 'ex...]
    ppermute x2, waiting for transfers between devices: 0.01 us -> 3.08 us  [on_device(): other = lax.ppermute(recv, 'tensor', [(0, 1), (1, 0)])]
    all_to_all x2, waiting for transfers between devices: 10.2 us -> 13.3 us  [on_device(): lax.all_to_all(ret.reshape(n_mem, n_ex, capacity, half + lanes), 'expert'...]
  transfers between devices with their start and end apart: 14 -> 13, of which waited for: 9 -> 9; matrix products, arithmetic and copies ran while one was open for 30% -> 15% of each run, Pallas kernels for 0% -> 0%
where the time goes in v6:
time: 257 us; the launch traced here: 256 us
  waiting for transfers between devices  109 us (42%)
  starting transfers between devices  39.4 us (15%)
  matrix products  39.2 us (15%)
  other arithmetic  28.6 us (11%)
  blocking collectives  19.9 us (8%)
  local copies, waits for them, and re-layouts  18.7 us (7%)
    all_to_all x1, waiting for transfers between devices, on_device(): lax.all_to_all(send.reshape(n_mem, n_ex, capacity, features + lanes), 'ex...  38.2 us
    ppermute x3, waiting for transfers between devices, on_device(): lax.ppermute(ext, 'dp', [(i, (i + s) % n_dp) for i in range(n_dp)])  34.5 us
    all_to_all x1, blocking collectives, on_device(): lax.all_to_all(send.reshape(n_mem, n_ex, capacity, features + lanes), 'ex...  19.9 us
    ppermute x3, waiting for transfers between devices, on_device(): part = lax.ppermute(part, 'dp', [(i, (i - s) % n_dp) for i in range(n_dp)])  18.6 us
    ppermute x3, starting transfers between devices, on_device(): part = lax.ppermute(part, 'dp', [(i, (i - s) % n_dp) for i in range(n_dp)])  17.3 us
    all_to_all x2, waiting for transfers between devices, on_device(): lax.all_to_all(ret.reshape(n_mem, n_ex, capacity, half + lanes), 'expert'...  13.3 us
    all_to_all x2, starting transfers between devices, on_device(): lax.all_to_all(ret.reshape(n_mem, n_ex, capacity, half + lanes), 'expert'...  8.8 us
    ppermute x3, starting transfers between devices, on_device(): lax.ppermute(ext, 'dp', [(i, (i + s) % n_dp) for i in range(n_dp)])  7.86 us
  transfers between devices with their start and end apart: 13, of which 9 were waited for; matrix products, arithmetic and copies ran while one was open for 15% of the time, Pallas kernels for 0%

profile of v6, /device:TPU:0, one launch (start us, length us, event | category | flops | bytes accessed | tf_op | source)
XLA Modules:
  0.0 256.2 jit_solution(10754889976563559989)
XLA Ops:
  0.7 0.8 convert_element_type.197
  1.5 1.3 copy.64
  2.8 1.3 copy.65
  4.2 1.1 fusion.121
  5.3 4.0 %collective-permute-start.3 = (bf16[128,2176]{0,1:T(8,128)(2,1)}, bf16[128,2176]{0,1:T(8,128)(2,1)S(1)}, u32[]{:S(2)}, u32[]{:S(2)}) collective-permute-start(bf16[128,2176]{0,1:T(8,128)(2,1)} %get-tuple-element.55), channel_id=1, source_target_pairs={{0,16},{8,24},{16,0},{24,8},{1,17},{9,25},{17,1},{25,9},{2,18},{10... | collective-permute-start | bytes 1671176 | tf_op jit(solution)/shard_map/ppermute | solution.py:25
  9.3 1.6 collective-permute-start.2
  10.9 2.2 collective-permute-start.4
  13.1 33.8 %collective-permute-done.3 = bf16[128,2176]{0,1:T(8,128)(2,1)S(1)} collective-permute-done((bf16[128,2176]{0,1:T(8,128)(2,1)}, bf16[128,2176]{0,1:T(8,128)(2,1)S(1)}, u32[]{:S(2)}, u32[]{:S(2)}) %collective-permute-start.3) | collective-permute-done | bytes 557088 | tf_op jit(solution)/shard_map/ppermute | solution.py:25
  46.9 0.7 collective-permute-done.4
  47.6 1.4 pad_maximum_fusion.11
  50.1 1.6 fusion.27
  51.7 1.6 select_reduce_fusion.1
  53.5 2.5 convolution_convert_fusion
  56.4 2.1 copy.78
  58.5 4.9 %all-to-all-start.2 = ((bf16[3,4,72,2176]{3,2,0,1:T(8,128)(2,1)}), bf16[3,4,72,2176]{3,2,0,1:T(8,128)(2,1)}, u32[]{:S(2)}, u32[]{:S(2)}) async-start(bf16[3,4,72,2176]{3,2,0,1:T(8,128)(2,1)} %copy.78), calls=%async_computation.2 | async-start | bytes 7520256 | tf_op jit(solution)/shard_map/all_to_all | solution.py:67
  63.6 0.8 fusion.66
  65.0 0.6 copy-done.20
  66.1 38.2 %all-to-all-done.2 = bf16[3,4,72,2176]{3,2,0,1:T(8,128)(2,1)} async-done(((bf16[3,4,72,2176]{3,2,0,1:T(8,128)(2,1)}), bf16[3,4,72,2176]{3,2,0,1:T(8,128)(2,1)}, u32[]{:S(2)}, u32[]{:S(2)}) %all-to-all-start.2) | async-done | bytes 3760160 | tf_op jit(solution)/shard_map/all_to_all | solution.py:67
  104.3 4.2 %copy.79 = bf16[3,4,72,2176]{3,2,1,0:T(8,128)(2,1)} copy(bf16[3,4,72,2176]{3,2,0,1:T(8,128)(2,1)} %all-to-all-done.2) | data formatting | bytes 7520256 | tf_op jit(solution)/shard_map/all_to_all | solution.py:67
  108.5 1.1 select_reduce_fusion.3
  109.8 19.9 %all_to_all.20 = bf16[1,4,72,2176]{3,2,0,1:T(8,128)(2,1)S(1)} all-to-all(bf16[1,4,72,2176]{3,2,0,1:T(8,128)(2,1)S(1)} %pad_maximum_fusion.12), channel_id=1, replica_groups=mesh['dp'=4,'expert'=4,'tensor'=2] {'expert'}, dimensions={1} | all-to-all | bytes 2506752 | tf_op jit(solution)/shard_map/all_to_all | solution.py:67
  129.7 3.1 %collective-permute-done = bf16[288,2176]{1,0:T(8,128)(2,1)} collective-permute-done((bf16[288,2176]{1,0:T(8,128)(2,1)S(1)}, bf16[288,2176]{1,0:T(8,128)(2,1)}, u32[]{:S(2)}, u32[]{:S(2)}) %collective-permute-start) | collective-permute-done | bytes 1253408 | tf_op jit(solution)/shard_map/ppermute | solution.py:70
  132.8 1.5 broadcast_select_fusion.2
  134.3 0.8 fusion.42
  135.3 1.3 copy-done.1
  136.5 0.8 fusion.38
  137.3 3.3 %broadcast_select_fusion = (bf16[864,2048]{1,0:T(8,128)(2,1)S(1)}, bf16[864,2048]{1,0:T(8,128)(2,1)S(1)}) fusion(pred[]{:T(512)S(6)} %eq.88, bf16[864,2176]{1,0:T(8,128)(2,1)} %bitcast.32, bf16[864,2176]{1,0:T(8,128)(2,1)} %collective-permute-done.5), kind=kLoop, calls=%fused_computation.22 | loop fusion | flops 3538944 | bytes 14155777 | tf_op jit(solution)/shard_map/jit(_where)/select_n | solution.py:72
  140.7 2.0 fusion.40
  142.7 2.0 fusion.36
  144.7 1.2 convert_reduce_fusion.1
  145.9 3.5 %multiply_convert_fusion.1 = (bf16[864,384]{1,0:T(8,128)(2,1)S(1)}, bf16[864,384]{1,0:T(8,128)(2,1)S(1)}, bf16[864,384]{1,0:T(8,128)(2,1)}, bf16[864,384]{1,0:T(8,128)(2,1)S(1)}) fusion(f32[864,384]{1,0:T(8,128)S(1)} %fusion.40, f32[864]{0:T(1024)S(1)} %convert_reduce_fusion.1, f32[864,384]{1,0:T(8,128)S(1)} %fusion.36, ...), kind=kOutput, calls=%fused_computation.69 | convolution fusion | flops 1365258240 | bytes 10423680 | tf_op jit(solution)/shard_map/dot_general | solution.py:76
  149.8 1.1 fusion.79
  150.9 1.1 convolution_add_fusion
  152.1 2.2 fusion.10
  154.5 1.0 convert_reduce_fusion.3
  155.5 1.6 multiply_convert_fusion.4
  158.4 1.2 fusion.50
  160.5 0.9 copy-done.2
  161.9 1.6 collective-permute-done.1
  163.4 2.4 fusion.52
  165.8 4.4 %all-to-all-start.1 = ((bf16[1,4,72,1152]{3,2,0,1:T(8,128)(2,1)}), bf16[1,4,72,1152]{3,2,0,1:T(8,128)(2,1)}, u32[]{:S(2)}, u32[]{:S(2)}) async-start(bf16[1,4,72,1152]{3,2,0,1:T(8,128)(2,1)} %bitcast.20), calls=%async_computation.1 | async-start | bytes 1327104 | tf_op jit(solution)/shard_map/all_to_all | solution.py:115
  170.2 1.1 fusion.85
  171.7 1.1 convolution_add_fusion.1
  172.9 2.7 %fusion.12 = bf16[864,1152]{1,0:T(8,128)(2,1)S(1)} fusion(f32[864,1152]{1,0:T(8,128)} %collective-permute-done.6, f32[864,1]{1,0:T(8,128)S(1)} %copy-done.5, f32[864,1024]{1,0:T(8,128)S(1)} %convolution_add_fusion.1), kind=kLoop, calls=%fused_computation.16 | loop fusion | flops 4976640 | bytes 9514368 | tf_op jit(solution)/shard_map/convert_element_type | solution.py:114
  175.6 1.4 copy.81
  177.0 3.0 %all-to-all-done.1 = bf16[1,4,72,1152]{3,2,0,1:T(8,128)(2,1)} async-done(((bf16[1,4,72,1152]{3,2,0,1:T(8,128)(2,1)}), bf16[1,4,72,1152]{3,2,0,1:T(8,128)(2,1)}, u32[]{:S(2)}, u32[]{:S(2)}) %all-to-all-start.1) | async-done | bytes 663584 | tf_op jit(solution)/shard_map/all_to_all | solution.py:115
  180.1 4.4 %all-to-all-start.3 = ((bf16[3,4,72,1152]{3,2,0,1:T(8,128)(2,1)}), bf16[3,4,72,1152]{3,2,0,1:T(8,128)(2,1)}, u32[]{:S(2)}, u32[]{:S(2)}) async-start(bf16[3,4,72,1152]{3,2,0,1:T(8,128)(2,1)} %copy.81), calls=%async_computation.3 | async-start | bytes 3981312 | tf_op jit(solution)/shard_map/all_to_all | solution.py:115
  184.5 1.0 convert_reduce_fusion.2
  186.1 1.4 convolution_convert_fusion.2
  187.5 6.5 %fusion.25 = bf16[1,2048,384]{2,1,0:T(8,128)(2,1)} fusion(bf16[864,2048]{1,0:T(8,128)(2,1)} %copy-done.8, bf16[288,2048]{1,0:T(8,128)(2,1)} %copy-done.15, bf16[864,384]{1,0:T(8,128)(2,1)S(1)} %copy-done.11, bf16[288,384]{1,0:T(8,128)(2,1)} %copy-done.17), kind=kOutput, calls=%fused_computation.32 | convolution fusion | flops 1823932416 | bytes 7176192 | tf_op jit(solution)/shard_map/dot_general | solution.py:144
  194.0 3.9 %fusion.26 = bf16[1,2048,384]{2,1,0:T(8,128)(2,1)} fusion(bf16[864,2048]{1,0:T(8,128)(2,1)S(1)} %copy-done.9, bf16[288,2048]{1,0:T(8,128)(2,1)S(1)} %copy-done.16, bf16[864,384]{1,0:T(8,128)(2,1)S(1)} %get-tuple-element.42, bf16[288,384]{1,0:T(8,128)(2,1)S(1)} %get-tuple-element.48), kind=kOutput, calls=%fused_computation.33 | convolution fusion | flops 1823932416 | bytes 7176192 | tf_op jit(solution)/shard_map/dot_general | solution.py:140
  197.9 10.2 %all-to-all-done.3 = bf16[3,4,72,1152]{3,2,0,1:T(8,128)(2,1)} async-done(((bf16[3,4,72,1152]{3,2,0,1:T(8,128)(2,1)}), bf16[3,4,72,1152]{3,2,0,1:T(8,128)(2,1)}, u32[]{:S(2)}, u32[]{:S(2)}) %all-to-all-start.3) | async-done | bytes 1990688 | tf_op jit(solution)/shard_map/all_to_all | solution.py:115
  208.1 1.7 copy.82
  210.0 1.5 fusion.44
  211.5 1.1 select_reduce_fusion
  212.7 1.4 fusion.67
  214.2 3.3 %collective-permute-start.7 = (bf16[128,1152]{1,0:T(8,128)(2,1)S(1)}, bf16[128,1152]{1,0:T(8,128)(2,1)S(1)}, u32[]{:S(2)}, u32[]{:S(2)}) collective-permute-start(bf16[128,1152]{1,0:T(8,128)(2,1)S(1)} %get-tuple-element.51), channel_id=1, source_target_pairs={{0,24},{8,0},{16,8},{24,16},{1,25},{9,1},{17,9},{25,17},{2,26},{10... | collective-permute-start | bytes 884744 | tf_op jit(solution)/shard_map/ppermute | solution.py:131
  217.5 10.3 %collective-permute-start.9 = (bf16[128,1152]{1,0:T(8,128)(2,1)S(1)}, bf16[128,1152]{1,0:T(8,128)(2,1)S(1)}, u32[]{:S(2)}, u32[]{:S(2)}) collective-permute-start(bf16[128,1152]{1,0:T(8,128)(2,1)S(1)} %get-tuple-element.52), channel_id=1, source_target_pairs={{0,8},{8,16},{16,24},{24,0},{1,9},{9,17},{17,25},{25,1},{2,10},{10... | collective-permute-start | bytes 884744 | tf_op jit(solution)/shard_map/ppermute | solution.py:131
  227.8 3.8 %collective-permute-start.8 = (bf16[128,1152]{1,0:T(8,128)(2,1)S(1)}, bf16[128,1152]{1,0:T(8,128)(2,1)S(1)}, u32[]{:S(2)}, u32[]{:S(2)}) collective-permute-start(bf16[128,1152]{1,0:T(8,128)(2,1)S(1)} %get-tuple-element.53), channel_id=1, source_target_pairs={{0,16},{8,24},{16,0},{24,8},{1,17},{9,25},{17,1},{25,9},{2,18},{10... | collective-permute-start | bytes 884744 | tf_op jit(solution)/shard_map/ppermute | solution.py:131
  231.5 4.5 %fusion.22 = bf16[1,384,2048]{2,1,0:T(8,128)(2,1)} fusion(bf16[864,2048]{1,0:T(8,128)(2,1)S(1)} %copy-done.7, bf16[288,2048]{1,0:T(8,128)(2,1)S(1)} %copy-done.14, bf16[864,384]{1,0:T(8,128)(2,1)} %get-tuple-element.43, bf16[288,384]{1,0:T(8,128)(2,1)} %get-tuple-element.49), kind=kOutput, calls=%fused_computation.31 | convolution fusion | flops 1823932416 | bytes 7176192 | tf_op jit(solution)/shard_map/dot_general | solution.py:148
  236.0 9.3 %collective-permute-done.9 = bf16[128,1152]{1,0:T(8,128)(2,1)S(1)} collective-permute-done((bf16[128,1152]{1,0:T(8,128)(2,1)S(1)}, bf16[128,1152]{1,0:T(8,128)(2,1)S(1)}, u32[]{:S(2)}, u32[]{:S(2)}) %collective-permute-start.9) | collective-permute-done | bytes 294944 | tf_op jit(solution)/shard_map/ppermute | solution.py:131
  245.3 9.3 %collective-permute-done.8 = bf16[128,1152]{1,0:T(8,128)(2,1)S(1)} collective-permute-done((bf16[128,1152]{1,0:T(8,128)(2,1)S(1)}, bf16[128,1152]{1,0:T(8,128)(2,1)S(1)}, u32[]{:S(2)}, u32[]{:S(2)}) %collective-permute-start.8) | collective-permute-done | bytes 294944 | tf_op jit(solution)/shard_map/ppermute | solution.py:131
  254.8 0.7 slice.117
  255.5 0.7 copy.84
  (95 shorter events, 8.1 us)
Async XLA Ops:
  0.6 145.3 %copy-start = (bf16[1,2048,384]{2,1,0:T(8,128)(2,1)S(1)}, bf16[1,2048,384]{2,1,0:T(8,128)(2,1)}, u32[]{:S(2)}) copy-start(bf16[1,2048,384]{2,1,0:T(8,128)(2,1)} %param.11) | copy-start | bytes 4718596
  0.6 3.5 %copy-start.22 = (bf16[128,8]{0,1:T(8,128)(2,1)S(1)}, bf16[128,8]{0,1:T(8,128)(2,1)}, u32[]{:S(2)}) copy-start(bf16[128,8]{0,1:T(8,128)(2,1)} %param.10) | copy-start | bytes 6148
  5.3 41.6 %collective-permute-start.3 = (bf16[128,2176]{0,1:T(8,128)(2,1)}, bf16[128,2176]{0,1:T(8,128)(2,1)S(1)}, u32[]{:S(2)}, u32[]{:S(2)}) collective-permute-start(bf16[128,2176]{0,1:T(8,128)(2,1)} %get-tuple-element.55), channel_id=1, source_target_pairs={{0,16},{8,24},{16,0},{24,8},{1,17},{9,25},{17,1},{25,9},{2,18},{10... | collective-permute-start | bytes 1671176 | tf_op jit(solution)/shard_map/ppermute | solution.py:25
  9.3 37.6 %collective-permute-start.2 = (bf16[128,2176]{0,1:T(8,128)(2,1)}, bf16[128,2176]{0,1:T(8,128)(2,1)S(1)}, u32[]{:S(2)}, u32[]{:S(2)}) collective-permute-start(bf16[128,2176]{0,1:T(8,128)(2,1)} %get-tuple-element.55), channel_id=1, source_target_pairs={{0,8},{8,16},{16,24},{24,0},{1,9},{9,17},{17,25},{25,1},{2,10},{10... | collective-permute-start | bytes 1671176 | tf_op jit(solution)/shard_map/ppermute | solution.py:25
  10.9 36.7 %collective-permute-start.4 = (bf16[128,2176]{0,1:T(8,128)(2,1)}, bf16[128,2176]{0,1:T(8,128)(2,1)S(1)}, u32[]{:S(2)}, u32[]{:S(2)}) collective-permute-start(bf16[128,2176]{0,1:T(8,128)(2,1)} %get-tuple-element.55), channel_id=1, source_target_pairs={{0,24},{8,0},{16,8},{24,16},{1,25},{9,1},{17,9},{25,17},{2,26},{10... | collective-permute-start | bytes 1671176 | tf_op jit(solution)/shard_map/ppermute | solution.py:25
  51.6 4.4 %copy-start.18 = (bf16[3,288,128]{2,1,0:T(8,128)(2,1)}, bf16[3,288,128]{2,1,0:T(8,128)(2,1)S(1)}, u32[]{:S(2)}) copy-start(bf16[3,288,128]{2,1,0:T(8,128)(2,1)S(1)} %fusion.27) | copy-start | bytes 663556
  58.5 4.9 %copy-start.12 = (bf16[1,128,2176]{1,2,0:T(8,128)(2,1)S(1)}, bf16[1,128,2176]{1,2,0:T(8,128)(2,1)}, u32[]{:S(2)}) copy-start(bf16[1,128,2176]{1,2,0:T(8,128)(2,1)} %get-tuple-element.54) | copy-start | bytes 1671172
  58.5 45.8 %all-to-all-start.2 = ((bf16[3,4,72,2176]{3,2,0,1:T(8,128)(2,1)}), bf16[3,4,72,2176]{3,2,0,1:T(8,128)(2,1)}, u32[]{:S(2)}, u32[]{:S(2)}) async-start(bf16[3,4,72,2176]{3,2,0,1:T(8,128)(2,1)} %copy.78), calls=%async_computation.2 | async-start | bytes 7520256 | tf_op jit(solution)/shard_map/all_to_all | solution.py:67
  65.0 0.6 copy-start.20
  108.5 28.8 %collective-permute-start.5 = (bf16[864,2176]{1,0:T(8,128)(2,1)}, bf16[864,2176]{1,0:T(8,128)(2,1)}, u32[]{:S(2)}, u32[]{:S(2)}) collective-permute-start(bf16[864,2176]{1,0:T(8,128)(2,1)} %bitcast.32), channel_id=1, source_target_pairs={{0,1},{1,0},{2,3},{3,2},{4,5},{5,4},{6,7},{7,6},{8,9},{9,8},{10,11... | collective-permute-start | bytes 11280392 | tf_op jit(solution)/shard_map/ppermute | solution.py:70
  129.7 3.1 %collective-permute-start = (bf16[288,2176]{1,0:T(8,128)(2,1)S(1)}, bf16[288,2176]{1,0:T(8,128)(2,1)}, u32[]{:S(2)}, u32[]{:S(2)}) collective-permute-start(bf16[288,2176]{1,0:T(8,128)(2,1)S(1)} %bitcast.151), channel_id=1, source_target_pairs={{0,1},{1,0},{2,3},{3,2},{4,5},{5,4},{6,7},{7,6},{8,9},{9,8},{10,11... | collective-permute-start | bytes 3760136 | tf_op jit(solution)/shard_map/ppermute | solution.py:70
  129.7 4.6 %copy-start.23 = (bf16[1,384,2048]{2,1,0:T(8,128)(2,1)S(1)}, bf16[1,384,2048]{2,1,0:T(8,128)(2,1)}, u32[]{:S(2)}) copy-start(bf16[1,384,2048]{2,1,0:T(8,128)(2,1)} %param.13) | copy-start | bytes 4718596
  134.3 1.0 copy-start.13
  134.3 21.2 %copy-start.15 = (bf16[288,2048]{1,0:T(8,128)(2,1)}, bf16[288,2048]{1,0:T(8,128)(2,1)S(1)}, u32[]{:S(2)}) copy-start(bf16[288,2048]{1,0:T(8,128)(2,1)S(1)} %get-tuple-element.45) | copy-start | bytes 3538948
  134.3 2.2 copy-start.1
  140.7 2.0 copy-start.6
  140.7 5.2 %copy-start.8 = (bf16[864,2048]{1,0:T(8,128)(2,1)}, bf16[864,2048]{1,0:T(8,128)(2,1)S(1)}, u32[]{:S(2)}) copy-start(bf16[864,2048]{1,0:T(8,128)(2,1)S(1)} %get-tuple-element.39) | copy-start | bytes 10616836
  149.4 1.5 copy-start.10
  149.8 2.3 copy-start.4
  154.3 18.5 %collective-permute-start.6 = (f32[864,1152]{1,0:T(8,128)}, f32[864,1152]{1,0:T(8,128)}, u32[]{:S(2)}, u32[]{:S(2)}) collective-permute-start(f32[864,1152]{1,0:T(8,128)} %fusion.10), channel_id=1, source_target_pairs={{0,1},{1,0},{2,3},{3,2},{4,5},{5,4},{6,7},{7,6},{8,9},{9,8},{10,11... | collective-permute-start | bytes 11943944 | tf_op jit(solution)/shard_map/ppermute | solution.py:113
  157.1 3.3 %copy-start.17 = (bf16[288,384]{1,0:T(8,128)(2,1)}, bf16[288,384]{1,0:T(8,128)(2,1)S(1)}, u32[]{:S(2)}) copy-start(bf16[288,384]{1,0:T(8,128)(2,1)S(1)} %get-tuple-element.47) | copy-start | bytes 663556
  159.6 3.8 %collective-permute-start.1 = (f32[288,1152]{1,0:T(8,128)}, f32[288,1152]{1,0:T(8,128)}, u32[]{:S(2)}, u32[]{:S(2)}) collective-permute-start(f32[288,1152]{1,0:T(8,128)} %fusion.50), channel_id=1, source_target_pairs={{0,1},{1,0},{2,3},{3,2},{4,5},{5,4},{6,7},{7,6},{8,9},{9,8},{10,11... | collective-permute-start | bytes 3981320 | tf_op jit(solution)/shard_map/ppermute | solution.py:113
  159.9 1.4 copy-start.2
  165.8 14.3 %all-to-all-start.1 = ((bf16[1,4,72,1152]{3,2,0,1:T(8,128)(2,1)}), bf16[1,4,72,1152]{3,2,0,1:T(8,128)(2,1)}, u32[]{:S(2)}, u32[]{:S(2)}) async-start(bf16[1,4,72,1152]{3,2,0,1:T(8,128)(2,1)} %bitcast.20), calls=%async_computation.1 | async-start | bytes 1327104 | tf_op jit(solution)/shard_map/all_to_all | solution.py:115
  170.2 1.4 copy-start.3
  170.2 1.6 copy-start.11
  171.7 1.1 copy-start.5
  177.0 9.0 %copy-start.21 = (bf16[288,128]{1,0:T(8,128)(2,1)S(1)}, bf16[288,128]{1,0:T(8,128)(2,1)}, u32[]{:S(2)}) copy-start(bf16[288,128]{1,0:T(8,128)(2,1)} %copy-done.20) | copy-start | bytes 221188
  180.1 28.0 %all-to-all-start.3 = ((bf16[3,4,72,1152]{3,2,0,1:T(8,128)(2,1)}), bf16[3,4,72,1152]{3,2,0,1:T(8,128)(2,1)}, u32[]{:S(2)}, u32[]{:S(2)}) async-start(bf16[3,4,72,1152]{3,2,0,1:T(8,128)(2,1)} %copy.81), calls=%async_computation.3 | async-start | bytes 3981312 | tf_op jit(solution)/shard_map/all_to_all | solution.py:115
  187.5 6.5 %copy-start.9 = (bf16[864,2048]{1,0:T(8,128)(2,1)S(1)}, bf16[864,2048]{1,0:T(8,128)(2,1)}, u32[]{:S(2)}) copy-start(bf16[864,2048]{1,0:T(8,128)(2,1)} %copy-done.8) | copy-start | bytes 10616836
  187.5 6.5 %copy-start.16 = (bf16[288,2048]{1,0:T(8,128)(2,1)S(1)}, bf16[288,2048]{1,0:T(8,128)(2,1)}, u32[]{:S(2)}) copy-start(bf16[288,2048]{1,0:T(8,128)(2,1)} %copy-done.15) | copy-start | bytes 3538948
  197.9 12.1 %copy-start.19 = (bf16[3,288,128]{2,1,0:T(8,128)(2,1)S(1)}, bf16[3,288,128]{2,1,0:T(8,128)(2,1)}, u32[]{:S(2)}) copy-start(bf16[3,288,128]{2,1,0:T(8,128)(2,1)} %copy-done.18) | copy-start | bytes 663556
  210.0 21.5 %copy-start.14 = (bf16[288,2048]{1,0:T(8,128)(2,1)S(1)}, bf16[288,2048]{1,0:T(8,128)(2,1)}, u32[]{:S(2)}) copy-start(bf16[288,2048]{1,0:T(8,128)(2,1)} %copy-done.13) | copy-start | bytes 3538948
  212.7 18.8 %copy-start.7 = (bf16[864,2048]{1,0:T(8,128)(2,1)S(1)}, bf16[864,2048]{1,0:T(8,128)(2,1)}, u32[]{:S(2)}) copy-start(bf16[864,2048]{1,0:T(8,128)(2,1)} %copy-done.6) | copy-start | bytes 10616836
  214.2 21.9 %collective-permute-start.7 = (bf16[128,1152]{1,0:T(8,128)(2,1)S(1)}, bf16[128,1152]{1,0:T(8,128)(2,1)S(1)}, u32[]{:S(2)}, u32[]{:S(2)}) collective-permute-start(bf16[128,1152]{1,0:T(8,128)(2,1)S(1)} %get-tuple-element.51), channel_id=1, source_target_pairs={{0,24},{8,0},{16,8},{24,16},{1,25},{9,1},{17,9},{25,17},{2,26},{10... | collective-permute-start | bytes 884744 | tf_op jit(solution)/shard_map/ppermute | solution.py:131
  217.5 27.8 %collective-permute-start.9 = (bf16[128,1152]{1,0:T(8,128)(2,1)S(1)}, bf16[128,1152]{1,0:T(8,128)(2,1)S(1)}, u32[]{:S(2)}, u32[]{:S(2)}) collective-permute-start(bf16[128,1152]{1,0:T(8,128)(2,1)S(1)} %get-tuple-element.52), channel_id=1, source_target_pairs={{0,8},{8,16},{16,24},{24,0},{1,9},{9,17},{17,25},{25,1},{2,10},{10... | collective-permute-start | bytes 884744 | tf_op jit(solution)/shard_map/ppermute | solution.py:131
  227.8 26.9 %collective-permute-start.8 = (bf16[128,1152]{1,0:T(8,128)(2,1)S(1)}, bf16[128,1152]{1,0:T(8,128)(2,1)S(1)}, u32[]{:S(2)}, u32[]{:S(2)}) collective-permute-start(bf16[128,1152]{1,0:T(8,128)(2,1)S(1)} %get-tuple-element.53), channel_id=1, source_target_pairs={{0,16},{8,24},{16,0},{24,8},{1,17},{9,25},{17,1},{25,9},{2,18},{10... | collective-permute-start | bytes 884744 | tf_op jit(solution)/shard_map/ppermute | solution.py:131

commit v7 on v6

--- a/solution.py
+++ b/solution.py
@@ -95,23 +95,19 @@
         rows_pre.append(pre_grad)
         rows_up.append(up_grad)
         rows_w.append(weighted)
-        gate_col = jnp.pad(gate_terms[:, None], ((0, 0), (0, lanes - 1)))
         half = features // 2
-
-        def hidden_part(c):
-            w_g = lax.dynamic_slice_in_dim(weight_g, c * half, half, axis=0)
-            w_u = lax.dynamic_slice_in_dim(weight_u, c * half, half, axis=0)
-            return jnp.concatenate([
-                lax.dot_general(
-                    pre_grad, w_g, (((1,), (1,)), ((), ())), preferred_element_type=jnp.float32
-                ) + lax.dot_general(
-                    up_grad, w_u, (((1,), (1,)), ((), ())), preferred_element_type=jnp.float32
-                ),
-                gate_col,
-            ], axis=1)
-
-        theirs = lax.ppermute(hidden_part(1 - core), "tensor", [(0, 1), (1, 0)])
-        ret = (hidden_part(core) + theirs).astype(jnp.bfloat16)
+        partial_value = lax.dot_general(
+            pre_grad, weight_g, (((1,), (1,)), ((), ())), preferred_element_type=jnp.float32
+        ) + lax.dot_general(
+            up_grad, weight_u, (((1,), (1,)), ((), ())), preferred_element_type=jnp.float32
+        )
+        routed_grad = lax.psum_scatter(
+            partial_value.astype(jnp.bfloat16), "tensor", scatter_dimension=1, tiled=True
+        )
+        slot_gate = lax.psum(gate_terms, "tensor").astype(jnp.bfloat16)
+        ret = jnp.concatenate(
+            [routed_grad, jnp.pad(slot_gate[:, None], ((0, 0), (0, lanes - 1)))], axis=1
+        )
         back = lax.all_to_all(
             ret.reshape(n_mem, n_ex, capacity, half + lanes), "expert", split_axis=1, concat_axis=1, tiled=True
         ).reshape(n_mem, block_slots, half + lanes)

time: 257 us -> 264 us (1.027)
  waiting for transfers between devices: 109 us -> 130 us
  blocking collectives: 19.9 us -> 2.49 us
  between operations: 1.29 us -> 14.7 us
  other arithmetic: 28.6 us -> 23.1 us
  starting transfers between devices: 39.4 us -> 35.9 us
    all_to_all x1 -> x0, blocking collectives: 19.9 us -> none  [on_device(): lax.all_to_all(send.reshape(n_mem, n_ex, capacity, features + lanes), 'ex...]
    reduce_scatter x0 -> x2, waiting for transfers between devices: none -> 12 us  [on_device(): lax.psum_scatter(partial_value.astype(jnp.bfloat16), 'tensor', scatter_di...]
    all_to_all x1 -> x2, waiting for transfers between devices: 38.2 us -> 47.3 us  [on_device(): lax.all_to_all(send.reshape(n_mem, n_ex, capacity, features + lanes), 'ex...]
    ppermute x3, starting transfers between devices: 17.3 us -> 11.1 us  [on_device(): part = lax.ppermute(part, 'dp', [(i, (i - s) % n_dp) for i in range(n_dp)])]
    convert_element_type x2 -> x0, other arithmetic: 5.1 us -> none  [on_device(): ret = (hidden_part(core) + theirs).astype(jnp.bfloat16)]
    ppermute x3, waiting for transfers between devices: 18.6 us -> 22.8 us  [on_device(): part = lax.ppermute(part, 'dp', [(i, (i - s) % n_dp) for i in range(n_dp)])]
    all_to_all x1 -> x2, starting transfers between devices: 4.9 us -> 8.43 us  [on_device(): lax.all_to_all(send.reshape(n_mem, n_ex, capacity, features + lanes), 'ex...]
    all_to_all x2, waiting for transfers between devices: 13.3 us -> 10.2 us  [on_device(): lax.all_to_all(ret.reshape(n_mem, n_ex, capacity, half + lanes), 'expert'...]
  transfers between devices with their start and end apart: 13 -> 14, of which waited for: 9 -> 10; matrix products, arithmetic and copies ran while one was open for 15% -> 21% of each run, Pallas kernels for 0% -> 0%
where the time goes in v7:
time: 264 us; the launch traced here: 263 us
  waiting for transfers between devices  130 us (49%)
  matrix products  38.3 us (15%)
  starting transfers between devices  35.9 us (14%)
  other arithmetic  23.1 us (9%)
  local copies, waits for them, and re-layouts  18.8 us (7%)
  between operations  14.7 us (6%)
    all_to_all x2, waiting for transfers between devices, on_device(): lax.all_to_all(send.reshape(n_mem, n_ex, capacity, features + lanes), 'ex...  47.3 us
    ppermute x3, waiting for transfers between devices, on_device(): lax.ppermute(ext, 'dp', [(i, (i + s) % n_dp) for i in range(n_dp)])  34.5 us
    ppermute x3, waiting for transfers between devices, on_device(): part = lax.ppermute(part, 'dp', [(i, (i - s) % n_dp) for i in range(n_dp)])  22.8 us
    reduce_scatter x2, waiting for transfers between devices, on_device(): lax.psum_scatter(partial_value.astype(jnp.bfloat16), 'tensor', scatter_di...  12 us
    ppermute x3, starting transfers between devices, on_device(): part = lax.ppermute(part, 'dp', [(i, (i - s) % n_dp) for i in range(n_dp)])  11.1 us
    all_to_all x2, waiting for transfers between devices, on_device(): lax.all_to_all(ret.reshape(n_mem, n_ex, capacity, half + lanes), 'expert'...  10.2 us
    all_to_all x2, starting transfers between devices, on_device(): lax.all_to_all(send.reshape(n_mem, n_ex, capacity, features + lanes), 'ex...  8.43 us
    all_to_all x2, starting transfers between devices, on_device(): lax.all_to_all(ret.reshape(n_mem, n_ex, capacity, half + lanes), 'expert'...  8.25 us
  transfers between devices with their start and end apart: 14, of which 10 were waited for; matrix products, arithmetic and copies ran while one was open for 21% of the time, Pallas kernels for 0%

profile of v7, /device:TPU:0, one launch (start us, length us, event | category | flops | bytes accessed | tf_op | source)
XLA Modules:
  0.0 263.0 jit_solution(9537330384449886724)
XLA Ops:
  7.2 0.8 convert_element_type.203
  8.0 1.3 copy.64
  9.3 1.3 copy.65
  10.7 1.1 fusion.96
  11.8 4.0 %collective-permute-start.2 = (bf16[128,2176]{0,1:T(8,128)(2,1)}, bf16[128,2176]{0,1:T(8,128)(2,1)S(1)}, u32[]{:S(2)}, u32[]{:S(2)}) collective-permute-start(bf16[128,2176]{0,1:T(8,128)(2,1)} %get-tuple-element.57), channel_id=1, source_target_pairs={{0,16},{8,24},{16,0},{24,8},{1,17},{9,25},{17,1},{25,9},{2,18},{10... | collective-permute-start | bytes 1671176 | tf_op jit(solution)/shard_map/ppermute | solution.py:25
  15.8 1.6 collective-permute-start.1
  17.4 2.2 collective-permute-start.3
  19.7 33.8 %collective-permute-done.2 = bf16[128,2176]{0,1:T(8,128)(2,1)S(1)} collective-permute-done((bf16[128,2176]{0,1:T(8,128)(2,1)}, bf16[128,2176]{0,1:T(8,128)(2,1)S(1)}, u32[]{:S(2)}, u32[]{:S(2)}) %collective-permute-start.2) | collective-permute-done | bytes 557088 | tf_op jit(solution)/shard_map/ppermute | solution.py:25
  53.4 0.7 collective-permute-done.3
  54.1 1.4 pad_maximum_fusion.11
  55.8 0.5 fusion.63
  56.6 1.6 fusion.26
  58.2 1.6 select_reduce_fusion.1
  60.1 2.5 convolution_convert_fusion
  62.9 2.1 copy.78
  65.0 4.9 %all-to-all-start.2 = ((bf16[3,4,72,2176]{3,2,0,1:T(8,128)(2,1)}), bf16[3,4,72,2176]{3,2,0,1:T(8,128)(2,1)}, u32[]{:S(2)}, u32[]{:S(2)}) async-start(bf16[3,4,72,2176]{3,2,0,1:T(8,128)(2,1)} %copy.78), calls=%async_computation.3 | async-start | bytes 7520256 | tf_op jit(solution)/shard_map/all_to_all | solution.py:67
  70.2 0.8 fusion.68
  71.1 1.1 select_reduce_fusion.3
  72.7 0.5 convolution_convert_fusion.1
  73.2 1.2 pad_maximum_fusion.12
  74.4 36.5 %all-to-all-done.2 = bf16[3,4,72,2176]{3,2,0,1:T(8,128)(2,1)} async-done(((bf16[3,4,72,2176]{3,2,0,1:T(8,128)(2,1)}), bf16[3,4,72,2176]{3,2,0,1:T(8,128)(2,1)}, u32[]{:S(2)}, u32[]{:S(2)}) %all-to-all-start.2) | async-done | bytes 3760160 | tf_op jit(solution)/shard_map/all_to_all | solution.py:67
  110.9 3.5 %all-to-all-start = ((bf16[1,4,72,2176]{3,2,0,1:T(8,128)(2,1)}), bf16[1,4,72,2176]{3,2,0,1:T(8,128)(2,1)S(1)}, u32[]{:S(2)}, u32[]{:S(2)}) async-start(bf16[1,4,72,2176]{3,2,0,1:T(8,128)(2,1)} %pad_maximum_fusion.12), calls=%async_computation | async-start | bytes 2506752 | tf_op jit(solution)/shard_map/all_to_all | solution.py:67
  114.6 4.2 %copy.79 = bf16[3,4,72,2176]{3,2,1,0:T(8,128)(2,1)} copy(bf16[3,4,72,2176]{3,2,0,1:T(8,128)(2,1)} %all-to-all-done.2) | data formatting | bytes 7520256 | tf_op jit(solution)/shard_map/all_to_all | solution.py:67
  118.8 10.8 %all-to-all-done = bf16[1,4,72,2176]{3,2,0,1:T(8,128)(2,1)S(1)} async-done(((bf16[1,4,72,2176]{3,2,0,1:T(8,128)(2,1)}), bf16[1,4,72,2176]{3,2,0,1:T(8,128)(2,1)S(1)}, u32[]{:S(2)}, u32[]{:S(2)}) %all-to-all-start) | async-done | bytes 1253408 | tf_op jit(solution)/shard_map/all_to_all | solution.py:67
  129.7 3.0 %collective-permute-done = bf16[288,2176]{1,0:T(8,128)(2,1)S(1)} collective-permute-done((bf16[288,2176]{1,0:T(8,128)(2,1)S(1)}, bf16[288,2176]{1,0:T(8,128)(2,1)S(1)}, u32[]{:S(2)}, u32[]{:S(2)}) %collective-permute-start) | collective-permute-done | bytes 1253408 | tf_op jit(solution)/shard_map/ppermute | solution.py:70
  132.9 1.9 copy-done.25
  134.8 0.8 fusion.47
  135.6 0.6 copy-done.1
  136.2 0.8 fusion.43
  137.0 1.7 multiply_convert_fusion.4
  138.7 0.8 fusion.35
  139.6 1.8 fusion.19
  141.5 3.4 %broadcast_select_fusion = (bf16[864,2048]{1,0:T(8,128)(2,1)S(1)}, bf16[864,2048]{1,0:T(8,128)(2,1)S(1)}) fusion(pred[]{:T(512)S(6)} %eq.88, bf16[864,2176]{1,0:T(8,128)(2,1)} %bitcast.28, bf16[864,2176]{1,0:T(8,128)(2,1)} %collective-permute-done.4), kind=kLoop, calls=%fused_computation.19 | loop fusion | flops 3538944 | bytes 14155777 | tf_op jit(solution)/shard_map/jit(_where)/select_n | solution.py:72
  145.0 2.0 fusion.45
  147.0 1.7 convert_reduce_fusion.1
  148.8 2.0 fusion.40
  150.8 3.7 %multiply_convert_fusion.1 = (bf16[864,384]{1,0:T(8,128)(2,1)S(1)}, bf16[864,384]{1,0:T(8,128)(2,1)S(1)}, bf16[864,384]{1,0:T(8,128)(2,1)}, bf16[864,384]{1,0:T(8,128)(2,1)}) fusion(f32[864,384]{1,0:T(8,128)S(1)} %fusion.45, f32[864]{0:T(1024)S(1)} %convert_reduce_fusion.1, f32[864,384]{1,0:T(8,128)S(1)} %fusion.40, ...), kind=kOutput, calls=%fused_computation.66 | convolution fusion | flops 1365258240 | bytes 10423680 | tf_op jit(solution)/shard_map/dot_general | solution.py:76
  154.4 2.0 fusion.31
  156.5 3.8 %add_convert_fusion = bf16[864,2048]{1,0:T(8,128)(2,1)} fusion(f32[864,2048]{1,0:T(8,128)S(1)} %fusion.31, bf16[864,384]{1,0:T(8,128)(2,1)S(1)} %get-tuple-element.43, bf16[1,2048,384]{2,1,0:T(8,128)(2,1)S(1)} %copy-done.1), kind=kOutput, calls=%fused_computation.2 | convolution fusion | flops 1362493440 | bytes 12853248 | tf_op jit(solution)/shard_map/dot_general | solution.py:101
  160.3 1.0 copy-done.21
  161.3 1.1 fusion.82
  162.4 1.3 fusion.52
  163.7 2.5 all-reduce.7
  166.4 2.0 fusion.79
  168.3 3.5 %all-to-all-start.1 = ((bf16[1,4,72,1152]{3,2,0,1:T(8,128)(2,1)}), bf16[1,4,72,1152]{3,2,0,1:T(8,128)(2,1)S(1)}, u32[]{:S(2)}, u32[]{:S(2)}) async-start(bf16[1,4,72,1152]{3,2,0,1:T(8,128)(2,1)} %bitcast.16), calls=%async_computation.2 | async-start | bytes 1327104 | tf_op jit(solution)/shard_map/all_to_all | solution.py:111
  172.0 12.0 %reduce-scatter.5.cloned.1.call-done = bf16[864,1024]{1,0:T(8,128)(2,1)} async-done(((bf16[864,2048]{1,0:T(8,128)(2,1)}), bf16[864,1024]{1,0:T(8,128)(2,1)}) %reduce-scatter.5.cloned.1.call-update) | async-done | bytes 1769488 | tf_op jit(solution)/shard_map/reduce_scatter | solution.py:104
  184.0 1.7 fusion.25
  185.7 1.4 copy.81
  187.1 4.8 %all-to-all-start.3 = ((bf16[3,4,72,1152]{3,2,0,1:T(8,128)(2,1)}), bf16[3,4,72,1152]{3,2,0,1:T(8,128)(2,1)}, u32[]{:S(2)}, u32[]{:S(2)}) async-start(bf16[3,4,72,1152]{3,2,0,1:T(8,128)(2,1)} %copy.81), calls=%async_computation.5 | async-start | bytes 3981312 | tf_op jit(solution)/shard_map/all_to_all | solution.py:111
  191.9 5.8 %fusion.20 = bf16[1,384,2048]{2,1,0:T(8,128)(2,1)} fusion(bf16[864,2048]{1,0:T(8,128)(2,1)} %copy-done.4, bf16[288,2048]{1,0:T(8,128)(2,1)S(1)} %copy-done.11, bf16[864,384]{1,0:T(8,128)(2,1)} %get-tuple-element.45, bf16[288,384]{1,0:T(8,128)(2,1)} %get-tuple-element.51), kind=kOutput, calls=%fused_computation.30 | convolution fusion | flops 1823932416 | bytes 7176192 | tf_op jit(solution)/shard_map/dot_general | solution.py:144
  197.8 3.9 %fusion.23 = bf16[1,2048,384]{2,1,0:T(8,128)(2,1)} fusion(bf16[864,2048]{1,0:T(8,128)(2,1)S(1)} %copy-done.3, bf16[288,2048]{1,0:T(8,128)(2,1)S(1)} %copy-done.9, bf16[864,384]{1,0:T(8,128)(2,1)S(1)} %copy-done.19, bf16[288,384]{1,0:T(8,128)(2,1)S(1)} %copy-done.23), kind=kOutput, calls=%fused_computation.31 | convolution fusion | flops 1823932416 | bytes 7176192 | tf_op jit(solution)/shard_map/dot_general | solution.py:140
  201.7 3.9 %fusion.24 = bf16[1,2048,384]{2,1,0:T(8,128)(2,1)} fusion(bf16[864,2048]{1,0:T(8,128)(2,1)S(1)} %copy-done.3, bf16[288,2048]{1,0:T(8,128)(2,1)S(1)} %copy-done.9, bf16[864,384]{1,0:T(8,128)(2,1)S(1)} %copy-done.13, bf16[288,384]{1,0:T(8,128)(2,1)S(1)} %copy-done.17), kind=kOutput, calls=%fused_computation.32 | convolution fusion | flops 1823932416 | bytes 7176192 | tf_op jit(solution)/shard_map/dot_general | solution.py:136
  206.3 10.2 %all-to-all-done.3 = bf16[3,4,72,1152]{3,2,0,1:T(8,128)(2,1)} async-done(((bf16[3,4,72,1152]{3,2,0,1:T(8,128)(2,1)}), bf16[3,4,72,1152]{3,2,0,1:T(8,128)(2,1)}, u32[]{:S(2)}, u32[]{:S(2)}) %all-to-all-start.3) | async-done | bytes 1990688 | tf_op jit(solution)/shard_map/all_to_all | solution.py:111
  216.4 1.7 copy.82
  218.3 0.6 fusion.49
  218.9 1.1 select_reduce_fusion
  220.4 3.4 %collective-permute-start.5 = (bf16[128,1152]{1,0:T(8,128)(2,1)S(1)}, bf16[128,1152]{1,0:T(8,128)(2,1)S(1)}, u32[]{:S(2)}, u32[]{:S(2)}) collective-permute-start(bf16[128,1152]{1,0:T(8,128)(2,1)S(1)} %get-tuple-element.53), channel_id=1, source_target_pairs={{0,24},{8,0},{16,8},{24,16},{1,25},{9,1},{17,9},{25,17},{2,26},{10... | collective-permute-start | bytes 884744 | tf_op jit(solution)/shard_map/ppermute | solution.py:127
  223.8 4.1 %collective-permute-start.7 = (bf16[128,1152]{1,0:T(8,128)(2,1)S(1)}, bf16[128,1152]{1,0:T(8,128)(2,1)S(1)}, u32[]{:S(2)}, u32[]{:S(2)}) collective-permute-start(bf16[128,1152]{1,0:T(8,128)(2,1)S(1)} %get-tuple-element.54), channel_id=1, source_target_pairs={{0,8},{8,16},{16,24},{24,0},{1,9},{9,17},{17,25},{25,1},{2,10},{10... | collective-permute-start | bytes 884744 | tf_op jit(solution)/shard_map/ppermute | solution.py:127
  227.8 3.6 %collective-permute-start.6 = (bf16[128,1152]{1,0:T(8,128)(2,1)S(1)}, bf16[128,1152]{1,0:T(8,128)(2,1)S(1)}, u32[]{:S(2)}, u32[]{:S(2)}) collective-permute-start(bf16[128,1152]{1,0:T(8,128)(2,1)S(1)} %get-tuple-element.55), channel_id=1, source_target_pairs={{0,16},{8,24},{16,0},{24,8},{1,17},{9,25},{17,1},{25,9},{2,18},{10... | collective-permute-start | bytes 884744 | tf_op jit(solution)/shard_map/ppermute | solution.py:127
  231.8 2.3 collective-permute-done.5
  234.0 11.2 %collective-permute-done.7 = bf16[128,1152]{1,0:T(8,128)(2,1)S(1)} collective-permute-done((bf16[128,1152]{1,0:T(8,128)(2,1)S(1)}, bf16[128,1152]{1,0:T(8,128)(2,1)S(1)}, u32[]{:S(2)}, u32[]{:S(2)}) %collective-permute-start.7) | collective-permute-done | bytes 294944 | tf_op jit(solution)/shard_map/ppermute | solution.py:127
  245.2 9.3 %collective-permute-done.6 = bf16[128,1152]{1,0:T(8,128)(2,1)S(1)} collective-permute-done((bf16[128,1152]{1,0:T(8,128)(2,1)S(1)}, bf16[128,1152]{1,0:T(8,128)(2,1)S(1)}, u32[]{:S(2)}, u32[]{:S(2)}) %collective-permute-start.6) | collective-permute-done | bytes 294944 | tf_op jit(solution)/shard_map/ppermute | solution.py:127
  254.7 0.7 slice.117
  255.5 0.7 copy.84
  (99 shorter events, 4.7 us)
Async XLA Ops:
  7.2 129.8 %copy-start = (bf16[1,2048,384]{2,1,0:T(8,128)(2,1)S(1)}, bf16[1,2048,384]{2,1,0:T(8,128)(2,1)}, u32[]{:S(2)}) copy-start(bf16[1,2048,384]{2,1,0:T(8,128)(2,1)} %param.11) | copy-start | bytes 4718596
  7.2 3.5 %copy-start.24 = (bf16[128,8]{0,1:T(8,128)(2,1)S(1)}, bf16[128,8]{0,1:T(8,128)(2,1)}, u32[]{:S(2)}) copy-start(bf16[128,8]{0,1:T(8,128)(2,1)} %param.10) | copy-start | bytes 6148
  11.8 41.6 %collective-permute-start.2 = (bf16[128,2176]{0,1:T(8,128)(2,1)}, bf16[128,2176]{0,1:T(8,128)(2,1)S(1)}, u32[]{:S(2)}, u32[]{:S(2)}) collective-permute-start(bf16[128,2176]{0,1:T(8,128)(2,1)} %get-tuple-element.57), channel_id=1, source_target_pairs={{0,16},{8,24},{16,0},{24,8},{1,17},{9,25},{17,1},{25,9},{2,18},{10... | collective-permute-start | bytes 1671176 | tf_op jit(solution)/shard_map/ppermute | solution.py:25
  15.8 37.6 %collective-permute-start.1 = (bf16[128,2176]{0,1:T(8,128)(2,1)}, bf16[128,2176]{0,1:T(8,128)(2,1)S(1)}, u32[]{:S(2)}, u32[]{:S(2)}) collective-permute-start(bf16[128,2176]{0,1:T(8,128)(2,1)} %get-tuple-element.57), channel_id=1, source_target_pairs={{0,8},{8,16},{16,24},{24,0},{1,9},{9,17},{17,25},{25,1},{2,10},{10... | collective-permute-start | bytes 1671176 | tf_op jit(solution)/shard_map/ppermute | solution.py:25
  17.4 36.7 %collective-permute-start.3 = (bf16[128,2176]{0,1:T(8,128)(2,1)}, bf16[128,2176]{0,1:T(8,128)(2,1)S(1)}, u32[]{:S(2)}, u32[]{:S(2)}) collective-permute-start(bf16[128,2176]{0,1:T(8,128)(2,1)} %get-tuple-element.57), channel_id=1, source_target_pairs={{0,24},{8,0},{16,8},{24,16},{1,25},{9,1},{17,9},{25,17},{2,26},{10... | collective-permute-start | bytes 1671176 | tf_op jit(solution)/shard_map/ppermute | solution.py:25
  58.2 4.4 %copy-start.14 = (bf16[3,288,128]{2,1,0:T(8,128)(2,1)}, bf16[3,288,128]{2,1,0:T(8,128)(2,1)S(1)}, u32[]{:S(2)}) copy-start(bf16[3,288,128]{2,1,0:T(8,128)(2,1)S(1)} %fusion.26) | copy-start | bytes 663556
  65.0 4.9 %copy-start.5 = (bf16[1,128,2176]{1,2,0:T(8,128)(2,1)S(1)}, bf16[1,128,2176]{1,2,0:T(8,128)(2,1)}, u32[]{:S(2)}) copy-start(bf16[1,128,2176]{1,2,0:T(8,128)(2,1)} %get-tuple-element.56) | copy-start | bytes 1671172
  65.0 45.8 %all-to-all-start.2 = ((bf16[3,4,72,2176]{3,2,0,1:T(8,128)(2,1)}), bf16[3,4,72,2176]{3,2,0,1:T(8,128)(2,1)}, u32[]{:S(2)}, u32[]{:S(2)}) async-start(bf16[3,4,72,2176]{3,2,0,1:T(8,128)(2,1)} %copy.78), calls=%async_computation.3 | async-start | bytes 7520256 | tf_op jit(solution)/shard_map/all_to_all | solution.py:67
  110.9 18.8 %all-to-all-start = ((bf16[1,4,72,2176]{3,2,0,1:T(8,128)(2,1)}), bf16[1,4,72,2176]{3,2,0,1:T(8,128)(2,1)S(1)}, u32[]{:S(2)}, u32[]{:S(2)}) async-start(bf16[1,4,72,2176]{3,2,0,1:T(8,128)(2,1)} %pad_maximum_fusion.12), calls=%async_computation | async-start | bytes 2506752 | tf_op jit(solution)/shard_map/all_to_all | solution.py:67
  114.4 51.9 %reduce-scatter.3.cloned.1.call-start = ((), (), s32[]{:S(2)}) async-start(), calls=%async_computation.6 | async-start | bytes 1769472 | tf_op jit(solution)/shard_map/reduce_scatter | solution.py:104
  118.8 22.7 %collective-permute-start.4 = (bf16[864,2176]{1,0:T(8,128)(2,1)}, bf16[864,2176]{1,0:T(8,128)(2,1)}, u32[]{:S(2)}, u32[]{:S(2)}) collective-permute-start(bf16[864,2176]{1,0:T(8,128)(2,1)} %bitcast.28), channel_id=1, source_target_pairs={{0,1},{1,0},{2,3},{3,2},{4,5},{5,4},{6,7},{7,6},{8,9},{9,8},{10,11... | collective-permute-start | bytes 11280392 | tf_op jit(solution)/shard_map/ppermute | solution.py:70
  129.7 3.0 %collective-permute-start = (bf16[288,2176]{1,0:T(8,128)(2,1)S(1)}, bf16[288,2176]{1,0:T(8,128)(2,1)S(1)}, u32[]{:S(2)}, u32[]{:S(2)}) collective-permute-start(bf16[288,2176]{1,0:T(8,128)(2,1)S(1)} %bitcast.135), channel_id=1, source_target_pairs={{0,1},{1,0},{2,3},{3,2},{4,5},{5,4},{6,7},{7,6},{8,9},{9,8},{10,11... | collective-permute-start | bytes 3760136 | tf_op jit(solution)/shard_map/ppermute | solution.py:70
  132.7 2.1 copy-start.25
  132.9 2.7 %copy-start.10 = (bf16[288,2048]{1,0:T(8,128)(2,1)}, bf16[288,2048]{1,0:T(8,128)(2,1)S(1)}, u32[]{:S(2)}) copy-start(bf16[288,2048]{1,0:T(8,128)(2,1)S(1)} %get-tuple-element.48) | copy-start | bytes 3538948
  132.9 4.1 %copy-start.8 = (bf16[288,2048]{1,0:T(8,128)(2,1)}, bf16[288,2048]{1,0:T(8,128)(2,1)S(1)}, u32[]{:S(2)}) copy-start(bf16[288,2048]{1,0:T(8,128)(2,1)S(1)} %get-tuple-element.47) | copy-start | bytes 3538948
  134.8 1.4 copy-start.1
  135.6 1.4 copy-start.20
  138.7 0.8 copy-start.16
  138.7 0.8 copy-start.22
  141.4 42.6 %reduce-scatter.5.cloned.1.call-start = ((), (), s32[]{:S(2)}) async-start(), calls=%async_computation.7 | async-start | bytes 5308416 | tf_op jit(solution)/shard_map/reduce_scatter | solution.py:104
  141.5 3.5 %copy-start.26 = (bf16[1,384,2048]{2,1,0:T(8,128)(2,1)S(1)}, bf16[1,384,2048]{2,1,0:T(8,128)(2,1)}, u32[]{:S(2)}) copy-start(bf16[1,384,2048]{2,1,0:T(8,128)(2,1)} %param.13) | copy-start | bytes 4718596
  145.0 2.0 copy-start.4
  145.0 5.8 %copy-start.2 = (bf16[864,2048]{1,0:T(8,128)(2,1)}, bf16[864,2048]{1,0:T(8,128)(2,1)S(1)}, u32[]{:S(2)}) copy-start(bf16[864,2048]{1,0:T(8,128)(2,1)S(1)} %get-tuple-element.41) | copy-start | bytes 10616836
  147.0 3.7 %copy-start.6 = (f32[864,384]{1,0:T(8,128)}, f32[864,384]{1,0:T(8,128)S(1)}, u32[]{:S(2)}) copy-start(f32[864,384]{1,0:T(8,128)S(1)} %fusion.45) | copy-start | bytes 3981316
  154.4 2.0 copy-start.12
  154.4 2.0 copy-start.18
  160.3 1.0 copy-start.21
  160.3 2.1 copy-start.7
  168.3 18.8 %all-to-all-start.1 = ((bf16[1,4,72,1152]{3,2,0,1:T(8,128)(2,1)}), bf16[1,4,72,1152]{3,2,0,1:T(8,128)(2,1)S(1)}, u32[]{:S(2)}, u32[]{:S(2)}) async-start(bf16[1,4,72,1152]{3,2,0,1:T(8,128)(2,1)} %bitcast.16), calls=%async_computation.2 | async-start | bytes 1327104 | tf_op jit(solution)/shard_map/all_to_all | solution.py:111
  187.1 4.8 %copy-start.11 = (bf16[288,2048]{1,0:T(8,128)(2,1)S(1)}, bf16[288,2048]{1,0:T(8,128)(2,1)}, u32[]{:S(2)}) copy-start(bf16[288,2048]{1,0:T(8,128)(2,1)} %copy-done.10) | copy-start | bytes 3538948
  187.1 29.3 %all-to-all-start.3 = ((bf16[3,4,72,1152]{3,2,0,1:T(8,128)(2,1)}), bf16[3,4,72,1152]{3,2,0,1:T(8,128)(2,1)}, u32[]{:S(2)}, u32[]{:S(2)}) async-start(bf16[3,4,72,1152]{3,2,0,1:T(8,128)(2,1)} %copy.81), calls=%async_computation.5 | async-start | bytes 3981312 | tf_op jit(solution)/shard_map/all_to_all | solution.py:111
  191.9 5.9 %copy-start.3 = (bf16[864,2048]{1,0:T(8,128)(2,1)S(1)}, bf16[864,2048]{1,0:T(8,128)(2,1)}, u32[]{:S(2)}) copy-start(bf16[864,2048]{1,0:T(8,128)(2,1)} %copy-done.2) | copy-start | bytes 10616836
  191.9 5.8 %copy-start.9 = (bf16[288,2048]{1,0:T(8,128)(2,1)S(1)}, bf16[288,2048]{1,0:T(8,128)(2,1)}, u32[]{:S(2)}) copy-start(bf16[288,2048]{1,0:T(8,128)(2,1)} %copy-done.8) | copy-start | bytes 3538948
  191.9 5.8 %copy-start.19 = (bf16[864,384]{1,0:T(8,128)(2,1)S(1)}, bf16[864,384]{1,0:T(8,128)(2,1)}, u32[]{:S(2)}) copy-start(bf16[864,384]{1,0:T(8,128)(2,1)} %copy-done.18) | copy-start | bytes 1990660
  191.9 5.8 %copy-start.23 = (bf16[288,384]{1,0:T(8,128)(2,1)S(1)}, bf16[288,384]{1,0:T(8,128)(2,1)}, u32[]{:S(2)}) copy-start(bf16[288,384]{1,0:T(8,128)(2,1)} %copy-done.22) | copy-start | bytes 663556
  197.8 4.0 %copy-start.13 = (bf16[864,384]{1,0:T(8,128)(2,1)S(1)}, bf16[864,384]{1,0:T(8,128)(2,1)}, u32[]{:S(2)}) copy-start(bf16[864,384]{1,0:T(8,128)(2,1)} %copy-done.12) | copy-start | bytes 1990660
  197.8 3.9 %copy-start.17 = (bf16[288,384]{1,0:T(8,128)(2,1)S(1)}, bf16[288,384]{1,0:T(8,128)(2,1)}, u32[]{:S(2)}) copy-start(bf16[288,384]{1,0:T(8,128)(2,1)} %copy-done.16) | copy-start | bytes 663556
  206.3 12.1 %copy-start.15 = (bf16[3,288,128]{2,1,0:T(8,128)(2,1)S(1)}, bf16[3,288,128]{2,1,0:T(8,128)(2,1)}, u32[]{:S(2)}) copy-start(bf16[3,288,128]{2,1,0:T(8,128)(2,1)} %copy-done.14) | copy-start | bytes 663556
  220.4 13.7 %collective-permute-start.5 = (bf16[128,1152]{1,0:T(8,128)(2,1)S(1)}, bf16[128,1152]{1,0:T(8,128)(2,1)S(1)}, u32[]{:S(2)}, u32[]{:S(2)}) collective-permute-start(bf16[128,1152]{1,0:T(8,128)(2,1)S(1)} %get-tuple-element.53), channel_id=1, source_target_pairs={{0,24},{8,0},{16,8},{24,16},{1,25},{9,1},{17,9},{25,17},{2,26},{10... | collective-permute-start | bytes 884744 | tf_op jit(solution)/shard_map/ppermute | solution.py:127
  223.8 21.5 %collective-permute-start.7 = (bf16[128,1152]{1,0:T(8,128)(2,1)S(1)}, bf16[128,1152]{1,0:T(8,128)(2,1)S(1)}, u32[]{:S(2)}, u32[]{:S(2)}) collective-permute-start(bf16[128,1152]{1,0:T(8,128)(2,1)S(1)} %get-tuple-element.54), channel_id=1, source_target_pairs={{0,8},{8,16},{16,24},{24,0},{1,9},{9,17},{17,25},{25,1},{2,10},{10... | collective-permute-start | bytes 884744 | tf_op jit(solution)/shard_map/ppermute | solution.py:127
  227.8 26.7 %collective-permute-start.6 = (bf16[128,1152]{1,0:T(8,128)(2,1)S(1)}, bf16[128,1152]{1,0:T(8,128)(2,1)S(1)}, u32[]{:S(2)}, u32[]{:S(2)}) collective-permute-start(bf16[128,1152]{1,0:T(8,128)(2,1)S(1)} %get-tuple-element.55), channel_id=1, source_target_pairs={{0,16},{8,24},{16,0},{24,8},{1,17},{9,25},{17,1},{25,9},{2,18},{10... | collective-permute-start | bytes 884744 | tf_op jit(solution)/shard_map/ppermute | solution.py:127
Sparse Core Ops, SparseCore 0:
  141.6 20.7 reduce-scatter.2
  164.7 19.2 reduce-scatter.4

commit v8 on v5

--- a/solution.py
+++ b/solution.py
@@ -134,20 +134,16 @@
     half = total.shape[1] - lanes
     token_grad = total[:, :half].astype(jnp.bfloat16)
     gate_grad = total[:, half:half + top_count].astype(jnp.bfloat16)
-    all_x = jnp.concatenate(rows_x, axis=0)
-    all_dy = jnp.concatenate(rows_dy, axis=0)
-    grad_g = lax.dot_general(
-        all_x, jnp.concatenate(rows_pre, axis=0), (((0,), (0,)), ((), ())),
-        preferred_element_type=jnp.float32,
-    ).astype(jnp.bfloat16)
-    grad_u = lax.dot_general(
-        all_x, jnp.concatenate(rows_up, axis=0), (((0,), (0,)), ((), ())),
-        preferred_element_type=jnp.float32,
-    ).astype(jnp.bfloat16)
-    grad_d = lax.dot_general(
-        jnp.concatenate(rows_w, axis=0), all_dy, (((0,), (0,)), ((), ())),
-        preferred_element_type=jnp.float32,
-    ).astype(jnp.bfloat16)
+    def over_groups(lhs, rhs):
+        total_w = None
+        for l, r in zip(lhs, rhs):
+            term = lax.dot_general(l, r, (((0,), (0,)), ((), ())), preferred_element_type=jnp.float32)
+            total_w = term if total_w is None else total_w + term
+        return total_w.astype(jnp.bfloat16)
+
+    grad_g = over_groups(rows_x, rows_pre)
+    grad_u = over_groups(rows_x, rows_up)
+    grad_d = over_groups(rows_w, rows_dy)
     return (token_grad, gate_grad, grad_g[None], grad_u[None], grad_d[None])
 
 

time: 253 us -> 269 us (1.063)
  matrix products: 37.1 us -> 56 us
  waiting for transfers between devices: 120 us -> 111 us
  local copies, waits for them, and re-layouts: 17.9 us -> 20.6 us
    reduce_scatter x2, waiting for transfers between devices: 22.6 us -> 5.75 us  [on_device(): lax.psum_scatter(jnp.concatenate(pieces, axis=1), 'tensor', scatter_dimen...]
    dot_general x3 -> x6, matrix products: 13.6 us -> 27.3 us  [over_groups(): lax.dot_general(l, r, (((0,), (0,)), ((), ())), preferred_element_type=jn...]
    dot_general x2, matrix products: 2.8 us -> 9.47 us  [on_device(): lax.dot_general(routed_dy, weight_d, (((1,), (1,)), ((), ())), preferred_...]
    ppermute x3, starting transfers between devices: 4.59 us -> 9.19 us  [on_device(): part = lax.ppermute(part, 'dp', [(i, (i - s) % n_dp) for i in range(n_dp)])]
    ppermute x3, waiting for transfers between devices: 22.7 us -> 25.8 us  [on_device(): lax.ppermute(ext, 'dp', [(i, (i + s) % n_dp) for i in range(n_dp)])]
    unnamed x44 -> x54, local copies, waits for them, and re-layouts: 6.14 us -> 5.51 us
  transfers between devices with their start and end apart: 14 -> 14, of which waited for: 9 -> 7; matrix products, arithmetic and copies ran while one was open for 30% -> 36% of each run, Pallas kernels for 0% -> 0%
where the time goes in v8:
time: 269 us; the launch traced here: 267 us
  waiting for transfers between devices  111 us (41%)
  matrix products  56 us (21%)
  starting transfers between devices  33.2 us (12%)
  other arithmetic  32.1 us (12%)
  local copies, waits for them, and re-layouts  20.6 us (8%)
  between operations  14.7 us (5%)
    all_to_all x2, waiting for transfers between devices, on_device(): lax.all_to_all(send.reshape(n_mem, n_ex, capacity, features + lanes), 'ex...  42.8 us
    dot_general x6, matrix products, over_groups(): lax.dot_general(l, r, (((0,), (0,)), ((), ())), preferred_element_type=jn...  27.3 us
    ppermute x3, waiting for transfers between devices, on_device(): lax.ppermute(ext, 'dp', [(i, (i + s) % n_dp) for i in range(n_dp)])  25.8 us
    ppermute x3, waiting for transfers between devices, on_device(): part = lax.ppermute(part, 'dp', [(i, (i - s) % n_dp) for i in range(n_dp)])  25.4 us
    all_to_all x2, waiting for transfers between devices, on_device(): lax.all_to_all(ret.reshape(n_mem, n_ex, capacity, half + lanes), 'expert'...  11 us
    dot_general x2, matrix products, on_device(): lax.dot_general(routed_dy, weight_d, (((1,), (1,)), ((), ())), preferred_...  9.47 us
    ppermute x3, starting transfers between devices, on_device(): part = lax.ppermute(part, 'dp', [(i, (i - s) % n_dp) for i in range(n_dp)])  9.19 us
    all_to_all x2, starting transfers between devices, on_device(): lax.all_to_all(send.reshape(n_mem, n_ex, capacity, features + lanes), 'ex...  8.47 us
  transfers between devices with their start and end apart: 14, of which 7 were waited for; matrix products, arithmetic and copies ran while one was open for 36% of the time, Pallas kernels for 0%

profile of v8, /device:TPU:0, one launch (start us, length us, event | category | flops | bytes accessed | tf_op | source)
XLA Modules:
  0.0 267.5 jit_solution(15859696810510542101)
XLA Ops:
  7.2 1.4 copy.64
  8.6 1.3 copy.65
  10.1 0.9 fusion.85
  11.0 3.0 %collective-permute-start.1 = (bf16[128,2176]{0,1:T(8,128)(2,1)}, bf16[128,2176]{0,1:T(8,128)(2,1)S(1)}, u32[]{:S(2)}, u32[]{:S(2)}) collective-permute-start(bf16[128,2176]{0,1:T(8,128)(2,1)} %get-tuple-element.47), channel_id=1, source_target_pairs={{0,8},{8,16},{16,24},{24,0},{1,9},{9,17},{17,25},{25,1},{2,10},{10... | collective-permute-start | bytes 1671176 | tf_op jit(solution)/shard_map/ppermute | solution.py:25
  14.0 2.6 collective-permute-start.2
  16.6 1.3 collective-permute-start.3
  18.1 0.8 fusion.45
  19.5 1.1 select_reduce_fusion.3
  20.7 1.5 convolution_convert_fusion.1
  22.3 1.1 pad_maximum_fusion.3
  23.4 3.7 %all-to-all-start = ((bf16[1,4,72,2176]{3,2,0,1:T(8,128)(2,1)}), bf16[1,4,72,2176]{3,2,0,1:T(8,128)(2,1)S(1)}, u32[]{:S(2)}, u32[]{:S(2)}) async-start(bf16[1,4,72,2176]{3,2,0,1:T(8,128)(2,1)} %pad_maximum_fusion.3), calls=%async_computation | async-start | bytes 2506752 | tf_op jit(solution)/shard_map/all_to_all | solution.py:67
  27.1 2.7 %collective-permute-done.1 = bf16[128,2176]{0,1:T(8,128)(2,1)S(1)} collective-permute-done((bf16[128,2176]{0,1:T(8,128)(2,1)}, bf16[128,2176]{0,1:T(8,128)(2,1)S(1)}, u32[]{:S(2)}, u32[]{:S(2)}) %collective-permute-start.1) | collective-permute-done | bytes 557088 | tf_op jit(solution)/shard_map/ppermute | solution.py:25
  29.8 23.1 %collective-permute-done.2 = bf16[128,2176]{0,1:T(8,128)(2,1)} collective-permute-done((bf16[128,2176]{0,1:T(8,128)(2,1)}, bf16[128,2176]{0,1:T(8,128)(2,1)}, u32[]{:S(2)}, u32[]{:S(2)}) %collective-permute-start.2) | collective-permute-done | bytes 557088 | tf_op jit(solution)/shard_map/ppermute | solution.py:25
  53.7 2.6 pad_maximum_fusion.2
  56.9 0.8 copy.74
  57.7 1.1 sub.48
  59.3 0.8 convert_element_type.215
  60.1 1.0 copy.75
  61.9 1.7 select_reduce_fusion.1
  63.7 1.6 fusion.10
  65.3 2.6 convolution_convert_fusion
  68.3 2.1 copy.78
  70.4 4.8 %all-to-all-start.2 = ((bf16[3,4,72,2176]{3,2,0,1:T(8,128)(2,1)}), bf16[3,4,72,2176]{3,2,0,1:T(8,128)(2,1)}, u32[]{:S(2)}, u32[]{:S(2)}) async-start(bf16[3,4,72,2176]{3,2,0,1:T(8,128)(2,1)} %copy.78), calls=%async_computation.3 | async-start | bytes 7520256 | tf_op jit(solution)/shard_map/all_to_all | solution.py:67
  75.5 42.8 %all-to-all-done.2 = bf16[3,4,72,2176]{3,2,0,1:T(8,128)(2,1)} async-done(((bf16[3,4,72,2176]{3,2,0,1:T(8,128)(2,1)}), bf16[3,4,72,2176]{3,2,0,1:T(8,128)(2,1)}, u32[]{:S(2)}, u32[]{:S(2)}) %all-to-all-start.2) | async-done | bytes 3760160 | tf_op jit(solution)/shard_map/all_to_all | solution.py:67
  118.3 4.2 %copy.79 = bf16[3,4,72,2176]{3,2,1,0:T(8,128)(2,1)} copy(bf16[3,4,72,2176]{3,2,0,1:T(8,128)(2,1)} %all-to-all-done.2) | data formatting | bytes 7520256 | tf_op jit(solution)/shard_map/all_to_all | solution.py:67
  122.6 1.0 convert_reduce_fusion.3
  123.6 1.5 broadcast_select_fusion.2
  125.3 0.8 fusion.17
  126.3 0.8 copy-done.6
  127.2 0.8 fusion.21
  128.0 2.9 %fusion.72 = (f32[288]{0:T(512)S(1)}, bf16[288,384]{1,0:T(8,128)(2,1)}, bf16[288,384]{1,0:T(8,128)(2,1)S(1)}, bf16[288,384]{1,0:T(8,128)(2,1)S(1)}) fusion(f32[288,384]{1,0:T(8,128)S(1)} %fusion.21, f32[288,384]{1,0:T(8,128)S(1)} %fusion.17, f32[288]{0:T(512)S(1)} %convert_reduce_fusion.3, bf16[1,384,2048]{2,1,0:T(8,128)(2,1)S(1)} %copy-done, ...), kind=kOutput, calls=%fused_computation.103 | convolution fusion | flops 455675616 | bytes 5483649 | tf_op jit(solution)/shard_map/dot_general | solution.py:81
  133.1 1.7 pad_maximum_fusion.1
  134.8 1.2 convert_reduce_fusion.1
  136.0 3.6 %broadcast_select_fusion = bf16[864,2048]{1,0:T(8,128)(2,1)S(1)} fusion(pred[]{:T(512)S(6)} %eq.88, bf16[864,2176]{1,0:T(8,128)(2,1)} %bitcast.32, bf16[864,2176]{1,0:T(8,128)(2,1)} %collective-permute-done.4), kind=kLoop, calls=%fused_computation.12 | loop fusion | flops 1769472 | bytes 10616833 | tf_op jit(solution)/shard_map/jit(_where)/select_n | solution.py:72
  139.6 2.0 fusion.15
  142.2 2.0 fusion.19
  144.2 6.6 %fusion.30 = (f32[864]{0:T(1024)S(1)}, bf16[864,384]{1,0:T(8,128)(2,1)}, bf16[864,384]{1,0:T(8,128)(2,1)S(1)}, bf16[864,384]{1,0:T(8,128)(2,1)S(1)}) fusion(f32[864,384]{1,0:T(8,128)S(1)} %fusion.19, f32[864,384]{1,0:T(8,128)S(1)} %fusion.15, f32[864]{0:T(1024)S(1)} %convert_reduce_fusion.1, bf16[1,384,2048]{2,1,0:T(8,128)(2,1)S(1)} %copy-done, ...), kind=kOutput, calls=%fused_computation.49 | convolution fusion | flops 1367026816 | bytes 13302529 | tf_op jit(solution)/shard_map/dot_general | solution.py:81
  151.0 1.1 fusion.55
  152.1 1.1 fusion.49
  153.2 1.1 convolution_add_fusion.1
  154.4 1.1 convolution_add_fusion
  155.5 3.4 %pad_maximum_fusion = f32[864,2304]{1,0:T(8,128)} fusion(f32[864,128]{1,0:T(8,128)S(1)} %pad.35, f32[864,1024]{1,0:T(8,128)S(1)} %convolution_add_fusion, f32[864,1024]{1,0:T(8,128)S(1)} %convolution_add_fusion.1), kind=kLoop, calls=%fused_computation | loop fusion | flops 5971968 | bytes 15482880 | tf_op jit(solution)/shard_map/concatenate | solution.py:112
  159.0 6.0 %fusion.87 = f32[2048,384]{1,0:T(8,128)} fusion(bf16[864,2048]{1,0:T(8,128)(2,1)} %copy-done.8, bf16[864,384]{1,0:T(8,128)(2,1)S(1)} %get-tuple-element.40), kind=kOutput, calls=%fused_computation.141 | convolution fusion | flops 1358954496 | bytes 7348224 | tf_op jit(solution)/shard_map/dot_general | solution.py:140
  165.0 2.3 convert_element_type.209
  167.3 3.7 %all-to-all-start.1 = ((bf16[1,4,72,1152]{3,2,0,1:T(8,128)(2,1)}), bf16[1,4,72,1152]{3,2,0,1:T(8,128)(2,1)S(1)}, u32[]{:S(2)}, u32[]{:S(2)}) async-start(bf16[1,4,72,1152]{3,2,0,1:T(8,128)(2,1)} %bitcast.157), calls=%async_computation.2 | async-start | bytes 1327104 | tf_op jit(solution)/shard_map/all_to_all | solution.py:114
  171.1 4.4 %fusion.8 = bf16[1,2048,384]{2,1,0:T(8,128)(2,1)} fusion(f32[2048,384]{1,0:T(8,128)} %fusion.87, bf16[288,2048]{1,0:T(8,128)(2,1)S(1)} %copy-done.3, bf16[288,384]{1,0:T(8,128)(2,1)S(1)} %copy-done.16), kind=kOutput, calls=%fused_computation.21 | convolution fusion | flops 454557696 | bytes 6119424 | tf_op jit(solution)/shard_map/dot_general | solution.py:140
  175.4 4.1 %fusion.86 = f32[2048,384]{1,0:T(8,128)} fusion(bf16[864,2048]{1,0:T(8,128)(2,1)S(1)} %copy-done.9, bf16[864,384]{1,0:T(8,128)(2,1)S(1)} %copy-done.11), kind=kOutput, calls=%fused_computation.140 | convolution fusion | flops 1358954496 | bytes 7348224 | tf_op jit(solution)/shard_map/dot_general | solution.py:140
  179.5 5.8 %reduce-scatter.5.cloned.1.call-done = f32[864,1152]{1,0:T(8,128)} async-done(((f32[864,2304]{1,0:T(8,128)}), f32[864,1152]{1,0:T(8,128)}) %reduce-scatter.5.cloned.1.call-update) | async-done | bytes 3981328 | tf_op jit(solution)/shard_map/reduce_scatter | solution.py:111
  185.3 2.3 convert_element_type.225
  187.6 1.4 copy.81
  189.0 4.5 %all-to-all-start.3 = ((bf16[3,4,72,1152]{3,2,0,1:T(8,128)(2,1)}), bf16[3,4,72,1152]{3,2,0,1:T(8,128)(2,1)}, u32[]{:S(2)}, u32[]{:S(2)}) async-start(bf16[3,4,72,1152]{3,2,0,1:T(8,128)(2,1)} %copy.81), calls=%async_computation.5 | async-start | bytes 3981312 | tf_op jit(solution)/shard_map/all_to_all | solution.py:114
  193.6 4.3 %fusion.7 = bf16[1,2048,384]{2,1,0:T(8,128)(2,1)} fusion(f32[2048,384]{1,0:T(8,128)} %fusion.86, bf16[288,2048]{1,0:T(8,128)(2,1)S(1)} %copy-done.3, bf16[288,384]{1,0:T(8,128)(2,1)S(1)} %copy-done.14), kind=kOutput, calls=%fused_computation.20 | convolution fusion | flops 454557696 | bytes 6119424 | tf_op jit(solution)/shard_map/dot_general | solution.py:140
  197.9 5.0 %fusion.67 = f32[384,2048]{1,0:T(8,128)S(1)} fusion(bf16[864,384]{1,0:T(8,128)(2,1)S(1)} %copy-done.24, f32[864]{0:T(1024)S(1)} %convert_reduce_fusion.1, pred[]{:T(512)S(6)} %eq.88, bf16[864,2176]{1,0:T(8,128)(2,1)} %bitcast.32, bf16[864,2176]{1,0:T(8,128)(2,1)} %collective-permute-done.4), kind=kOutput, calls=%fused_computation.91 | convolution fusion | flops 1361719296 | bytes 10890625 | tf_op jit(solution)/shard_map/dot_general | solution.py:140
  202.9 3.5 %fusion.9 = bf16[1,384,2048]{2,1,0:T(8,128)(2,1)} fusion(f32[384,2048]{1,0:T(8,128)S(1)} %fusion.67, bf16[288,384]{1,0:T(8,128)(2,1)S(1)} %copy-done.21, f32[288]{0:T(512)S(1)} %convert_reduce_fusion.3, pred[]{:T(512)S(6)} %eq.88, bf16[288,2176]{1,0:T(8,128)(2,1)S(1)} %bitcast.148, bf16[288,2176]{1,0:T(8,128)(2,1)} %collective-permute-done), kind=kOutput, calls=%fused_computation.22 | convolution fusion | flops 455479296 | bytes 7301121 | tf_op jit(solution)/shard_map/dot_general | solution.py:140
  207.1 11.0 %all-to-all-done.3 = bf16[3,4,72,1152]{3,2,0,1:T(8,128)(2,1)} async-done(((bf16[3,4,72,1152]{3,2,0,1:T(8,128)(2,1)}), bf16[3,4,72,1152]{3,2,0,1:T(8,128)(2,1)}, u32[]{:S(2)}, u32[]{:S(2)}) %all-to-all-start.3) | async-done | bytes 1990688 | tf_op jit(solution)/shard_map/all_to_all | solution.py:114
  218.2 1.7 copy.82
  219.9 1.5 fusion.27
  221.6 1.1 select_reduce_fusion
  222.8 1.2 fusion.46
  224.2 8.0 %collective-permute-start.5 = (bf16[128,1152]{1,0:T(8,128)(2,1)S(1)}, bf16[128,1152]{1,0:T(8,128)(2,1)S(1)}, u32[]{:S(2)}, u32[]{:S(2)}) collective-permute-start(bf16[128,1152]{1,0:T(8,128)(2,1)S(1)} %get-tuple-element.43), channel_id=1, source_target_pairs={{0,24},{8,0},{16,8},{24,16},{1,25},{9,1},{17,9},{25,17},{2,26},{10... | collective-permute-start | bytes 884744 | tf_op jit(solution)/shard_map/ppermute | solution.py:130
  232.2 1.2 collective-permute-start.6
  233.7 6.0 %collective-permute-done.5 = bf16[128,1152]{1,0:T(8,128)(2,1)S(1)} collective-permute-done((bf16[128,1152]{1,0:T(8,128)(2,1)S(1)}, bf16[128,1152]{1,0:T(8,128)(2,1)S(1)}, u32[]{:S(2)}, u32[]{:S(2)}) %collective-permute-start.5) | collective-permute-done | bytes 294944 | tf_op jit(solution)/shard_map/ppermute | solution.py:130
  239.7 19.4 %collective-permute-done.6 = bf16[128,1152]{1,0:T(8,128)(2,1)S(1)} collective-permute-done((bf16[128,1152]{1,0:T(8,128)(2,1)S(1)}, bf16[128,1152]{1,0:T(8,128)(2,1)S(1)}, u32[]{:S(2)}, u32[]{:S(2)}) %collective-permute-start.6) | collective-permute-done | bytes 294944 | tf_op jit(solution)/shard_map/ppermute | solution.py:130
  259.2 0.7 slice.153
  (103 shorter events, 10.2 us)
Async XLA Ops:
  7.2 120.8 %copy-start = (bf16[1,384,2048]{2,1,0:T(8,128)(2,1)S(1)}, bf16[1,384,2048]{2,1,0:T(8,128)(2,1)}, u32[]{:S(2)}) copy-start(bf16[1,384,2048]{2,1,0:T(8,128)(2,1)} %param.13) | copy-start | bytes 4718596
  7.2 2.8 %copy-start.22 = (s32[128,8]{0,1:T(8,128)S(1)}, s32[128,8]{0,1:T(8,128)}, u32[]{:S(2)}) copy-start(s32[128,8]{0,1:T(8,128)} %param.9) | copy-start | bytes 12292
  7.2 2.8 %copy-start.23 = (bf16[128,8]{0,1:T(8,128)(2,1)S(1)}, bf16[128,8]{0,1:T(8,128)(2,1)}, u32[]{:S(2)}) copy-start(bf16[128,8]{0,1:T(8,128)(2,1)} %param.10) | copy-start | bytes 6148
  11.0 9.8 %copy-start.12 = (bf16[1,128,2176]{1,2,0:T(8,128)(2,1)}, bf16[1,128,2176]{1,2,0:T(8,128)(2,1)S(1)}, u32[]{:S(2)}) copy-start(bf16[1,128,2176]{1,2,0:T(8,128)(2,1)S(1)} %get-tuple-element.46) | copy-start | bytes 1671172
  11.0 18.9 %collective-permute-start.1 = (bf16[128,2176]{0,1:T(8,128)(2,1)}, bf16[128,2176]{0,1:T(8,128)(2,1)S(1)}, u32[]{:S(2)}, u32[]{:S(2)}) collective-permute-start(bf16[128,2176]{0,1:T(8,128)(2,1)} %get-tuple-element.47), channel_id=1, source_target_pairs={{0,8},{8,16},{16,24},{24,0},{1,9},{9,17},{17,25},{25,1},{2,10},{10... | collective-permute-start | bytes 1671176 | tf_op jit(solution)/shard_map/ppermute | solution.py:25
  14.0 39.0 %collective-permute-start.2 = (bf16[128,2176]{0,1:T(8,128)(2,1)}, bf16[128,2176]{0,1:T(8,128)(2,1)}, u32[]{:S(2)}, u32[]{:S(2)}) collective-permute-start(bf16[128,2176]{0,1:T(8,128)(2,1)} %get-tuple-element.47), channel_id=1, source_target_pairs={{0,16},{8,24},{16,0},{24,8},{1,17},{9,25},{17,1},{25,9},{2,18},{10... | collective-permute-start | bytes 1671176 | tf_op jit(solution)/shard_map/ppermute | solution.py:25
  16.6 36.4 %collective-permute-start.3 = (bf16[128,2176]{0,1:T(8,128)(2,1)}, bf16[128,2176]{0,1:T(8,128)(2,1)}, u32[]{:S(2)}, u32[]{:S(2)}) collective-permute-start(bf16[128,2176]{0,1:T(8,128)(2,1)} %get-tuple-element.47), channel_id=1, source_target_pairs={{0,24},{8,0},{16,8},{24,16},{1,25},{9,1},{17,9},{25,17},{2,26},{10... | collective-permute-start | bytes 1671176 | tf_op jit(solution)/shard_map/ppermute | solution.py:25
  19.5 3.9 %copy-start.19 = (bf16[288,128]{1,0:T(8,128)(2,1)}, bf16[288,128]{1,0:T(8,128)(2,1)S(1)}, u32[]{:S(2)}) copy-start(bf16[288,128]{1,0:T(8,128)(2,1)S(1)} %fusion.70) | copy-start | bytes 221188
  23.4 47.0 %all-to-all-start = ((bf16[1,4,72,2176]{3,2,0,1:T(8,128)(2,1)}), bf16[1,4,72,2176]{3,2,0,1:T(8,128)(2,1)S(1)}, u32[]{:S(2)}, u32[]{:S(2)}) async-start(bf16[1,4,72,2176]{3,2,0,1:T(8,128)(2,1)} %pad_maximum_fusion.3), calls=%async_computation | async-start | bytes 2506752 | tf_op jit(solution)/shard_map/all_to_all | solution.py:67
  65.3 2.6 copy-start.17
  70.4 47.9 %all-to-all-start.2 = ((bf16[3,4,72,2176]{3,2,0,1:T(8,128)(2,1)}), bf16[3,4,72,2176]{3,2,0,1:T(8,128)(2,1)}, u32[]{:S(2)}, u32[]{:S(2)}) async-start(bf16[3,4,72,2176]{3,2,0,1:T(8,128)(2,1)} %copy.78), calls=%async_computation.3 | async-start | bytes 7520256 | tf_op jit(solution)/shard_map/all_to_all | solution.py:67
  75.2 89.8 %reduce-scatter.3.cloned.1.call-start = ((), (), s32[]{:S(2)}) async-start(), calls=%async_computation.6 | async-start | bytes 3981312 | tf_op jit(solution)/shard_map/reduce_scatter | solution.py:111
  75.4 47.1 %collective-permute-start = (bf16[288,2176]{1,0:T(8,128)(2,1)S(1)}, bf16[288,2176]{1,0:T(8,128)(2,1)}, u32[]{:S(2)}, u32[]{:S(2)}) collective-permute-start(bf16[288,2176]{1,0:T(8,128)(2,1)S(1)} %bitcast.144), channel_id=1, source_target_pairs={{0,1},{1,0},{2,3},{3,2},{4,5},{5,4},{6,7},{7,6},{8,9},{9,8},{10,11... | collective-permute-start | bytes 3760136 | tf_op jit(solution)/shard_map/ppermute | solution.py:70
  122.6 12.3 %collective-permute-start.4 = (bf16[864,2176]{1,0:T(8,128)(2,1)}, bf16[864,2176]{1,0:T(8,128)(2,1)}, u32[]{:S(2)}, u32[]{:S(2)}) collective-permute-start(bf16[864,2176]{1,0:T(8,128)(2,1)} %bitcast.32), channel_id=1, source_target_pairs={{0,1},{1,0},{2,3},{3,2},{4,5},{5,4},{6,7},{7,6},{8,9},{9,8},{10,11... | collective-permute-start | bytes 11280392 | tf_op jit(solution)/shard_map/ppermute | solution.py:70
  123.6 1.8 copy-start.4
  125.3 1.0 copy-start.2
  125.3 1.8 copy-start.6
  130.9 1.1 copy-start.13
  130.9 1.7 copy-start.15
  134.8 50.5 %reduce-scatter.5.cloned.1.call-start = ((), (), s32[]{:S(2)}) async-start(), calls=%async_computation.7 | async-start | bytes 11943936 | tf_op jit(solution)/shard_map/reduce_scatter | solution.py:111
  136.0 3.6 %copy-start.5 = (bf16[1,2048,384]{2,1,0:T(8,128)(2,1)S(1)}, bf16[1,2048,384]{2,1,0:T(8,128)(2,1)}, u32[]{:S(2)}) copy-start(bf16[1,2048,384]{2,1,0:T(8,128)(2,1)} %param.11) | copy-start | bytes 4718596
  139.6 2.0 copy-start.8
  139.6 2.6 copy-start.7
  150.8 1.3 copy-start.10
  165.0 6.1 %copy-start.3 = (bf16[288,2048]{1,0:T(8,128)(2,1)S(1)}, bf16[288,2048]{1,0:T(8,128)(2,1)}, u32[]{:S(2)}) copy-start(bf16[288,2048]{1,0:T(8,128)(2,1)} %copy-done.2) | copy-start | bytes 3538948
  165.0 6.1 %copy-start.16 = (bf16[288,384]{1,0:T(8,128)(2,1)S(1)}, bf16[288,384]{1,0:T(8,128)(2,1)}, u32[]{:S(2)}) copy-start(bf16[288,384]{1,0:T(8,128)(2,1)} %copy-done.15) | copy-start | bytes 663556
  167.3 21.7 %all-to-all-start.1 = ((bf16[1,4,72,1152]{3,2,0,1:T(8,128)(2,1)}), bf16[1,4,72,1152]{3,2,0,1:T(8,128)(2,1)S(1)}, u32[]{:S(2)}, u32[]{:S(2)}) async-start(bf16[1,4,72,1152]{3,2,0,1:T(8,128)(2,1)} %bitcast.157), calls=%async_computation.2 | async-start | bytes 1327104 | tf_op jit(solution)/shard_map/all_to_all | solution.py:114
  171.0 4.4 %copy-start.9 = (bf16[864,2048]{1,0:T(8,128)(2,1)S(1)}, bf16[864,2048]{1,0:T(8,128)(2,1)}, u32[]{:S(2)}) copy-start(bf16[864,2048]{1,0:T(8,128)(2,1)} %copy-done.8) | copy-start | bytes 10616836
  171.0 4.4 %copy-start.11 = (bf16[864,384]{1,0:T(8,128)(2,1)S(1)}, bf16[864,384]{1,0:T(8,128)(2,1)}, u32[]{:S(2)}) copy-start(bf16[864,384]{1,0:T(8,128)(2,1)} %copy-done.10) | copy-start | bytes 1990660
  189.0 4.6 %copy-start.14 = (bf16[288,384]{1,0:T(8,128)(2,1)S(1)}, bf16[288,384]{1,0:T(8,128)(2,1)}, u32[]{:S(2)}) copy-start(bf16[288,384]{1,0:T(8,128)(2,1)} %copy-done.13) | copy-start | bytes 663556
  189.0 29.1 %all-to-all-start.3 = ((bf16[3,4,72,1152]{3,2,0,1:T(8,128)(2,1)}), bf16[3,4,72,1152]{3,2,0,1:T(8,128)(2,1)}, u32[]{:S(2)}, u32[]{:S(2)}) async-start(bf16[3,4,72,1152]{3,2,0,1:T(8,128)(2,1)} %copy.81), calls=%async_computation.5 | async-start | bytes 3981312 | tf_op jit(solution)/shard_map/all_to_all | solution.py:114
  193.6 4.3 %copy-start.24 = (bf16[864,384]{1,0:T(8,128)(2,1)S(1)}, bf16[864,384]{1,0:T(8,128)(2,1)}, u32[]{:S(2)}) copy-start(bf16[864,384]{1,0:T(8,128)(2,1)} %get-tuple-element.38) | copy-start | bytes 1990660
  197.9 5.0 %copy-start.21 = (bf16[288,384]{1,0:T(8,128)(2,1)S(1)}, bf16[288,384]{1,0:T(8,128)(2,1)}, u32[]{:S(2)}) copy-start(bf16[288,384]{1,0:T(8,128)(2,1)} %get-tuple-element.36) | copy-start | bytes 663556
  207.1 12.8 %copy-start.18 = (bf16[3,288,128]{2,1,0:T(8,128)(2,1)S(1)}, bf16[3,288,128]{2,1,0:T(8,128)(2,1)}, u32[]{:S(2)}) copy-start(bf16[3,288,128]{2,1,0:T(8,128)(2,1)} %copy-done.17) | copy-start | bytes 663556
  222.8 10.6 %copy-start.20 = (bf16[288,128]{1,0:T(8,128)(2,1)S(1)}, bf16[288,128]{1,0:T(8,128)(2,1)}, u32[]{:S(2)}) copy-start(bf16[288,128]{1,0:T(8,128)(2,1)} %copy-done.19) | copy-start | bytes 221188
  224.1 36.6 %copy-start.1 = (bf16[1,384,2048]{2,1,0:T(8,128)(2,1)S(1)}, bf16[1,384,2048]{2,1,0:T(8,128)(2,1)}, u32[]{:S(2)}) copy-start(bf16[1,384,2048]{2,1,0:T(8,128)(2,1)} %param.13) | copy-start | bytes 4718596
  224.2 15.5 %collective-permute-start.5 = (bf16[128,1152]{1,0:T(8,128)(2,1)S(1)}, bf16[128,1152]{1,0:T(8,128)(2,1)S(1)}, u32[]{:S(2)}, u32[]{:S(2)}) collective-permute-start(bf16[128,1152]{1,0:T(8,128)(2,1)S(1)} %get-tuple-element.43), channel_id=1, source_target_pairs={{0,24},{8,0},{16,8},{24,16},{1,25},{9,1},{17,9},{25,17},{2,26},{10... | collective-permute-start | bytes 884744 | tf_op jit(solution)/shard_map/ppermute | solution.py:130
  232.2 26.9 %collective-permute-start.6 = (bf16[128,1152]{1,0:T(8,128)(2,1)S(1)}, bf16[128,1152]{1,0:T(8,128)(2,1)S(1)}, u32[]{:S(2)}, u32[]{:S(2)}) collective-permute-start(bf16[128,1152]{1,0:T(8,128)(2,1)S(1)} %get-tuple-element.45), channel_id=1, source_target_pairs={{0,16},{8,24},{16,0},{24,8},{1,17},{9,25},{17,1},{25,9},{2,18},{10... | collective-permute-start | bytes 884744 | tf_op jit(solution)/shard_map/ppermute | solution.py:130
  233.4 25.7 %collective-permute-start.7 = (bf16[128,1152]{1,0:T(8,128)(2,1)S(1)}, bf16[128,1152]{1,0:T(8,128)(2,1)S(1)}, u32[]{:S(2)}, u32[]{:S(2)}) collective-permute-start(bf16[128,1152]{1,0:T(8,128)(2,1)S(1)} %get-tuple-element.44), channel_id=1, source_target_pairs={{0,8},{8,16},{16,24},{24,0},{1,9},{9,17},{17,25},{25,1},{2,10},{10... | collective-permute-start | bytes 884744 | tf_op jit(solution)/shard_map/ppermute | solution.py:130
Sparse Core Ops, SparseCore 0:
  134.9 19.5 reduce-scatter.2
  159.1 26.1 reduce-scatter.4

commit v9 on v5

--- a/solution.py
+++ b/solution.py
@@ -124,13 +124,12 @@
         parts = jnp.concatenate(
             [col_grad, jnp.pad(col_gate, ((0, 0), (0, 0), (0, lanes - top_count)))], axis=2
         ).astype(jnp.bfloat16)
-        for m, s in enumerate(members):
-            part = parts[m]
-            if s:
-                part = lax.ppermute(part, "dp", [(i, (i - s) % n_dp) for i in range(n_dp)])
-            col_parts.append(part.astype(jnp.float32))
+        col_parts.extend(parts[m] for m in range(n_mem))
 
-    total = sum(col_parts[1:], col_parts[0])
+    by_shift = jnp.stack(col_parts)
+    by_dest = jnp.take(by_shift, (plane - jnp.arange(n_dp, dtype=jnp.int32)) % n_dp, axis=0)
+    arrived = lax.all_to_all(by_dest, "dp", split_axis=0, concat_axis=0, tiled=True)
+    total = jnp.sum(arrived.astype(jnp.float32), axis=0)
     half = total.shape[1] - lanes
     token_grad = total[:, :half].astype(jnp.bfloat16)
     gate_grad = total[:, half:half + top_count].astype(jnp.bfloat16)

time: 253 us -> 255 us (level)
  waiting for transfers between devices: 120 us -> 124 us
    ppermute x3 -> x0, waiting for transfers between devices: 23.4 us -> none  [on_device(): part = lax.ppermute(part, 'dp', [(i, (i - s) % n_dp) for i in range(n_dp)])]
    all_to_all x0 -> x1, waiting for transfers between devices: none -> 14.3 us  [on_device(): lax.all_to_all(by_dest, 'dp', split_axis=0, concat_axis=0, tiled=True)]
    all_to_all x2, waiting for transfers between devices: 10.2 us -> 23.6 us  [on_device(): lax.all_to_all(ret.reshape(n_mem, n_ex, capacity, half + lanes), 'expert'...]
    all_to_all x0 -> x1, starting transfers between devices: none -> 5.14 us  [on_device(): lax.all_to_all(by_dest, 'dp', split_axis=0, concat_axis=0, tiled=True)]
    ppermute x3 -> x0, starting transfers between devices: 4.59 us -> none  [on_device(): part = lax.ppermute(part, 'dp', [(i, (i - s) % n_dp) for i in range(n_dp)])]
    unnamed x44 -> x50, local copies, waits for them, and re-layouts: 6.14 us -> 4.5 us
  transfers between devices with their start and end apart: 14 -> 12, of which waited for: 9 -> 6; matrix products, arithmetic and copies ran while one was open for 30% -> 29% of each run, Pallas kernels for 0% -> 0%
where the time goes in v9:
time: 255 us; the launch traced here: 254 us
  waiting for transfers between devices  124 us (49%)
  matrix products  37.2 us (15%)
  other arithmetic  31.6 us (12%)
  starting transfers between devices  29.4 us (12%)
  local copies, waits for them, and re-layouts  16.9 us (7%)
  between operations  14.7 us (6%)
    all_to_all x2, waiting for transfers between devices, on_device(): lax.all_to_all(send.reshape(n_mem, n_ex, capacity, features + lanes), 'ex...  42.8 us
    all_to_all x2, waiting for transfers between devices, on_device(): lax.all_to_all(ret.reshape(n_mem, n_ex, capacity, half + lanes), 'expert'...  23.6 us
    ppermute x3, waiting for transfers between devices, on_device(): lax.ppermute(ext, 'dp', [(i, (i + s) % n_dp) for i in range(n_dp)])  23.1 us
    reduce_scatter x2, waiting for transfers between devices, on_device(): lax.psum_scatter(jnp.concatenate(pieces, axis=1), 'tensor', scatter_dimen...  20.5 us
    all_to_all x1, waiting for transfers between devices, on_device(): lax.all_to_all(by_dest, 'dp', split_axis=0, concat_axis=0, tiled=True)  14.3 us
    all_to_all x2, starting transfers between devices, on_device(): lax.all_to_all(send.reshape(n_mem, n_ex, capacity, features + lanes), 'ex...  9.04 us
    all_to_all x2, starting transfers between devices, on_device(): lax.all_to_all(ret.reshape(n_mem, n_ex, capacity, half + lanes), 'expert'...  7.92 us
    ppermute x3, starting transfers between devices, on_device(): lax.ppermute(ext, 'dp', [(i, (i + s) % n_dp) for i in range(n_dp)])  6.96 us
  transfers between devices with their start and end apart: 12, of which 6 were waited for; matrix products, arithmetic and copies ran while one was open for 29% of the time, Pallas kernels for 0%

profile of v9, /device:TPU:0, one launch (start us, length us, event | category | flops | bytes accessed | tf_op | source)
XLA Modules:
  0.0 254.1 jit_solution(14020932557517883698)
XLA Ops:
  7.2 1.4 copy.64
  8.6 1.3 copy.65
  10.1 1.1 fusion.116
  11.1 3.0 %collective-permute-start.1 = (bf16[128,2176]{0,1:T(8,128)(2,1)}, bf16[128,2176]{0,1:T(8,128)(2,1)S(1)}, u32[]{:S(2)}, u32[]{:S(2)}) collective-permute-start(bf16[128,2176]{0,1:T(8,128)(2,1)} %get-tuple-element.52), channel_id=1, source_target_pairs={{0,8},{8,16},{16,24},{24,0},{1,9},{9,17},{17,25},{25,1},{2,10},{10... | collective-permute-start | bytes 1671176 | tf_op jit(solution)/shard_map/ppermute | solution.py:25
  14.2 2.6 %collective-permute-start.2 = (bf16[128,2176]{0,1:T(8,128)(2,1)}, bf16[128,2176]{0,1:T(8,128)(2,1)S(1)}, u32[]{:S(2)}, u32[]{:S(2)}) collective-permute-start(bf16[128,2176]{0,1:T(8,128)(2,1)} %get-tuple-element.52), channel_id=1, source_target_pairs={{0,16},{8,24},{16,0},{24,8},{1,17},{9,25},{17,1},{25,9},{2,18},{10... | collective-permute-start | bytes 1671176 | tf_op jit(solution)/shard_map/ppermute | solution.py:25
  16.7 1.3 collective-permute-start.3
  18.1 0.7 fusion.109
  18.8 0.7 convert_subtract_fusion.1
  19.7 0.8 fusion.67
  20.6 0.7 fusion.108
  21.7 1.1 select_reduce_fusion.3
  22.9 1.5 convolution_convert_fusion.1
  24.5 1.2 pad_maximum_fusion.14
  25.6 4.3 %all-to-all-start = ((bf16[1,4,72,2176]{3,2,0,1:T(8,128)(2,1)}), bf16[1,4,72,2176]{3,2,0,1:T(8,128)(2,1)}, u32[]{:S(2)}, u32[]{:S(2)}) async-start(bf16[1,4,72,2176]{3,2,0,1:T(8,128)(2,1)} %pad_maximum_fusion.14), calls=%async_computation | async-start | bytes 2506752 | tf_op jit(solution)/shard_map/all_to_all | solution.py:67
  30.0 23.0 %collective-permute-done.2 = bf16[128,2176]{0,1:T(8,128)(2,1)S(1)} collective-permute-done((bf16[128,2176]{0,1:T(8,128)(2,1)}, bf16[128,2176]{0,1:T(8,128)(2,1)S(1)}, u32[]{:S(2)}, u32[]{:S(2)}) %collective-permute-start.2) | collective-permute-done | bytes 557088 | tf_op jit(solution)/shard_map/ppermute | solution.py:25
  53.0 1.4 pad_maximum_fusion.13
  54.7 0.5 fusion.62
  55.5 1.7 select_reduce_fusion.1
  57.4 1.6 fusion.29
  59.0 2.6 %convolution_convert_fusion = bf16[3,288,2048]{2,1,0:T(8,128)(2,1)S(1)} fusion(bf16[3,288,128]{2,1,0:T(8,128)(2,1)S(1)} %fusion.29, bf16[3,128,2176]{1,2,0:T(8,128)(2,1)} %pad_maximum_fusion.13), kind=kOutput, calls=%fused_computation.20 | convolution fusion | flops 454754304 | bytes 5332992 | tf_op jit(solution)/shard_map/mqt,mtf->mqf/dot_general | solution.py:58
  61.9 2.1 copy.78
  64.0 4.8 %all-to-all-start.2 = ((bf16[3,4,72,2176]{3,2,0,1:T(8,128)(2,1)}), bf16[3,4,72,2176]{3,2,0,1:T(8,128)(2,1)}, u32[]{:S(2)}, u32[]{:S(2)}) async-start(bf16[3,4,72,2176]{3,2,0,1:T(8,128)(2,1)} %copy.78), calls=%async_computation.3 | async-start | bytes 7520256 | tf_op jit(solution)/shard_map/all_to_all | solution.py:67
  69.1 42.8 %all-to-all-done.2 = bf16[3,4,72,2176]{3,2,0,1:T(8,128)(2,1)} async-done(((bf16[3,4,72,2176]{3,2,0,1:T(8,128)(2,1)}), bf16[3,4,72,2176]{3,2,0,1:T(8,128)(2,1)}, u32[]{:S(2)}, u32[]{:S(2)}) %all-to-all-start.2) | async-done | bytes 3760160 | tf_op jit(solution)/shard_map/all_to_all | solution.py:67
  111.9 4.2 %copy.79 = bf16[3,4,72,2176]{3,2,1,0:T(8,128)(2,1)} copy(bf16[3,4,72,2176]{3,2,0,1:T(8,128)(2,1)} %all-to-all-done.2) | data formatting | bytes 7520256 | tf_op jit(solution)/shard_map/all_to_all | solution.py:67
  116.1 1.0 convert_reduce_fusion.3
  117.1 1.5 broadcast_select_fusion.3
  118.8 0.8 fusion.39
  119.6 0.8 fusion.43
  120.4 0.6 copy-done.2
  121.0 1.7 multiply_convert_fusion.4
  123.0 0.5 fusion.87
  123.5 0.5 fusion.81
  124.0 0.5 convolution_add_fusion.3
  124.5 0.5 convolution_add_fusion.2
  125.0 1.7 pad_maximum_fusion.8
  126.8 1.2 convert_reduce_fusion.1
  128.1 3.4 %broadcast_select_fusion = (bf16[864,2048]{1,0:T(8,128)(2,1)S(1)}, bf16[864,2048]{1,0:T(8,128)(2,1)S(1)}) fusion(pred[]{:T(512)S(6)} %eq.90, bf16[864,2176]{1,0:T(8,128)(2,1)} %bitcast.32, bf16[864,2176]{1,0:T(8,128)(2,1)} %collective-permute-done.4), kind=kLoop, calls=%fused_computation.18 | loop fusion | flops 3538944 | bytes 14155777 | tf_op jit(solution)/shard_map/jit(_where)/select_n | solution.py:72
  131.5 2.0 fusion.37
  133.5 2.0 fusion.41
  135.6 3.4 %multiply_convert_fusion.1 = (bf16[864,384]{1,0:T(8,128)(2,1)S(1)}, bf16[864,384]{1,0:T(8,128)(2,1)S(1)}, bf16[864,384]{1,0:T(8,128)(2,1)}, bf16[864,384]{1,0:T(8,128)(2,1)S(1)}) fusion(f32[864,384]{1,0:T(8,128)S(1)} %fusion.41, f32[864]{0:T(1024)S(1)} %convert_reduce_fusion.1, f32[864,384]{1,0:T(8,128)S(1)} %fusion.37, ...), kind=kOutput, calls=%fused_computation.67 | convolution fusion | flops 1365258240 | bytes 10423680 | tf_op jit(solution)/shard_map/dot_general | solution.py:76
  139.5 1.1 fusion.85
  140.6 1.1 fusion.79
  141.7 1.1 convolution_add_fusion.1
  142.8 1.1 convolution_add_fusion
  144.0 3.6 %pad_maximum_fusion = f32[864,2304]{1,0:T(8,128)} fusion(f32[864,128]{1,0:T(8,128)S(1)} %pad.35, f32[864,1024]{1,0:T(8,128)S(1)} %convolution_add_fusion, f32[864,1024]{1,0:T(8,128)S(1)} %convolution_add_fusion.1), kind=kLoop, calls=%fused_computation.1 | loop fusion | flops 5971968 | bytes 15482880 | tf_op jit(solution)/shard_map/concatenate | solution.py:112
  147.6 2.3 convert_element_type.205
  149.9 3.5 %all-to-all-start.1 = ((bf16[1,4,72,1152]{3,2,0,1:T(8,128)(2,1)}), bf16[1,4,72,1152]{3,2,0,1:T(8,128)(2,1)S(1)}, u32[]{:S(2)}, u32[]{:S(2)}) async-start(bf16[1,4,72,1152]{3,2,0,1:T(8,128)(2,1)} %bitcast.20), calls=%async_computation.2 | async-start | bytes 1327104 | tf_op jit(solution)/shard_map/all_to_all | solution.py:114
  153.4 20.5 %reduce-scatter.5.cloned.1.call-done = f32[864,1152]{1,0:T(8,128)} async-done(((f32[864,2304]{1,0:T(8,128)}), f32[864,1152]{1,0:T(8,128)}) %reduce-scatter.5.cloned.1.call-update) | async-done | bytes 3981328 | tf_op jit(solution)/shard_map/reduce_scatter | solution.py:111
  173.8 2.3 convert_element_type.220
  176.2 1.4 copy.81
  177.6 4.4 %all-to-all-start.3 = ((bf16[3,4,72,1152]{3,2,0,1:T(8,128)(2,1)}), bf16[3,4,72,1152]{3,2,0,1:T(8,128)(2,1)}, u32[]{:S(2)}, u32[]{:S(2)}) async-start(bf16[3,4,72,1152]{3,2,0,1:T(8,128)(2,1)} %copy.81), calls=%async_computation.5 | async-start | bytes 3981312 | tf_op jit(solution)/shard_map/all_to_all | solution.py:114
  183.1 23.6 %all-to-all-done.3 = bf16[3,4,72,1152]{3,2,0,1:T(8,128)(2,1)} async-done(((bf16[3,4,72,1152]{3,2,0,1:T(8,128)(2,1)}), bf16[3,4,72,1152]{3,2,0,1:T(8,128)(2,1)}, u32[]{:S(2)}, u32[]{:S(2)}) %all-to-all-start.3) | async-done | bytes 1990688 | tf_op jit(solution)/shard_map/all_to_all | solution.py:114
  206.7 1.7 copy.82
  208.4 0.6 fusion.45
  209.2 1.1 select_reduce_fusion
  210.6 0.7 gather_fusion
  211.3 1.2 broadcast_select_fusion.2
  212.5 5.1 %all-to-all-start.4 = ((bf16[4,128,1152]{2,1,0:T(8,128)(2,1)}), bf16[4,128,1152]{2,1,0:T(8,128)(2,1)S(1)}, u32[]{:S(2)}, u32[]{:S(2)}) async-start(bf16[4,128,1152]{2,1,0:T(8,128)(2,1)} %broadcast_select_fusion.2), calls=%async_computation.6 | async-start | bytes 2359296 | tf_op jit(solution)/shard_map/all_to_all | solution.py:131
  217.7 5.9 %fusion.18 = bf16[1,384,2048]{2,1,0:T(8,128)(2,1)} fusion(bf16[864,2048]{1,0:T(8,128)(2,1)} %copy-done.7, bf16[288,2048]{1,0:T(8,128)(2,1)} %copy-done.14, bf16[864,384]{1,0:T(8,128)(2,1)S(1)} %copy-done.22, bf16[288,384]{1,0:T(8,128)(2,1)S(1)} %copy-done.21), kind=kOutput, calls=%fused_computation.28 | convolution fusion | flops 1823932416 | bytes 7176192 | tf_op jit(solution)/shard_map/dot_general | solution.py:146
  223.6 3.9 %fusion.21 = bf16[1,2048,384]{2,1,0:T(8,128)(2,1)} fusion(bf16[864,2048]{1,0:T(8,128)(2,1)S(1)} %copy-done.6, bf16[288,2048]{1,0:T(8,128)(2,1)S(1)} %copy-done.13, bf16[864,384]{1,0:T(8,128)(2,1)S(1)} %copy-done.9, bf16[288,384]{1,0:T(8,128)(2,1)S(1)} %copy-done.16), kind=kOutput, calls=%fused_computation.29 | convolution fusion | flops 1823932416 | bytes 7176192 | tf_op jit(solution)/shard_map/dot_general | solution.py:142
  227.5 3.9 %fusion.22 = bf16[1,2048,384]{2,1,0:T(8,128)(2,1)} fusion(bf16[864,2048]{1,0:T(8,128)(2,1)S(1)} %copy-done.6, bf16[288,2048]{1,0:T(8,128)(2,1)S(1)} %copy-done.13, bf16[864,384]{1,0:T(8,128)(2,1)S(1)} %copy-done.11, bf16[288,384]{1,0:T(8,128)(2,1)S(1)} %get-tuple-element.48), kind=kOutput, calls=%fused_computation.30 | convolution fusion | flops 1823932416 | bytes 7176192 | tf_op jit(solution)/shard_map/dot_general | solution.py:138
  231.5 14.3 %all-to-all-done.4 = bf16[4,128,1152]{2,1,0:T(8,128)(2,1)S(1)} async-done(((bf16[4,128,1152]{2,1,0:T(8,128)(2,1)}), bf16[4,128,1152]{2,1,0:T(8,128)(2,1)S(1)}, u32[]{:S(2)}, u32[]{:S(2)}) %all-to-all-start.4) | async-done | bytes 1179680 | tf_op jit(solution)/shard_map/all_to_all | solution.py:131
  245.9 0.7 slice.144
  246.6 0.7 copy.84
  (97 shorter events, 5.2 us)
Async XLA Ops:
  7.2 112.5 %copy-start = (bf16[1,384,2048]{2,1,0:T(8,128)(2,1)S(1)}, bf16[1,384,2048]{2,1,0:T(8,128)(2,1)}, u32[]{:S(2)}) copy-start(bf16[1,384,2048]{2,1,0:T(8,128)(2,1)} %param.13) | copy-start | bytes 4718596
  7.2 2.8 %copy-start.19 = (s32[128,8]{0,1:T(8,128)S(1)}, s32[128,8]{0,1:T(8,128)}, u32[]{:S(2)}) copy-start(s32[128,8]{0,1:T(8,128)} %param.9) | copy-start | bytes 12292
  7.2 2.8 %copy-start.20 = (bf16[128,8]{0,1:T(8,128)(2,1)S(1)}, bf16[128,8]{0,1:T(8,128)(2,1)}, u32[]{:S(2)}) copy-start(bf16[128,8]{0,1:T(8,128)(2,1)} %param.10) | copy-start | bytes 6148
  11.1 18.9 %collective-permute-start.1 = (bf16[128,2176]{0,1:T(8,128)(2,1)}, bf16[128,2176]{0,1:T(8,128)(2,1)S(1)}, u32[]{:S(2)}, u32[]{:S(2)}) collective-permute-start(bf16[128,2176]{0,1:T(8,128)(2,1)} %get-tuple-element.52), channel_id=1, source_target_pairs={{0,8},{8,16},{16,24},{24,0},{1,9},{9,17},{17,25},{25,1},{2,10},{10... | collective-permute-start | bytes 1671176 | tf_op jit(solution)/shard_map/ppermute | solution.py:25
  14.2 38.9 %collective-permute-start.2 = (bf16[128,2176]{0,1:T(8,128)(2,1)}, bf16[128,2176]{0,1:T(8,128)(2,1)S(1)}, u32[]{:S(2)}, u32[]{:S(2)}) collective-permute-start(bf16[128,2176]{0,1:T(8,128)(2,1)} %get-tuple-element.52), channel_id=1, source_target_pairs={{0,16},{8,24},{16,0},{24,8},{1,17},{9,25},{17,1},{25,9},{2,18},{10... | collective-permute-start | bytes 1671176 | tf_op jit(solution)/shard_map/ppermute | solution.py:25
  16.7 36.3 %collective-permute-start.3 = (bf16[128,2176]{0,1:T(8,128)(2,1)}, bf16[128,2176]{0,1:T(8,128)(2,1)S(1)}, u32[]{:S(2)}, u32[]{:S(2)}) collective-permute-start(bf16[128,2176]{0,1:T(8,128)(2,1)} %get-tuple-element.52), channel_id=1, source_target_pairs={{0,24},{8,0},{16,8},{24,16},{1,25},{9,1},{17,9},{25,17},{2,26},{10... | collective-permute-start | bytes 1671176 | tf_op jit(solution)/shard_map/ppermute | solution.py:25
  25.6 38.4 %all-to-all-start = ((bf16[1,4,72,2176]{3,2,0,1:T(8,128)(2,1)}), bf16[1,4,72,2176]{3,2,0,1:T(8,128)(2,1)}, u32[]{:S(2)}, u32[]{:S(2)}) async-start(bf16[1,4,72,2176]{3,2,0,1:T(8,128)(2,1)} %pad_maximum_fusion.14), calls=%async_computation | async-start | bytes 2506752 | tf_op jit(solution)/shard_map/all_to_all | solution.py:67
  59.0 2.6 %copy-start.17 = (bf16[3,288,128]{2,1,0:T(8,128)(2,1)}, bf16[3,288,128]{2,1,0:T(8,128)(2,1)S(1)}, u32[]{:S(2)}) copy-start(bf16[3,288,128]{2,1,0:T(8,128)(2,1)S(1)} %fusion.29) | copy-start | bytes 663556
  64.0 47.9 %all-to-all-start.2 = ((bf16[3,4,72,2176]{3,2,0,1:T(8,128)(2,1)}), bf16[3,4,72,2176]{3,2,0,1:T(8,128)(2,1)}, u32[]{:S(2)}, u32[]{:S(2)}) async-start(bf16[3,4,72,2176]{3,2,0,1:T(8,128)(2,1)} %copy.78), calls=%async_computation.3 | async-start | bytes 7520256 | tf_op jit(solution)/shard_map/all_to_all | solution.py:67
  68.8 78.8 %reduce-scatter.3.cloned.1.call-start = ((), (), s32[]{:S(2)}) async-start(), calls=%async_computation.7 | async-start | bytes 3981312 | tf_op jit(solution)/shard_map/reduce_scatter | solution.py:111
  69.0 47.1 %collective-permute-start = (bf16[288,2176]{1,0:T(8,128)(2,1)}, bf16[288,2176]{1,0:T(8,128)(2,1)S(1)}, u32[]{:S(2)}, u32[]{:S(2)}) collective-permute-start(bf16[288,2176]{1,0:T(8,128)(2,1)} %bitcast.11), channel_id=1, source_target_pairs={{0,1},{1,0},{2,3},{3,2},{4,5},{5,4},{6,7},{7,6},{8,9},{9,8},{10,11... | collective-permute-start | bytes 3760136 | tf_op jit(solution)/shard_map/ppermute | solution.py:70
  116.0 10.8 %collective-permute-start.4 = (bf16[864,2176]{1,0:T(8,128)(2,1)}, bf16[864,2176]{1,0:T(8,128)(2,1)}, u32[]{:S(2)}, u32[]{:S(2)}) collective-permute-start(bf16[864,2176]{1,0:T(8,128)(2,1)} %bitcast.32), channel_id=1, source_target_pairs={{0,1},{1,0},{2,3},{3,2},{4,5},{5,4},{6,7},{7,6},{8,9},{9,8},{10,11... | collective-permute-start | bytes 11280392 | tf_op jit(solution)/shard_map/ppermute | solution.py:70
  117.1 1.8 copy-start.3
  118.6 1.0 copy-start.14
  118.6 1.8 copy-start.12
  119.6 1.4 copy-start.2
  122.7 1.8 copy-start.15
  126.8 47.1 %reduce-scatter.5.cloned.1.call-start = ((), (), s32[]{:S(2)}) async-start(), calls=%async_computation.8 | async-start | bytes 11943936 | tf_op jit(solution)/shard_map/reduce_scatter | solution.py:111
  128.0 3.5 %copy-start.4 = (bf16[1,2048,384]{2,1,0:T(8,128)(2,1)S(1)}, bf16[1,2048,384]{2,1,0:T(8,128)(2,1)}, u32[]{:S(2)}) copy-start(bf16[1,2048,384]{2,1,0:T(8,128)(2,1)} %param.12) | copy-start | bytes 4718596
  131.5 2.0 copy-start.7
  131.5 4.0 %copy-start.5 = (bf16[864,2048]{1,0:T(8,128)(2,1)}, bf16[864,2048]{1,0:T(8,128)(2,1)S(1)}, u32[]{:S(2)}) copy-start(bf16[864,2048]{1,0:T(8,128)(2,1)S(1)} %get-tuple-element.39) | copy-start | bytes 10616836
  139.0 1.6 copy-start.10
  139.0 3.8 %copy-start.8 = (bf16[864,384]{1,0:T(8,128)(2,1)}, bf16[864,384]{1,0:T(8,128)(2,1)S(1)}, u32[]{:S(2)}) copy-start(bf16[864,384]{1,0:T(8,128)(2,1)S(1)} %get-tuple-element.41) | copy-start | bytes 1990660
  149.9 27.7 %all-to-all-start.1 = ((bf16[1,4,72,1152]{3,2,0,1:T(8,128)(2,1)}), bf16[1,4,72,1152]{3,2,0,1:T(8,128)(2,1)S(1)}, u32[]{:S(2)}, u32[]{:S(2)}) async-start(bf16[1,4,72,1152]{3,2,0,1:T(8,128)(2,1)} %bitcast.20), calls=%async_computation.2 | async-start | bytes 1327104 | tf_op jit(solution)/shard_map/all_to_all | solution.py:114
  177.6 29.0 %all-to-all-start.3 = ((bf16[3,4,72,1152]{3,2,0,1:T(8,128)(2,1)}), bf16[3,4,72,1152]{3,2,0,1:T(8,128)(2,1)}, u32[]{:S(2)}, u32[]{:S(2)}) async-start(bf16[3,4,72,1152]{3,2,0,1:T(8,128)(2,1)} %copy.81), calls=%async_computation.5 | async-start | bytes 3981312 | tf_op jit(solution)/shard_map/all_to_all | solution.py:114
  183.1 25.3 %copy-start.18 = (bf16[3,288,128]{2,1,0:T(8,128)(2,1)S(1)}, bf16[3,288,128]{2,1,0:T(8,128)(2,1)}, u32[]{:S(2)}) copy-start(bf16[3,288,128]{2,1,0:T(8,128)(2,1)} %copy-done.17) | copy-start | bytes 663556
  212.5 5.2 %copy-start.21 = (bf16[288,384]{1,0:T(8,128)(2,1)S(1)}, bf16[288,384]{1,0:T(8,128)(2,1)}, u32[]{:S(2)}) copy-start(bf16[288,384]{1,0:T(8,128)(2,1)} %get-tuple-element.49) | copy-start | bytes 663556
  212.5 5.2 %copy-start.22 = (bf16[864,384]{1,0:T(8,128)(2,1)S(1)}, bf16[864,384]{1,0:T(8,128)(2,1)}, u32[]{:S(2)}) copy-start(bf16[864,384]{1,0:T(8,128)(2,1)} %get-tuple-element.43) | copy-start | bytes 1990660
  212.5 33.2 %all-to-all-start.4 = ((bf16[4,128,1152]{2,1,0:T(8,128)(2,1)}), bf16[4,128,1152]{2,1,0:T(8,128)(2,1)S(1)}, u32[]{:S(2)}, u32[]{:S(2)}) async-start(bf16[4,128,1152]{2,1,0:T(8,128)(2,1)} %broadcast_select_fusion.2), calls=%async_computation.6 | async-start | bytes 2359296 | tf_op jit(solution)/shard_map/all_to_all | solution.py:131
  217.7 5.9 %copy-start.6 = (bf16[864,2048]{1,0:T(8,128)(2,1)S(1)}, bf16[864,2048]{1,0:T(8,128)(2,1)}, u32[]{:S(2)}) copy-start(bf16[864,2048]{1,0:T(8,128)(2,1)} %copy-done.5) | copy-start | bytes 10616836
  217.7 5.9 %copy-start.9 = (bf16[864,384]{1,0:T(8,128)(2,1)S(1)}, bf16[864,384]{1,0:T(8,128)(2,1)}, u32[]{:S(2)}) copy-start(bf16[864,384]{1,0:T(8,128)(2,1)} %copy-done.8) | copy-start | bytes 1990660
  217.7 5.9 %copy-start.13 = (bf16[288,2048]{1,0:T(8,128)(2,1)S(1)}, bf16[288,2048]{1,0:T(8,128)(2,1)}, u32[]{:S(2)}) copy-start(bf16[288,2048]{1,0:T(8,128)(2,1)} %copy-done.12) | copy-start | bytes 3538948
  217.7 5.9 %copy-start.16 = (bf16[288,384]{1,0:T(8,128)(2,1)S(1)}, bf16[288,384]{1,0:T(8,128)(2,1)}, u32[]{:S(2)}) copy-start(bf16[288,384]{1,0:T(8,128)(2,1)} %copy-done.15) | copy-start | bytes 663556
  223.6 4.0 %copy-start.11 = (bf16[864,384]{1,0:T(8,128)(2,1)S(1)}, bf16[864,384]{1,0:T(8,128)(2,1)}, u32[]{:S(2)}) copy-start(bf16[864,384]{1,0:T(8,128)(2,1)} %copy-done.10) | copy-start | bytes 1990660
  227.5 19.8 %copy-start.1 = (bf16[1,384,2048]{2,1,0:T(8,128)(2,1)S(1)}, bf16[1,384,2048]{2,1,0:T(8,128)(2,1)}, u32[]{:S(2)}) copy-start(bf16[1,384,2048]{2,1,0:T(8,128)(2,1)} %param.13) | copy-start | bytes 4718596
Sparse Core Ops, SparseCore 0:
  126.9 19.5 reduce-scatter.2
  148.8 25.0 reduce-scatter.4

commit v10 on v5

--- a/solution.py
+++ b/solution.py
@@ -55,12 +55,9 @@
         key = jnp.where(in_plane, local_ex * capacity + position, -1).reshape(n_mem, tok_rows, top_count)
         match = key[:, None, :, :] == q_iota[None, :, None, None]
         select = jnp.sum(match.astype(jnp.bfloat16), axis=3)
-        send_rows = jnp.einsum(
-            "mqt,mtf->mqf", select, carried_m, preferred_element_type=jnp.float32
+        send = jnp.einsum(
+            "mqt,mtf->mqf", select, stacked, preferred_element_type=jnp.float32
         ).astype(tokens.dtype)
-        send_gate = jnp.sum(jnp.where(match, gates_m[:, None, :, :], 0.0), axis=(2, 3))
-        gate_cols = jnp.pad(send_gate.astype(tokens.dtype)[:, :, None], ((0, 0), (0, 0), (0, lanes - 1)))
-        send = jnp.concatenate([send_rows, gate_cols], axis=2)
 
         if gi >= 2:
             send = lax.optimization_barrier((send, anchors[gi - 2]))[0]
@@ -71,7 +68,10 @@
         mine_x = core == 0
         routed_x = jnp.where(mine_x, recv[:, :features], other[:, :features])
         routed_dy = jnp.where(mine_x, other[:, :features], recv[:, :features])
-        routed_gate = jnp.where(mine_x, recv[:, features], other[:, features])
+        slot_ids = recv[:, features:features + top_count].astype(jnp.float32)
+        slot_gates = recv[:, features + top_count:features + 2 * top_count].astype(jnp.float32)
+        mine_e = (plane * n_ex + lax.axis_index("expert")).astype(jnp.float32)
+        routed_gate = jnp.sum(jnp.where(slot_ids == mine_e, slot_gates, 0.0), axis=1)
 
         gate_pre = jnp.dot(routed_x, weight_g, preferred_element_type=jnp.float32)
         up_pre = jnp.dot(routed_x, weight_u, preferred_element_type=jnp.float32)

time: 253 us -> 252 us (level)
  waiting for transfers between devices: 120 us -> 126 us
  other arithmetic: 32.2 us -> 28 us
  starting transfers between devices: 30.6 us -> 27.6 us
    ppermute x3, waiting for transfers between devices: 22.7 us -> 41 us  [on_device(): lax.ppermute(ext, 'dp', [(i, (i + s) % n_dp) for i in range(n_dp)])]
    reduce_scatter x2, waiting for transfers between devices: 22.6 us -> 8.31 us  [on_device(): lax.psum_scatter(jnp.concatenate(pieces, axis=1), 'tensor', scatter_dimen...]
    unnamed x44 -> x40, local copies, waits for them, and re-layouts: 6.14 us -> 3.57 us
  transfers between devices with their start and end apart: 14 -> 14, of which waited for: 9 -> 9; matrix products, arithmetic and copies ran while one was open for 30% -> 28% of each run, Pallas kernels for 0% -> 0%
where the time goes in v10:
time: 252 us; the launch traced here: 251 us
  waiting for transfers between devices  126 us (50%)
  matrix products  37 us (15%)
  other arithmetic  28 us (11%)
  starting transfers between devices  27.6 us (11%)
  local copies, waits for them, and re-layouts  17.5 us (7%)
  between operations  14.6 us (6%)
    all_to_all x2, waiting for transfers between devices, on_device(): lax.all_to_all(send.reshape(n_mem, n_ex, capacity, features + lanes), 'ex...  43.1 us
    ppermute x3, waiting for transfers between devices, on_device(): lax.ppermute(ext, 'dp', [(i, (i + s) % n_dp) for i in range(n_dp)])  41 us
    ppermute x3, waiting for transfers between devices, on_device(): part = lax.ppermute(part, 'dp', [(i, (i - s) % n_dp) for i in range(n_dp)])  23.4 us
    all_to_all x2, waiting for transfers between devices, on_device(): lax.all_to_all(ret.reshape(n_mem, n_ex, capacity, half + lanes), 'expert'...  10.3 us
    all_to_all x2, starting transfers between devices, on_device(): lax.all_to_all(send.reshape(n_mem, n_ex, capacity, features + lanes), 'ex...  8.48 us
    reduce_scatter x2, waiting for transfers between devices, on_device(): lax.psum_scatter(jnp.concatenate(pieces, axis=1), 'tensor', scatter_dimen...  8.31 us
    all_to_all x2, starting transfers between devices, on_device(): lax.all_to_all(ret.reshape(n_mem, n_ex, capacity, half + lanes), 'expert'...  8.26 us
    ppermute x3, starting transfers between devices, on_device(): lax.ppermute(ext, 'dp', [(i, (i + s) % n_dp) for i in range(n_dp)])  6.06 us
  transfers between devices with their start and end apart: 14, of which 9 were waited for; matrix products, arithmetic and copies ran while one was open for 28% of the time, Pallas kernels for 0%

profile of v10, /device:TPU:0, one launch (start us, length us, event | category | flops | bytes accessed | tf_op | source)
XLA Modules:
  0.0 250.8 jit_solution(15272528017045528751)
XLA Ops:
  7.2 0.8 convert_element_type.173
  8.0 0.7 pad_maximum_fusion.13
  8.8 1.1 broadcast_select_fusion.4
  9.9 0.9 fusion.107
  10.8 3.0 %collective-permute-start.1 = (bf16[128,2176]{1,0:T(8,128)(2,1)}, bf16[128,2176]{1,0:T(8,128)(2,1)S(1)}, u32[]{:S(2)}, u32[]{:S(2)}) collective-permute-start(bf16[128,2176]{1,0:T(8,128)(2,1)} %get-tuple-element.60), channel_id=1, source_target_pairs={{0,8},{8,16},{16,24},{24,0},{1,9},{9,17},{17,25},{25,1},{2,10},{10... | collective-permute-start | bytes 1671176 | tf_op jit(solution)/shard_map/ppermute | solution.py:25
  13.8 2.0 collective-permute-start.3
  15.9 1.0 collective-permute-start.2
  17.0 0.8 fusion.61
  18.4 1.5 convolution_convert_fusion.1
  19.9 3.7 %all-to-all-start = ((bf16[1,4,72,2176]{3,2,0,1:T(8,128)(2,1)}), bf16[1,4,72,2176]{3,2,0,1:T(8,128)(2,1)S(1)}, u32[]{:S(2)}, u32[]{:S(2)}) async-start(bf16[1,4,72,2176]{3,2,0,1:T(8,128)(2,1)} %bitcast.135), calls=%async_computation | async-start | bytes 2506752 | tf_op jit(solution)/shard_map/all_to_all | solution.py:64
  23.6 5.9 %collective-permute-done.1 = bf16[128,2176]{1,0:T(8,128)(2,1)S(1)} collective-permute-done((bf16[128,2176]{1,0:T(8,128)(2,1)}, bf16[128,2176]{1,0:T(8,128)(2,1)S(1)}, u32[]{:S(2)}, u32[]{:S(2)}) %collective-permute-start.1) | collective-permute-done | bytes 557088 | tf_op jit(solution)/shard_map/ppermute | solution.py:25
  29.6 10.6 %collective-permute-done.3 = bf16[128,2176]{1,0:T(8,128)(2,1)} collective-permute-done((bf16[128,2176]{1,0:T(8,128)(2,1)}, bf16[128,2176]{1,0:T(8,128)(2,1)}, u32[]{:S(2)}, u32[]{:S(2)}) %collective-permute-start.3) | collective-permute-done | bytes 557088 | tf_op jit(solution)/shard_map/ppermute | solution.py:25
  40.2 24.4 %collective-permute-done.2 = bf16[128,2176]{1,0:T(8,128)(2,1)} collective-permute-done((bf16[128,2176]{1,0:T(8,128)(2,1)}, bf16[128,2176]{1,0:T(8,128)(2,1)}, u32[]{:S(2)}, u32[]{:S(2)}) %collective-permute-start.2) | collective-permute-done | bytes 557088 | tf_op jit(solution)/shard_map/ppermute | solution.py:25
  64.6 1.5 convert_subtract_fusion
  66.1 1.1 sub.48
  67.1 0.5 fusion.56
  67.7 0.8 convert_element_type.192
  68.5 1.7 add_select_fusion
  70.2 1.0 copy.65
  71.2 1.6 fusion.21
  72.8 2.4 convolution_convert_fusion
  75.3 2.1 copy.66
  77.4 4.8 %all-to-all-start.2 = ((bf16[3,4,72,2176]{3,2,0,1:T(8,128)(2,1)}), bf16[3,4,72,2176]{3,2,0,1:T(8,128)(2,1)}, u32[]{:S(2)}, u32[]{:S(2)}) async-start(bf16[3,4,72,2176]{3,2,0,1:T(8,128)(2,1)} %copy.66), calls=%async_computation.3 | async-start | bytes 7520256 | tf_op jit(solution)/shard_map/all_to_all | solution.py:64
  82.3 43.1 %all-to-all-done.2 = bf16[3,4,72,2176]{3,2,0,1:T(8,128)(2,1)} async-done(((bf16[3,4,72,2176]{3,2,0,1:T(8,128)(2,1)}), bf16[3,4,72,2176]{3,2,0,1:T(8,128)(2,1)}, u32[]{:S(2)}, u32[]{:S(2)}) %all-to-all-start.2) | async-done | bytes 3760160 | tf_op jit(solution)/shard_map/all_to_all | solution.py:64
  125.4 4.2 %copy.67 = bf16[3,4,72,2176]{3,2,1,0:T(8,128)(2,1)} copy(bf16[3,4,72,2176]{3,2,0,1:T(8,128)(2,1)} %all-to-all-done.2) | data formatting | bytes 7520256 | tf_op jit(solution)/shard_map/all_to_all | solution.py:64
  129.7 1.4 broadcast_select_fusion.2
  131.2 0.8 fusion.40
  132.2 1.3 copy-done.3
  133.5 0.8 fusion.36
  134.3 0.6 copy-done.2
  134.9 1.7 multiply_convert_fusion.4
  138.4 0.5 convolution_add_fusion.3
  138.9 1.7 pad_maximum_fusion.8
  140.9 1.3 select_reduce_fusion.2
  142.2 4.2 %broadcast_select_fusion = (bf16[864,2048]{1,0:T(8,128)(2,1)S(1)}, bf16[864,2048]{1,0:T(8,128)(2,1)S(1)}) fusion(pred[]{:T(512)S(6)} %eq.96, bf16[864,2176]{1,0:T(8,128)(2,1)} %bitcast.27, bf16[864,2176]{1,0:T(8,128)(2,1)} %collective-permute-done.4), kind=kLoop, calls=%fused_computation.15 | loop fusion | flops 3538944 | bytes 14155777 | tf_op jit(solution)/shard_map/jit(_where)/select_n | solution.py:69
  146.4 2.0 fusion.38
  148.5 0.6 copy-done.4
  149.1 2.0 fusion.34
  151.1 3.4 %multiply_convert_fusion.1 = (bf16[864,384]{1,0:T(8,128)(2,1)S(1)}, bf16[864,384]{1,0:T(8,128)(2,1)S(1)}, bf16[864,384]{1,0:T(8,128)(2,1)}, bf16[864,384]{1,0:T(8,128)(2,1)S(1)}) fusion(f32[864,384]{1,0:T(8,128)S(1)} %fusion.38, f32[864]{0:T(1024)S(1)} %select_reduce_fusion.2, f32[864,384]{1,0:T(8,128)S(1)} %fusion.34, ...), kind=kOutput, calls=%fused_computation.58 | convolution fusion | flops 1365258240 | bytes 10423680 | tf_op jit(solution)/shard_map/dot_general | solution.py:76
  155.0 1.1 fusion.74
  156.1 1.1 fusion.80
  157.2 1.1 convolution_add_fusion
  158.3 1.1 convolution_add_fusion.1
  159.5 3.5 %pad_maximum_fusion = f32[864,2304]{1,0:T(8,128)} fusion(f32[864,128]{1,0:T(8,128)S(1)} %pad.25, f32[864,1024]{1,0:T(8,128)S(1)} %convolution_add_fusion, f32[864,1024]{1,0:T(8,128)S(1)} %convolution_add_fusion.1), kind=kLoop, calls=%fused_computation | loop fusion | flops 5971968 | bytes 15482880 | tf_op jit(solution)/shard_map/concatenate | solution.py:112
  163.0 2.2 convert_element_type.186
  165.2 3.5 %all-to-all-start.1 = ((bf16[1,4,72,1152]{3,2,0,1:T(8,128)(2,1)}), bf16[1,4,72,1152]{3,2,0,1:T(8,128)(2,1)S(1)}, u32[]{:S(2)}, u32[]{:S(2)}) async-start(bf16[1,4,72,1152]{3,2,0,1:T(8,128)(2,1)} %bitcast.16), calls=%async_computation.2 | async-start | bytes 1327104 | tf_op jit(solution)/shard_map/all_to_all | solution.py:114
  168.7 8.3 %reduce-scatter.5.cloned.1.call-done = f32[864,1152]{1,0:T(8,128)} async-done(((f32[864,2304]{1,0:T(8,128)}), f32[864,1152]{1,0:T(8,128)}) %reduce-scatter.5.cloned.1.call-update) | async-done | bytes 3981328 | tf_op jit(solution)/shard_map/reduce_scatter | solution.py:111
  177.0 2.3 convert_element_type.201
  179.3 1.5 copy.69
  180.8 4.8 %all-to-all-start.3 = ((bf16[3,4,72,1152]{3,2,0,1:T(8,128)(2,1)}), bf16[3,4,72,1152]{3,2,0,1:T(8,128)(2,1)}, u32[]{:S(2)}, u32[]{:S(2)}) async-start(bf16[3,4,72,1152]{3,2,0,1:T(8,128)(2,1)} %copy.69), calls=%async_computation.5 | async-start | bytes 3981312 | tf_op jit(solution)/shard_map/all_to_all | solution.py:114
  185.6 5.7 %fusion.16 = bf16[1,384,2048]{2,1,0:T(8,128)(2,1)} fusion(bf16[864,2048]{1,0:T(8,128)(2,1)} %copy-done.7, bf16[288,2048]{1,0:T(8,128)(2,1)S(1)} %copy-done.13, bf16[864,384]{1,0:T(8,128)(2,1)} %get-tuple-element.48, bf16[288,384]{1,0:T(8,128)(2,1)S(1)} %copy-done.18), kind=kOutput, calls=%fused_computation.23 | convolution fusion | flops 1823932416 | bytes 7176192 | tf_op jit(solution)/shard_map/dot_general | solution.py:147
  191.4 3.9 %fusion.19 = bf16[1,2048,384]{2,1,0:T(8,128)(2,1)} fusion(bf16[864,2048]{1,0:T(8,128)(2,1)S(1)} %copy-done.6, bf16[288,2048]{1,0:T(8,128)(2,1)S(1)} %copy-done.11, bf16[864,384]{1,0:T(8,128)(2,1)S(1)} %get-tuple-element.46, bf16[288,384]{1,0:T(8,128)(2,1)S(1)} %copy-done.17), kind=kOutput, calls=%fused_computation.24 | convolution fusion | flops 1823932416 | bytes 7176192 | tf_op jit(solution)/shard_map/dot_general | solution.py:143
  195.3 3.9 %fusion.20 = bf16[1,2048,384]{2,1,0:T(8,128)(2,1)} fusion(bf16[864,2048]{1,0:T(8,128)(2,1)S(1)} %copy-done.6, bf16[288,2048]{1,0:T(8,128)(2,1)S(1)} %copy-done.11, bf16[864,384]{1,0:T(8,128)(2,1)S(1)} %get-tuple-element.47, bf16[288,384]{1,0:T(8,128)(2,1)S(1)} %copy-done.15), kind=kOutput, calls=%fused_computation.25 | convolution fusion | flops 1823932416 | bytes 7176192 | tf_op jit(solution)/shard_map/dot_general | solution.py:139
  199.9 10.3 %all-to-all-done.3 = bf16[3,4,72,1152]{3,2,0,1:T(8,128)(2,1)} async-done(((bf16[3,4,72,1152]{3,2,0,1:T(8,128)(2,1)}), bf16[3,4,72,1152]{3,2,0,1:T(8,128)(2,1)}, u32[]{:S(2)}, u32[]{:S(2)}) %all-to-all-start.3) | async-done | bytes 1990688 | tf_op jit(solution)/shard_map/all_to_all | solution.py:114
  210.2 1.7 copy.70
  212.1 0.6 fusion.42
  212.7 1.1 select_reduce_fusion
  214.1 3.4 %collective-permute-start.5 = (bf16[128,1152]{1,0:T(8,128)(2,1)S(1)}, bf16[128,1152]{1,0:T(8,128)(2,1)S(1)}, u32[]{:S(2)}, u32[]{:S(2)}) collective-permute-start(bf16[128,1152]{1,0:T(8,128)(2,1)S(1)} %get-tuple-element.56), channel_id=1, source_target_pairs={{0,24},{8,0},{16,8},{24,16},{1,25},{9,1},{17,9},{25,17},{2,26},{10... | collective-permute-start | bytes 884744 | tf_op jit(solution)/shard_map/ppermute | solution.py:130
  217.5 1.1 collective-permute-start.6
  219.0 6.0 %collective-permute-done.5 = bf16[128,1152]{1,0:T(8,128)(2,1)S(1)} collective-permute-done((bf16[128,1152]{1,0:T(8,128)(2,1)S(1)}, bf16[128,1152]{1,0:T(8,128)(2,1)S(1)}, u32[]{:S(2)}, u32[]{:S(2)}) %collective-permute-start.5) | collective-permute-done | bytes 294944 | tf_op jit(solution)/shard_map/ppermute | solution.py:130
  225.0 7.4 %collective-permute-done.7 = bf16[128,1152]{1,0:T(8,128)(2,1)S(1)} collective-permute-done((bf16[128,1152]{1,0:T(8,128)(2,1)S(1)}, bf16[128,1152]{1,0:T(8,128)(2,1)S(1)}, u32[]{:S(2)}, u32[]{:S(2)}) %collective-permute-start.7) | collective-permute-done | bytes 294944 | tf_op jit(solution)/shard_map/ppermute | solution.py:130
  232.4 10.0 %collective-permute-done.6 = bf16[128,1152]{1,0:T(8,128)(2,1)S(1)} collective-permute-done((bf16[128,1152]{1,0:T(8,128)(2,1)S(1)}, bf16[128,1152]{1,0:T(8,128)(2,1)S(1)}, u32[]{:S(2)}, u32[]{:S(2)}) %collective-permute-start.6) | collective-permute-done | bytes 294944 | tf_op jit(solution)/shard_map/ppermute | solution.py:130
  242.6 0.7 slice.134
  243.3 0.7 copy.72
  (77 shorter events, 5.5 us)
Async XLA Ops:
  7.2 124.0 %copy-start = (bf16[1,384,2048]{2,1,0:T(8,128)(2,1)S(1)}, bf16[1,384,2048]{2,1,0:T(8,128)(2,1)}, u32[]{:S(2)}) copy-start(bf16[1,384,2048]{2,1,0:T(8,128)(2,1)} %param.13) | copy-start | bytes 4718596
  10.8 18.8 %collective-permute-start.1 = (bf16[128,2176]{1,0:T(8,128)(2,1)}, bf16[128,2176]{1,0:T(8,128)(2,1)S(1)}, u32[]{:S(2)}, u32[]{:S(2)}) collective-permute-start(bf16[128,2176]{1,0:T(8,128)(2,1)} %get-tuple-element.60), channel_id=1, source_target_pairs={{0,8},{8,16},{16,24},{24,0},{1,9},{9,17},{17,25},{25,1},{2,10},{10... | collective-permute-start | bytes 1671176 | tf_op jit(solution)/shard_map/ppermute | solution.py:25
  13.8 26.3 %collective-permute-start.3 = (bf16[128,2176]{1,0:T(8,128)(2,1)}, bf16[128,2176]{1,0:T(8,128)(2,1)}, u32[]{:S(2)}, u32[]{:S(2)}) collective-permute-start(bf16[128,2176]{1,0:T(8,128)(2,1)} %get-tuple-element.60), channel_id=1, source_target_pairs={{0,24},{8,0},{16,8},{24,16},{1,25},{9,1},{17,9},{25,17},{2,26},{10... | collective-permute-start | bytes 1671176 | tf_op jit(solution)/shard_map/ppermute | solution.py:25
  15.9 48.8 %collective-permute-start.2 = (bf16[128,2176]{1,0:T(8,128)(2,1)}, bf16[128,2176]{1,0:T(8,128)(2,1)}, u32[]{:S(2)}, u32[]{:S(2)}) collective-permute-start(bf16[128,2176]{1,0:T(8,128)(2,1)} %get-tuple-element.60), channel_id=1, source_target_pairs={{0,16},{8,24},{16,0},{24,8},{1,17},{9,25},{17,1},{25,9},{2,18},{10... | collective-permute-start | bytes 1671176 | tf_op jit(solution)/shard_map/ppermute | solution.py:25
  19.9 57.5 %all-to-all-start = ((bf16[1,4,72,2176]{3,2,0,1:T(8,128)(2,1)}), bf16[1,4,72,2176]{3,2,0,1:T(8,128)(2,1)S(1)}, u32[]{:S(2)}, u32[]{:S(2)}) async-start(bf16[1,4,72,2176]{3,2,0,1:T(8,128)(2,1)} %bitcast.135), calls=%async_computation | async-start | bytes 2506752 | tf_op jit(solution)/shard_map/all_to_all | solution.py:64
  72.8 2.5 copy-start.8
  77.4 48.0 %all-to-all-start.2 = ((bf16[3,4,72,2176]{3,2,0,1:T(8,128)(2,1)}), bf16[3,4,72,2176]{3,2,0,1:T(8,128)(2,1)}, u32[]{:S(2)}, u32[]{:S(2)}) async-start(bf16[3,4,72,2176]{3,2,0,1:T(8,128)(2,1)} %copy.66), calls=%async_computation.3 | async-start | bytes 7520256 | tf_op jit(solution)/shard_map/all_to_all | solution.py:64
  82.1 80.8 %reduce-scatter.3.cloned.1.call-start = ((), (), s32[]{:S(2)}) async-start(), calls=%async_computation.6 | async-start | bytes 3981312 | tf_op jit(solution)/shard_map/reduce_scatter | solution.py:111
  82.2 47.5 %collective-permute-start = (bf16[288,2176]{1,0:T(8,128)(2,1)S(1)}, bf16[288,2176]{1,0:T(8,128)(2,1)}, u32[]{:S(2)}, u32[]{:S(2)}) collective-permute-start(bf16[288,2176]{1,0:T(8,128)(2,1)S(1)} %bitcast.125), channel_id=1, source_target_pairs={{0,1},{1,0},{2,3},{3,2},{4,5},{5,4},{6,7},{7,6},{8,9},{9,8},{10,11... | collective-permute-start | bytes 3760136 | tf_op jit(solution)/shard_map/ppermute | solution.py:67
  129.5 12.6 %collective-permute-start.4 = (bf16[864,2176]{1,0:T(8,128)(2,1)}, bf16[864,2176]{1,0:T(8,128)(2,1)}, u32[]{:S(2)}, u32[]{:S(2)}) collective-permute-start(bf16[864,2176]{1,0:T(8,128)(2,1)} %bitcast.27), channel_id=1, source_target_pairs={{0,1},{1,0},{2,3},{3,2},{4,5},{5,4},{6,7},{7,6},{8,9},{9,8},{10,11... | collective-permute-start | bytes 11280392 | tf_op jit(solution)/shard_map/ppermute | solution.py:67
  131.2 1.0 copy-start.12
  131.2 3.1 %copy-start.10 = (bf16[288,2048]{1,0:T(8,128)(2,1)}, bf16[288,2048]{1,0:T(8,128)(2,1)S(1)}, u32[]{:S(2)}) copy-start(bf16[288,2048]{1,0:T(8,128)(2,1)S(1)} %get-tuple-element.50) | copy-start | bytes 3538948
  131.2 2.2 copy-start.3
  133.5 1.4 copy-start.2
  136.5 0.8 copy-start.14
  136.6 1.8 copy-start.16
  140.6 36.4 %reduce-scatter.5.cloned.1.call-start = ((), (), s32[]{:S(2)}) async-start(), calls=%async_computation.7 | async-start | bytes 11943936 | tf_op jit(solution)/shard_map/reduce_scatter | solution.py:111
  146.4 2.0 copy-start.7
  146.4 4.7 %copy-start.5 = (bf16[864,2048]{1,0:T(8,128)(2,1)}, bf16[864,2048]{1,0:T(8,128)(2,1)S(1)}, u32[]{:S(2)}) copy-start(bf16[864,2048]{1,0:T(8,128)(2,1)S(1)} %get-tuple-element.44) | copy-start | bytes 10616836
  146.4 2.7 %copy-start.4 = (bf16[1,2048,384]{2,1,0:T(8,128)(2,1)S(1)}, bf16[1,2048,384]{2,1,0:T(8,128)(2,1)}, u32[]{:S(2)}) copy-start(bf16[1,2048,384]{2,1,0:T(8,128)(2,1)} %param.12) | copy-start | bytes 4718596
  165.2 15.6 %all-to-all-start.1 = ((bf16[1,4,72,1152]{3,2,0,1:T(8,128)(2,1)}), bf16[1,4,72,1152]{3,2,0,1:T(8,128)(2,1)S(1)}, u32[]{:S(2)}, u32[]{:S(2)}) async-start(bf16[1,4,72,1152]{3,2,0,1:T(8,128)(2,1)} %bitcast.16), calls=%async_computation.2 | async-start | bytes 1327104 | tf_op jit(solution)/shard_map/all_to_all | solution.py:114
  180.8 4.8 %copy-start.13 = (bf16[288,2048]{1,0:T(8,128)(2,1)S(1)}, bf16[288,2048]{1,0:T(8,128)(2,1)}, u32[]{:S(2)}) copy-start(bf16[288,2048]{1,0:T(8,128)(2,1)} %copy-done.12) | copy-start | bytes 3538948
  180.8 4.8 %copy-start.18 = (bf16[288,384]{1,0:T(8,128)(2,1)S(1)}, bf16[288,384]{1,0:T(8,128)(2,1)}, u32[]{:S(2)}) copy-start(bf16[288,384]{1,0:T(8,128)(2,1)} %get-tuple-element.54) | copy-start | bytes 663556
  180.8 29.4 %all-to-all-start.3 = ((bf16[3,4,72,1152]{3,2,0,1:T(8,128)(2,1)}), bf16[3,4,72,1152]{3,2,0,1:T(8,128)(2,1)}, u32[]{:S(2)}, u32[]{:S(2)}) async-start(bf16[3,4,72,1152]{3,2,0,1:T(8,128)(2,1)} %copy.69), calls=%async_computation.5 | async-start | bytes 3981312 | tf_op jit(solution)/shard_map/all_to_all | solution.py:114
  185.6 5.8 %copy-start.6 = (bf16[864,2048]{1,0:T(8,128)(2,1)S(1)}, bf16[864,2048]{1,0:T(8,128)(2,1)}, u32[]{:S(2)}) copy-start(bf16[864,2048]{1,0:T(8,128)(2,1)} %copy-done.5) | copy-start | bytes 10616836
  185.6 5.8 %copy-start.11 = (bf16[288,2048]{1,0:T(8,128)(2,1)S(1)}, bf16[288,2048]{1,0:T(8,128)(2,1)}, u32[]{:S(2)}) copy-start(bf16[288,2048]{1,0:T(8,128)(2,1)} %copy-done.10) | copy-start | bytes 3538948
  185.6 5.8 %copy-start.17 = (bf16[288,384]{1,0:T(8,128)(2,1)S(1)}, bf16[288,384]{1,0:T(8,128)(2,1)}, u32[]{:S(2)}) copy-start(bf16[288,384]{1,0:T(8,128)(2,1)} %copy-done.16) | copy-start | bytes 663556
  191.4 3.9 %copy-start.15 = (bf16[288,384]{1,0:T(8,128)(2,1)S(1)}, bf16[288,384]{1,0:T(8,128)(2,1)}, u32[]{:S(2)}) copy-start(bf16[288,384]{1,0:T(8,128)(2,1)} %copy-done.14) | copy-start | bytes 663556
  199.9 12.2 %copy-start.9 = (bf16[3,288,128]{2,1,0:T(8,128)(2,1)S(1)}, bf16[3,288,128]{2,1,0:T(8,128)(2,1)}, u32[]{:S(2)}) copy-start(bf16[3,288,128]{2,1,0:T(8,128)(2,1)} %copy-done.8) | copy-start | bytes 663556
  214.0 29.9 %copy-start.1 = (bf16[1,384,2048]{2,1,0:T(8,128)(2,1)S(1)}, bf16[1,384,2048]{2,1,0:T(8,128)(2,1)}, u32[]{:S(2)}) copy-start(bf16[1,384,2048]{2,1,0:T(8,128)(2,1)} %param.13) | copy-start | bytes 4718596
  214.1 10.9 %collective-permute-start.5 = (bf16[128,1152]{1,0:T(8,128)(2,1)S(1)}, bf16[128,1152]{1,0:T(8,128)(2,1)S(1)}, u32[]{:S(2)}, u32[]{:S(2)}) collective-permute-start(bf16[128,1152]{1,0:T(8,128)(2,1)S(1)} %get-tuple-element.56), channel_id=1, source_target_pairs={{0,24},{8,0},{16,8},{24,16},{1,25},{9,1},{17,9},{25,17},{2,26},{10... | collective-permute-start | bytes 884744 | tf_op jit(solution)/shard_map/ppermute | solution.py:130
  217.5 14.9 %collective-permute-start.7 = (bf16[128,1152]{1,0:T(8,128)(2,1)S(1)}, bf16[128,1152]{1,0:T(8,128)(2,1)S(1)}, u32[]{:S(2)}, u32[]{:S(2)}) collective-permute-start(bf16[128,1152]{1,0:T(8,128)(2,1)S(1)} %get-tuple-element.57), channel_id=1, source_target_pairs={{0,8},{8,16},{16,24},{24,0},{1,9},{9,17},{17,25},{25,1},{2,10},{10... | collective-permute-start | bytes 884744 | tf_op jit(solution)/shard_map/ppermute | solution.py:130
  217.5 24.9 %collective-permute-start.6 = (bf16[128,1152]{1,0:T(8,128)(2,1)S(1)}, bf16[128,1152]{1,0:T(8,128)(2,1)S(1)}, u32[]{:S(2)}, u32[]{:S(2)}) collective-permute-start(bf16[128,1152]{1,0:T(8,128)(2,1)S(1)} %get-tuple-element.58), channel_id=1, source_target_pairs={{0,16},{8,24},{16,0},{24,8},{1,17},{9,25},{17,1},{25,9},{2,18},{10... | collective-permute-start | bytes 884744 | tf_op jit(solution)/shard_map/ppermute | solution.py:130
Sparse Core Ops, SparseCore 0:
  140.8 7.6 reduce-scatter.2
  163.1 13.8 reduce-scatter.4

commit v11 on v10

--- a/solution.py
+++ b/solution.py
@@ -55,14 +55,15 @@
         key = jnp.where(in_plane, local_ex * capacity + position, -1).reshape(n_mem, tok_rows, top_count)
         match = key[:, None, :, :] == q_iota[None, :, None, None]
         select = jnp.sum(match.astype(jnp.bfloat16), axis=3)
+        select4 = select.reshape(n_mem, n_ex, capacity, tok_rows)
         send = jnp.einsum(
-            "mqt,mtf->mqf", select, stacked, preferred_element_type=jnp.float32
+            "mjpt,mtf->jmpf", select4, stacked, preferred_element_type=jnp.float32
         ).astype(tokens.dtype)
 
         if gi >= 2:
             send = lax.optimization_barrier((send, anchors[gi - 2]))[0]
         recv = lax.all_to_all(
-            send.reshape(n_mem, n_ex, capacity, features + lanes), "expert", split_axis=1, concat_axis=1, tiled=True
+            send, "expert", split_axis=0, concat_axis=0, tiled=True
         ).reshape(n_mem * block_slots, features + lanes)
         other = lax.ppermute(recv, "tensor", [(0, 1), (1, 0)])
         mine_x = core == 0
@@ -112,14 +113,15 @@
             jnp.concatenate(pieces, axis=1), "tensor", scatter_dimension=1, tiled=True
         ).astype(jnp.bfloat16)
         back = lax.all_to_all(
-            ret.reshape(n_mem, n_ex, capacity, half + lanes), "expert", split_axis=1, concat_axis=1, tiled=True
-        ).reshape(n_mem, block_slots, half + lanes)
+            ret.reshape(n_ex, n_mem, capacity, half + lanes), "expert", split_axis=0, concat_axis=0, tiled=True
+        )
 
         col_grad = jnp.einsum(
-            "mqt,mqf->mtf", select, back[:, :, :half], preferred_element_type=jnp.float32
+            "mjpt,jmpf->mtf", select4, back[:, :, :, :half], preferred_element_type=jnp.float32
         )
+        back_gate = jnp.transpose(back[:, :, :, half], (1, 0, 2)).reshape(n_mem, block_slots)
         col_gate = jnp.sum(
-            jnp.where(match, back[:, :, half].astype(jnp.float32)[:, :, None, None], 0.0), axis=1
+            jnp.where(match, back_gate.astype(jnp.float32)[:, :, None, None], 0.0), axis=1
         )
         parts = jnp.concatenate(
             [col_grad, jnp.pad(col_gate, ((0, 0), (0, 0), (0, lanes - top_count)))], axis=2

time: 252 us -> 251 us (level)
  local copies, waits for them, and re-layouts: 17.5 us -> 12.4 us
  other arithmetic: 28 us -> 30.8 us
    all_to_all x2 -> x0, local copies, waits for them, and re-layouts: 5.89 us -> none  [the longest x1 4.18 us: on_device(): lax.all_to_all(send.reshape(n_mem, n_ex, capacity, features + lanes), 'ex...]
    reshape x2 -> x0, local copies, waits for them, and re-layouts: 3.57 us -> none  [the longest x1 2.1 us: on_device(): send.reshape(n_mem, n_ex, capacity, features + lanes)]
    unnamed x40 -> x43, local copies, waits for them, and re-layouts: 3.57 us -> 5.61 us
  transfers between devices with their start and end apart: 14 -> 14, of which waited for: 9 -> 9; matrix products, arithmetic and copies ran while one was open for 28% -> 27% of each run, Pallas kernels for 0% -> 0%
where the time goes in v11:
time: 251 us; the launch traced here: 250 us
  waiting for transfers between devices  126 us (50%)
  matrix products  38.3 us (15%)
  other arithmetic  30.8 us (12%)
  starting transfers between devices  27.7 us (11%)
  between operations  14.6 us (6%)
  local copies, waits for them, and re-layouts  12.4 us (5%)
    all_to_all x2, waiting for transfers between devices, on_device(): lax.all_to_all(send, 'expert', split_axis=0, concat_axis=0, tiled=True)  43.1 us
    ppermute x3, waiting for transfers between devices, on_device(): lax.ppermute(ext, 'dp', [(i, (i + s) % n_dp) for i in range(n_dp)])  41 us
    ppermute x3, waiting for transfers between devices, on_device(): part = lax.ppermute(part, 'dp', [(i, (i - s) % n_dp) for i in range(n_dp)])  23.4 us
    all_to_all x2, waiting for transfers between devices, on_device(): lax.all_to_all(ret.reshape(n_ex, n_mem, capacity, half + lanes), 'expert'...  10.3 us
    all_to_all x2, starting transfers between devices, on_device(): lax.all_to_all(send, 'expert', split_axis=0, concat_axis=0, tiled=True)  8.48 us
    reduce_scatter x2, waiting for transfers between devices, on_device(): lax.psum_scatter(jnp.concatenate(pieces, axis=1), 'tensor', scatter_dimen...  8.3 us
    all_to_all x2, starting transfers between devices, on_device(): lax.all_to_all(ret.reshape(n_ex, n_mem, capacity, half + lanes), 'expert'...  8.26 us
    ppermute x3, starting transfers between devices, on_device(): lax.ppermute(ext, 'dp', [(i, (i + s) % n_dp) for i in range(n_dp)])  6.06 us
  transfers between devices with their start and end apart: 14, of which 9 were waited for; matrix products, arithmetic and copies ran while one was open for 27% of the time, Pallas kernels for 0%

profile of v11, /device:TPU:0, one launch (start us, length us, event | category | flops | bytes accessed | tf_op | source)
XLA Modules:
  0.0 249.8 jit_solution(7902237284065785356)
XLA Ops:
  7.2 0.8 convert_element_type.187
  8.0 0.7 pad_maximum_fusion.14
  8.8 1.1 broadcast_select_fusion.4
  9.9 0.9 fusion.105
  10.8 3.0 %collective-permute-start.1 = (bf16[128,2176]{1,0:T(8,128)(2,1)}, bf16[128,2176]{1,0:T(8,128)(2,1)S(1)}, u32[]{:S(2)}, u32[]{:S(2)}) collective-permute-start(bf16[128,2176]{1,0:T(8,128)(2,1)} %get-tuple-element.50), channel_id=1, source_target_pairs={{0,8},{8,16},{16,24},{24,0},{1,9},{9,17},{17,25},{25,1},{2,10},{10... | collective-permute-start | bytes 1671176 | tf_op jit(solution)/shard_map/ppermute | solution.py:25
  13.8 2.0 collective-permute-start.3
  15.9 1.0 collective-permute-start.2
  17.0 0.8 fusion.59
  18.4 1.5 fusion.9
  19.9 3.7 %all-to-all-start = ((bf16[4,1,72,2176]{3,2,1,0:T(8,128)(2,1)}), bf16[4,1,72,2176]{3,2,1,0:T(8,128)(2,1)S(1)}, u32[]{:S(2)}, u32[]{:S(2)}) async-start(bf16[4,1,72,2176]{3,2,1,0:T(8,128)(2,1)} %fusion.9), calls=%async_computation | async-start | bytes 2506752 | tf_op jit(solution)/shard_map/all_to_all | solution.py:65
  23.6 5.9 %collective-permute-done.1 = bf16[128,2176]{1,0:T(8,128)(2,1)S(1)} collective-permute-done((bf16[128,2176]{1,0:T(8,128)(2,1)}, bf16[128,2176]{1,0:T(8,128)(2,1)S(1)}, u32[]{:S(2)}, u32[]{:S(2)}) %collective-permute-start.1) | collective-permute-done | bytes 557088 | tf_op jit(solution)/shard_map/ppermute | solution.py:25
  29.6 10.6 %collective-permute-done.3 = bf16[128,2176]{1,0:T(8,128)(2,1)} collective-permute-done((bf16[128,2176]{1,0:T(8,128)(2,1)}, bf16[128,2176]{1,0:T(8,128)(2,1)}, u32[]{:S(2)}, u32[]{:S(2)}) %collective-permute-start.3) | collective-permute-done | bytes 557088 | tf_op jit(solution)/shard_map/ppermute | solution.py:25
  40.2 24.4 %collective-permute-done.2 = bf16[128,2176]{1,0:T(8,128)(2,1)} collective-permute-done((bf16[128,2176]{1,0:T(8,128)(2,1)}, bf16[128,2176]{1,0:T(8,128)(2,1)}, u32[]{:S(2)}, u32[]{:S(2)}) %collective-permute-start.2) | collective-permute-done | bytes 557088 | tf_op jit(solution)/shard_map/ppermute | solution.py:25
  64.6 1.4 pad_maximum_fusion.13
  66.1 1.2 copy-done.8
  67.2 0.7 convert_subtract_fusion
  68.0 1.1 sub.48
  69.0 0.5 fusion.54
  69.6 0.8 convert_element_type.208
  70.4 1.7 add_select_fusion
  72.1 1.0 copy.54
  73.1 1.6 fusion.23
  74.7 0.7 copy-done.17
  75.4 2.4 fusion.4
  77.8 2.1 copy.55
  79.9 4.8 %all-to-all-start.2 = ((bf16[4,3,72,2176]{3,2,1,0:T(8,128)(2,1)}), bf16[4,3,72,2176]{3,2,1,0:T(8,128)(2,1)}, u32[]{:S(2)}, u32[]{:S(2)}) async-start(bf16[4,3,72,2176]{3,2,1,0:T(8,128)(2,1)} %copy.55), calls=%async_computation.3 | async-start | bytes 7520256 | tf_op jit(solution)/shard_map/all_to_all | solution.py:65
  84.8 43.1 %all-to-all-done.2 = bf16[4,3,72,2176]{3,2,1,0:T(8,128)(2,1)} async-done(((bf16[4,3,72,2176]{3,2,1,0:T(8,128)(2,1)}), bf16[4,3,72,2176]{3,2,1,0:T(8,128)(2,1)}, u32[]{:S(2)}, u32[]{:S(2)}) %all-to-all-start.2) | async-done | bytes 3760160 | tf_op jit(solution)/shard_map/all_to_all | solution.py:65
  128.1 1.4 broadcast_select_fusion.2
  129.6 0.8 fusion.38
  130.5 1.3 copy-done.3
  131.8 0.8 fusion.34
  132.6 0.6 copy-done.2
  133.2 1.7 multiply_convert_fusion.4
  137.2 1.7 pad_maximum_fusion.8
  139.2 1.3 select_reduce_fusion.2
  140.6 4.2 %broadcast_select_fusion = (bf16[864,2048]{1,0:T(8,128)(2,1)S(1)}, bf16[864,2048]{1,0:T(8,128)(2,1)S(1)}) fusion(pred[]{:T(512)S(6)} %eq.96, bf16[864,2176]{1,0:T(8,128)(2,1)} %bitcast.34, bf16[864,2176]{1,0:T(8,128)(2,1)} %collective-permute-done.4), kind=kLoop, calls=%fused_computation.17 | loop fusion | flops 3538944 | bytes 14155777 | tf_op jit(solution)/shard_map/jit(_where)/select_n | solution.py:70
  144.8 2.0 fusion.36
  146.8 0.6 copy-done.4
  147.5 2.0 fusion.32
  149.5 3.4 %multiply_convert_fusion.1 = (bf16[864,384]{1,0:T(8,128)(2,1)S(1)}, bf16[864,384]{1,0:T(8,128)(2,1)S(1)}, bf16[864,384]{1,0:T(8,128)(2,1)}, bf16[864,384]{1,0:T(8,128)(2,1)S(1)}) fusion(f32[864,384]{1,0:T(8,128)S(1)} %fusion.36, f32[864]{0:T(1024)S(1)} %select_reduce_fusion.2, f32[864,384]{1,0:T(8,128)S(1)} %fusion.32, ...), kind=kOutput, calls=%fused_computation.57 | convolution fusion | flops 1365258240 | bytes 10423680 | tf_op jit(solution)/shard_map/dot_general | solution.py:77
  153.4 1.1 fusion.72
  154.5 1.1 fusion.78
  155.6 1.1 convolution_add_fusion
  156.7 1.1 convolution_add_fusion.1
  157.9 3.4 %pad_maximum_fusion = f32[864,2304]{1,0:T(8,128)} fusion(f32[864,128]{1,0:T(8,128)S(1)} %pad.25, f32[864,1024]{1,0:T(8,128)S(1)} %convolution_add_fusion, f32[864,1024]{1,0:T(8,128)S(1)} %convolution_add_fusion.1), kind=kLoop, calls=%fused_computation | loop fusion | flops 5971968 | bytes 15482880 | tf_op jit(solution)/shard_map/concatenate | solution.py:113
  161.4 2.2 convert_element_type.202
  163.6 3.5 %all-to-all-start.1 = ((bf16[4,1,72,1152]{3,2,1,0:T(8,128)(2,1)}), bf16[4,1,72,1152]{3,2,1,0:T(8,128)(2,1)S(1)}, u32[]{:S(2)}, u32[]{:S(2)}) async-start(bf16[4,1,72,1152]{3,2,1,0:T(8,128)(2,1)} %bitcast.19), calls=%async_computation.2 | async-start | bytes 1327104 | tf_op jit(solution)/shard_map/all_to_all | solution.py:115
  167.1 8.3 %reduce-scatter.5.cloned.1.call-done = f32[864,1152]{1,0:T(8,128)} async-done(((f32[864,2304]{1,0:T(8,128)}), f32[864,1152]{1,0:T(8,128)}) %reduce-scatter.5.cloned.1.call-update) | async-done | bytes 3981328 | tf_op jit(solution)/shard_map/reduce_scatter | solution.py:112
  175.4 3.6 %convert_element_type.218 = bf16[864,1152]{1,0:T(8,128)(2,1)} convert(f32[864,1152]{1,0:T(8,128)} %reduce-scatter.5.cloned.1.call-done) | non-fusion elementwise | flops 995328 | bytes 5971968 | tf_op jit(solution)/shard_map/convert_element_type | solution.py:114
  179.0 4.8 %all-to-all-start.3 = ((bf16[4,3,72,1152]{3,2,1,0:T(8,128)(2,1)}), bf16[4,3,72,1152]{3,2,1,0:T(8,128)(2,1)}, u32[]{:S(2)}, u32[]{:S(2)}) async-start(bf16[4,3,72,1152]{3,2,1,0:T(8,128)(2,1)} %bitcast.149), calls=%async_computation.5 | async-start | bytes 3981312 | tf_op jit(solution)/shard_map/all_to_all | solution.py:115
  183.9 5.7 %fusion.18 = bf16[1,384,2048]{2,1,0:T(8,128)(2,1)} fusion(bf16[864,2048]{1,0:T(8,128)(2,1)} %copy-done.7, bf16[288,2048]{1,0:T(8,128)(2,1)S(1)} %copy-done.12, bf16[864,384]{1,0:T(8,128)(2,1)} %get-tuple-element.38, bf16[288,384]{1,0:T(8,128)(2,1)S(1)} %copy-done.19), kind=kOutput, calls=%fused_computation.25 | convolution fusion | flops 1823932416 | bytes 7176192 | tf_op jit(solution)/shard_map/dot_general | solution.py:149
  189.6 3.9 %fusion.21 = bf16[1,2048,384]{2,1,0:T(8,128)(2,1)} fusion(bf16[864,2048]{1,0:T(8,128)(2,1)S(1)} %copy-done.6, bf16[288,2048]{1,0:T(8,128)(2,1)S(1)} %copy-done.10, bf16[864,384]{1,0:T(8,128)(2,1)S(1)} %get-tuple-element.36, bf16[288,384]{1,0:T(8,128)(2,1)S(1)} %copy-done.16), kind=kOutput, calls=%fused_computation.26 | convolution fusion | flops 1823932416 | bytes 7176192 | tf_op jit(solution)/shard_map/dot_general | solution.py:145
  193.5 3.9 %fusion.22 = bf16[1,2048,384]{2,1,0:T(8,128)(2,1)} fusion(bf16[864,2048]{1,0:T(8,128)(2,1)S(1)} %copy-done.6, bf16[288,2048]{1,0:T(8,128)(2,1)S(1)} %copy-done.10, bf16[864,384]{1,0:T(8,128)(2,1)S(1)} %get-tuple-element.37, bf16[288,384]{1,0:T(8,128)(2,1)S(1)} %copy-done.14), kind=kOutput, calls=%fused_computation.27 | convolution fusion | flops 1823932416 | bytes 7176192 | tf_op jit(solution)/shard_map/dot_general | solution.py:141
  198.2 10.2 %all-to-all-done.3 = bf16[4,3,72,1152]{3,2,1,0:T(8,128)(2,1)} async-done(((bf16[4,3,72,1152]{3,2,1,0:T(8,128)(2,1)}), bf16[4,3,72,1152]{3,2,1,0:T(8,128)(2,1)}, u32[]{:S(2)}, u32[]{:S(2)}) %all-to-all-start.3) | async-done | bytes 1990688 | tf_op jit(solution)/shard_map/all_to_all | solution.py:115
  208.4 1.0 slice_convert_fusion
  209.6 1.1 select_reduce_fusion
  210.9 2.1 bitcast_convert_fusion
  213.2 3.4 %collective-permute-start.5 = (bf16[128,1152]{1,0:T(8,128)(2,1)S(1)}, bf16[128,1152]{1,0:T(8,128)(2,1)S(1)}, u32[]{:S(2)}, u32[]{:S(2)}) collective-permute-start(bf16[128,1152]{1,0:T(8,128)(2,1)S(1)} %get-tuple-element.46), channel_id=1, source_target_pairs={{0,24},{8,0},{16,8},{24,16},{1,25},{9,1},{17,9},{25,17},{2,26},{10... | collective-permute-start | bytes 884744 | tf_op jit(solution)/shard_map/ppermute | solution.py:132
  216.6 1.1 collective-permute-start.6
  218.0 6.0 %collective-permute-done.5 = bf16[128,1152]{1,0:T(8,128)(2,1)S(1)} collective-permute-done((bf16[128,1152]{1,0:T(8,128)(2,1)S(1)}, bf16[128,1152]{1,0:T(8,128)(2,1)S(1)}, u32[]{:S(2)}, u32[]{:S(2)}) %collective-permute-start.5) | collective-permute-done | bytes 294944 | tf_op jit(solution)/shard_map/ppermute | solution.py:132
  224.1 7.4 %collective-permute-done.7 = bf16[128,1152]{1,0:T(8,128)(2,1)S(1)} collective-permute-done((bf16[128,1152]{1,0:T(8,128)(2,1)S(1)}, bf16[128,1152]{1,0:T(8,128)(2,1)S(1)}, u32[]{:S(2)}, u32[]{:S(2)}) %collective-permute-start.7) | collective-permute-done | bytes 294944 | tf_op jit(solution)/shard_map/ppermute | solution.py:132
  231.5 10.0 %collective-permute-done.6 = bf16[128,1152]{1,0:T(8,128)(2,1)S(1)} collective-permute-done((bf16[128,1152]{1,0:T(8,128)(2,1)S(1)}, bf16[128,1152]{1,0:T(8,128)(2,1)S(1)}, u32[]{:S(2)}, u32[]{:S(2)}) %collective-permute-start.6) | collective-permute-done | bytes 294944 | tf_op jit(solution)/shard_map/ppermute | solution.py:132
  241.6 0.7 slice.135
  242.3 0.7 copy.60
  (81 shorter events, 6.2 us)
Async XLA Ops:
  7.2 122.4 %copy-start = (bf16[1,384,2048]{2,1,0:T(8,128)(2,1)S(1)}, bf16[1,384,2048]{2,1,0:T(8,128)(2,1)}, u32[]{:S(2)}) copy-start(bf16[1,384,2048]{2,1,0:T(8,128)(2,1)} %param.13) | copy-start | bytes 4718596
  10.8 18.8 %collective-permute-start.1 = (bf16[128,2176]{1,0:T(8,128)(2,1)}, bf16[128,2176]{1,0:T(8,128)(2,1)S(1)}, u32[]{:S(2)}, u32[]{:S(2)}) collective-permute-start(bf16[128,2176]{1,0:T(8,128)(2,1)} %get-tuple-element.50), channel_id=1, source_target_pairs={{0,8},{8,16},{16,24},{24,0},{1,9},{9,17},{17,25},{25,1},{2,10},{10... | collective-permute-start | bytes 1671176 | tf_op jit(solution)/shard_map/ppermute | solution.py:25
  13.8 26.3 %collective-permute-start.3 = (bf16[128,2176]{1,0:T(8,128)(2,1)}, bf16[128,2176]{1,0:T(8,128)(2,1)}, u32[]{:S(2)}, u32[]{:S(2)}) collective-permute-start(bf16[128,2176]{1,0:T(8,128)(2,1)} %get-tuple-element.50), channel_id=1, source_target_pairs={{0,24},{8,0},{16,8},{24,16},{1,25},{9,1},{17,9},{25,17},{2,26},{10... | collective-permute-start | bytes 1671176 | tf_op jit(solution)/shard_map/ppermute | solution.py:25
  15.9 48.8 %collective-permute-start.2 = (bf16[128,2176]{1,0:T(8,128)(2,1)}, bf16[128,2176]{1,0:T(8,128)(2,1)}, u32[]{:S(2)}, u32[]{:S(2)}) collective-permute-start(bf16[128,2176]{1,0:T(8,128)(2,1)} %get-tuple-element.50), channel_id=1, source_target_pairs={{0,16},{8,24},{16,0},{24,8},{1,17},{9,25},{17,1},{25,9},{2,18},{10... | collective-permute-start | bytes 1671176 | tf_op jit(solution)/shard_map/ppermute | solution.py:25
  19.9 60.0 %all-to-all-start = ((bf16[4,1,72,2176]{3,2,1,0:T(8,128)(2,1)}), bf16[4,1,72,2176]{3,2,1,0:T(8,128)(2,1)S(1)}, u32[]{:S(2)}, u32[]{:S(2)}) async-start(bf16[4,1,72,2176]{3,2,1,0:T(8,128)(2,1)} %fusion.9), calls=%async_computation | async-start | bytes 2506752 | tf_op jit(solution)/shard_map/all_to_all | solution.py:65
  66.0 1.2 copy-start.8
  74.7 0.7 copy-start.17
  79.9 48.0 %all-to-all-start.2 = ((bf16[4,3,72,2176]{3,2,1,0:T(8,128)(2,1)}), bf16[4,3,72,2176]{3,2,1,0:T(8,128)(2,1)}, u32[]{:S(2)}, u32[]{:S(2)}) async-start(bf16[4,3,72,2176]{3,2,1,0:T(8,128)(2,1)} %copy.55), calls=%async_computation.3 | async-start | bytes 7520256 | tf_op jit(solution)/shard_map/all_to_all | solution.py:65
  84.7 76.7 %reduce-scatter.3.cloned.1.call-start = ((), (), s32[]{:S(2)}) async-start(), calls=%async_computation.6 | async-start | bytes 3981312 | tf_op jit(solution)/shard_map/reduce_scatter | solution.py:112
  84.7 43.4 %collective-permute-start = (bf16[288,2176]{1,0:T(8,128)(2,1)S(1)}, bf16[288,2176]{1,0:T(8,128)(2,1)}, u32[]{:S(2)}, u32[]{:S(2)}) collective-permute-start(bf16[288,2176]{1,0:T(8,128)(2,1)S(1)} %bitcast.150), channel_id=1, source_target_pairs={{0,1},{1,0},{2,3},{3,2},{4,5},{5,4},{6,7},{7,6},{8,9},{9,8},{10,11... | collective-permute-start | bytes 3760136 | tf_op jit(solution)/shard_map/ppermute | solution.py:68
  127.9 12.7 %collective-permute-start.4 = (bf16[864,2176]{1,0:T(8,128)(2,1)}, bf16[864,2176]{1,0:T(8,128)(2,1)}, u32[]{:S(2)}, u32[]{:S(2)}) collective-permute-start(bf16[864,2176]{1,0:T(8,128)(2,1)} %bitcast.34), channel_id=1, source_target_pairs={{0,1},{1,0},{2,3},{3,2},{4,5},{5,4},{6,7},{7,6},{8,9},{9,8},{10,11... | collective-permute-start | bytes 11280392 | tf_op jit(solution)/shard_map/ppermute | solution.py:68
  129.5 1.0 copy-start.11
  129.5 3.1 %copy-start.9 = (bf16[288,2048]{1,0:T(8,128)(2,1)}, bf16[288,2048]{1,0:T(8,128)(2,1)S(1)}, u32[]{:S(2)}) copy-start(bf16[288,2048]{1,0:T(8,128)(2,1)S(1)} %get-tuple-element.40) | copy-start | bytes 3538948
  129.6 2.2 copy-start.3
  131.8 1.4 copy-start.2
  134.9 1.3 copy-start.13
  134.9 1.8 copy-start.15
  139.0 36.4 %reduce-scatter.5.cloned.1.call-start = ((), (), s32[]{:S(2)}) async-start(), calls=%async_computation.7 | async-start | bytes 11943936 | tf_op jit(solution)/shard_map/reduce_scatter | solution.py:112
  144.8 2.0 copy-start.7
  144.8 4.7 %copy-start.5 = (bf16[864,2048]{1,0:T(8,128)(2,1)}, bf16[864,2048]{1,0:T(8,128)(2,1)S(1)}, u32[]{:S(2)}) copy-start(bf16[864,2048]{1,0:T(8,128)(2,1)S(1)} %get-tuple-element.34) | copy-start | bytes 10616836
  144.8 2.7 %copy-start.4 = (bf16[1,2048,384]{2,1,0:T(8,128)(2,1)S(1)}, bf16[1,2048,384]{2,1,0:T(8,128)(2,1)}, u32[]{:S(2)}) copy-start(bf16[1,2048,384]{2,1,0:T(8,128)(2,1)} %param.12) | copy-start | bytes 4718596
  163.6 15.4 %all-to-all-start.1 = ((bf16[4,1,72,1152]{3,2,1,0:T(8,128)(2,1)}), bf16[4,1,72,1152]{3,2,1,0:T(8,128)(2,1)S(1)}, u32[]{:S(2)}, u32[]{:S(2)}) async-start(bf16[4,1,72,1152]{3,2,1,0:T(8,128)(2,1)} %bitcast.19), calls=%async_computation.2 | async-start | bytes 1327104 | tf_op jit(solution)/shard_map/all_to_all | solution.py:115
  179.0 4.8 %copy-start.12 = (bf16[288,2048]{1,0:T(8,128)(2,1)S(1)}, bf16[288,2048]{1,0:T(8,128)(2,1)}, u32[]{:S(2)}) copy-start(bf16[288,2048]{1,0:T(8,128)(2,1)} %copy-done.11) | copy-start | bytes 3538948
  179.0 4.8 %copy-start.19 = (bf16[288,384]{1,0:T(8,128)(2,1)S(1)}, bf16[288,384]{1,0:T(8,128)(2,1)}, u32[]{:S(2)}) copy-start(bf16[288,384]{1,0:T(8,128)(2,1)} %get-tuple-element.44) | copy-start | bytes 663556
  179.0 29.4 %all-to-all-start.3 = ((bf16[4,3,72,1152]{3,2,1,0:T(8,128)(2,1)}), bf16[4,3,72,1152]{3,2,1,0:T(8,128)(2,1)}, u32[]{:S(2)}, u32[]{:S(2)}) async-start(bf16[4,3,72,1152]{3,2,1,0:T(8,128)(2,1)} %bitcast.149), calls=%async_computation.5 | async-start | bytes 3981312 | tf_op jit(solution)/shard_map/all_to_all | solution.py:115
  183.8 5.8 %copy-start.6 = (bf16[864,2048]{1,0:T(8,128)(2,1)S(1)}, bf16[864,2048]{1,0:T(8,128)(2,1)}, u32[]{:S(2)}) copy-start(bf16[864,2048]{1,0:T(8,128)(2,1)} %copy-done.5) | copy-start | bytes 10616836
  183.8 5.8 %copy-start.10 = (bf16[288,2048]{1,0:T(8,128)(2,1)S(1)}, bf16[288,2048]{1,0:T(8,128)(2,1)}, u32[]{:S(2)}) copy-start(bf16[288,2048]{1,0:T(8,128)(2,1)} %copy-done.9) | copy-start | bytes 3538948
  183.8 5.8 %copy-start.16 = (bf16[288,384]{1,0:T(8,128)(2,1)S(1)}, bf16[288,384]{1,0:T(8,128)(2,1)}, u32[]{:S(2)}) copy-start(bf16[288,384]{1,0:T(8,128)(2,1)} %copy-done.15) | copy-start | bytes 663556
  189.6 3.9 %copy-start.14 = (bf16[288,384]{1,0:T(8,128)(2,1)S(1)}, bf16[288,384]{1,0:T(8,128)(2,1)}, u32[]{:S(2)}) copy-start(bf16[288,384]{1,0:T(8,128)(2,1)} %copy-done.13) | copy-start | bytes 663556
  193.5 17.4 %copy-start.18 = (bf16[3,288,128]{2,1,0:T(8,128)(2,1)S(1)}, bf16[3,288,128]{2,1,0:T(8,128)(2,1)}, u32[]{:S(2)}) copy-start(bf16[3,288,128]{2,1,0:T(8,128)(2,1)} %copy-done.17) | copy-start | bytes 663556
  213.1 29.9 %copy-start.1 = (bf16[1,384,2048]{2,1,0:T(8,128)(2,1)S(1)}, bf16[1,384,2048]{2,1,0:T(8,128)(2,1)}, u32[]{:S(2)}) copy-start(bf16[1,384,2048]{2,1,0:T(8,128)(2,1)} %param.13) | copy-start | bytes 4718596
  213.2 10.9 %collective-permute-start.5 = (bf16[128,1152]{1,0:T(8,128)(2,1)S(1)}, bf16[128,1152]{1,0:T(8,128)(2,1)S(1)}, u32[]{:S(2)}, u32[]{:S(2)}) collective-permute-start(bf16[128,1152]{1,0:T(8,128)(2,1)S(1)} %get-tuple-element.46), channel_id=1, source_target_pairs={{0,24},{8,0},{16,8},{24,16},{1,25},{9,1},{17,9},{25,17},{2,26},{10... | collective-permute-start | bytes 884744 | tf_op jit(solution)/shard_map/ppermute | solution.py:132
  216.6 14.9 %collective-permute-start.7 = (bf16[128,1152]{1,0:T(8,128)(2,1)S(1)}, bf16[128,1152]{1,0:T(8,128)(2,1)S(1)}, u32[]{:S(2)}, u32[]{:S(2)}) collective-permute-start(bf16[128,1152]{1,0:T(8,128)(2,1)S(1)} %get-tuple-element.47), channel_id=1, source_target_pairs={{0,8},{8,16},{16,24},{24,0},{1,9},{9,17},{17,25},{25,1},{2,10},{10... | collective-permute-start | bytes 884744 | tf_op jit(solution)/shard_map/ppermute | solution.py:132
  216.6 24.8 %collective-permute-start.6 = (bf16[128,1152]{1,0:T(8,128)(2,1)S(1)}, bf16[128,1152]{1,0:T(8,128)(2,1)S(1)}, u32[]{:S(2)}, u32[]{:S(2)}) collective-permute-start(bf16[128,1152]{1,0:T(8,128)(2,1)S(1)} %get-tuple-element.48), channel_id=1, source_target_pairs={{0,16},{8,24},{16,0},{24,8},{1,17},{9,25},{17,1},{25,9},{2,18},{10... | collective-permute-start | bytes 884744 | tf_op jit(solution)/shard_map/ppermute | solution.py:132
Sparse Core Ops, SparseCore 0:
  139.1 7.6 reduce-scatter.2
  161.5 13.8 reduce-scatter.4
